TPU v7x, 512 devices: a whole 4x4x16 slice. The times are simulated.
512 devices in a mesh: seg: 64 (over y, z_lo, core), blk: 8 (over x, z_hi).
Axes of the slice: x: 4, y: 4, z: 16 (z_hi: 2, z_lo: 8; z = z_hi * 8 + z_lo), core: 2. Of those that a mesh axis runs over, the one named last changes fastest.
Arguments:
- record: float32 [24, 262144], P(None, ('seg', 'blk')), may hold values from -8 to 8, as said below
- templates: bfloat16 [128, 24, 512], P('blk'), may hold values from -6 to 6
Outputs:
- detection: float32 [128, 262144], P(None, ('seg', 'blk'))
Inputs may be any that keep to these rules, and one draw needn't show every extreme that they name: `record`: network samples.
All inputs are finite; a program needn't handle non-finite values.
Results may differ from a plain program's by a relative error of at most 0.0032.
Values may be sent and summed in bfloat16 or wider, within the bound.
No kernel may reach another device: no remote copies, remote signals or barrier semaphores. Data moves between devices by JAX's collectives and lax.ppermute only.
A program may use at most 64 MiB of HBM per device.

v0:
```python
import jax
import jax.numpy as jnp
from jax import lax
from jax.sharding import PartitionSpec as P


def passed_along(block, axis, distance):
    devices = range(lax.axis_size(axis))
    route = [(i - distance, i) for i in devices if i - distance in devices]
    return lax.ppermute(block, axis, route)


def normalize(templates):
    widened = templates.astype(jnp.float32)
    centred = widened - jnp.mean(widened, axis=2, keepdims=True)
    return (centred / jnp.sqrt(jnp.sum(centred * centred, axis=2, keepdims=True) + 1e-06)).astype(
        jnp.bfloat16
    )


def band_matrix(samples, window):
    span = samples + window - 1
    rows = jnp.arange(span, dtype=jnp.int32)[:, None]
    cols = jnp.arange(samples, dtype=jnp.int32)[None, :]
    inside = jnp.logical_and(rows >= cols, rows < cols + window)
    return inside.astype(jnp.float32)


def window_scale(extended, band, window):
    stacked_rows = jnp.concatenate([extended, extended * extended], axis=0)
    sums = jnp.dot(
        stacked_rows, band, precision=lax.Precision.HIGHEST, preferred_element_type=jnp.float32
    )
    channels = extended.shape[0]
    window_sum = sums[:channels]
    window_sq = sums[channels:]
    spread = window_sq - window_sum * window_sum / window
    return 1.0 / jnp.sqrt(jnp.maximum(spread, 1.0))


def correlate(record_bf, kernel_block, scale):
    members = kernel_block.shape[0]
    channels = kernel_block.shape[1]
    window = kernel_block.shape[2]
    samples = scale.shape[1]
    span = record_bf.shape[1]
    kernels = jnp.transpose(kernel_block, (1, 0, 2))

    def one_channel(total, inputs):
        channel_row, kernel_rows, factor = inputs
        repeated = jnp.tile(channel_row, window + 1)[: window * (span + 1)]
        hankel = repeated.reshape(window, span + 1)[:, :samples]
        product = jnp.dot(kernel_rows, hankel, preferred_element_type=jnp.float32)
        return (total + product * factor[None, :], None)

    total, unused = lax.scan(
        one_channel, jnp.zeros((members, samples), jnp.float32), (record_bf, kernels, scale)
    )
    return total / channels


def body(record, templates):
    samples = record.shape[1]
    window = templates.shape[2]
    trailing = passed_along(record, ("seg", "blk"), -1)
    padded_rec = jnp.concatenate([record, trailing], axis=1)
    normalized = normalize(templates)
    band = band_matrix(samples, window)
    extended = padded_rec[:, : samples + window - 1]
    scale = window_scale(extended, band, window)
    record_bf = extended.astype(jnp.bfloat16)
    collected = lax.all_gather(normalized, "blk", axis=0, tiled=True)
    stacked = correlate(record_bf, collected, scale)
    power_sum = lax.psum(jnp.sum(stacked * stacked, axis=1), ("seg", "blk"))
    record_len = samples * lax.axis_size("seg") * lax.axis_size("blk")
    return stacked / jnp.sqrt(power_sum / record_len + 1e-06)[:, None]


def solution(mesh):
    return jax.shard_map(
        body,
        mesh=mesh,
        in_specs=(P(None, ("seg", "blk")), P("blk", None, None)),
        out_specs=P(None, ("seg", "blk")),
        check_vma=False,
    )
```

profile of v0, /device:TPU:1, one launch (start us, length us, event | category | flops | bytes accessed | tf_op | source)
XLA Modules:
  0.0 357.7 jit_solution(17654023932856735463)
XLA Ops:
  9.0 1.9 fusion.12
  11.0 19.0 %collective-permute-start = (f32[24,512]{1,0:T(8,128)}, f32[24,512]{1,0:T(8,128)S(1)}, u32[]{:S(2)}, u32[]{:S(2)}) collective-permute-start(f32[24,512]{1,0:T(8,128)} %param.4), channel_id=1, source_target_pairs={{1,0},{2,1},{3,2},{4,3},{5,4},{6,5},{7,6},{8,7},{9,8},{10,9},{11,1... | collective-permute-start | bytes 147464 | tf_op jit(solution)/shard_map/ppermute | solution.py:10
  32.4 129.1 %all-gather.2.cloned.1.call-done = bf16[128,24,512]{2,0,1:T(8,128)(2,1)} async-done(((bf16[16,24,512]{2,0,1:T(8,128)(2,1)}), bf16[128,24,512]{2,0,1:T(8,128)(2,1)}) %all-gather.2.cloned.1.call-update) | async-done | bytes 3145744 | tf_op jit(solution)/shard_map/all_gather | solution.py:72
  161.6 86.4 %while.11 = (s32[]{:T(128)}, f32[128,512]{1,0:T(8,128)S(1)}, bf16[24,128,512]{2,1,0:T(8,128)(2,1)}, bf16[24,1023]{1,0:T(8,128)(2,1)S(1)}, f32[24,512]{1,0:T(8,128)S(1)}, /*index=5*/s32[]{:T(128)}, s32[]{:T(128)}) while((s32[]{:T(128)}, f32[128,512]{1,0:T(8,128)S(1)}, bf16[24,128,512]{2,1,0:T(8,128)(2,1)}, ...), condition=%wide.region_3.4_spmd.clone, body=%wide.region_2.3_spmd.clone.sunk | while | flops 67305472 | bytes 8535635 | solution.py:56
  161.7 1.6 tile.17
  165.3 1.6 tile.17
  168.9 1.6 tile.17
  172.5 1.6 tile.17
  176.1 1.6 tile.17
  179.7 1.6 tile.17
  183.3 1.6 tile.17
  186.9 1.6 tile.17
  190.5 1.6 tile.17
  194.1 1.6 tile.17
  197.7 1.6 tile.17
  201.3 1.6 tile.17
  204.9 1.6 tile.17
  208.5 1.6 tile.17
  212.1 1.6 tile.17
  219.3 1.6 tile.17
  226.5 1.6 tile.17
  233.7 1.6 tile.17
  240.9 1.6 tile.17
  248.1 102.0 %psum.7 = f32[128]{0:T(128)S(1)} all-reduce(f32[128]{0:T(128)S(1)} %multiply_reduce_fusion), channel_id=1, replica_groups=mesh['seg'=64,'blk'=8] {'seg','blk'}, use_global_device_ids=true, to_apply=%region_5.6 | all-reduce | flops 128 | bytes 1024 | tf_op jit(solution)/shard_map/psum | solution.py:74
  (167 shorter events, 59.5 us)
Async XLA Ops:
  6.5 25.0 %copy-start = (f32[24,512]{1,0:T(8,128)S(1)}, f32[24,512]{1,0:T(8,128)}, u32[]{:S(2)}) copy-start(f32[24,512]{1,0:T(8,128)} %param.4) | copy-start | bytes 147460
  6.5 155.0 %all-gather.2.cloned.1.call-start = ((), (), s32[]{:S(2)}) async-start(), calls=%async_computation | async-start | bytes 3538944 | tf_op jit(solution)/shard_map/all_gather | solution.py:72
  11.0 20.5 %collective-permute-start = (f32[24,512]{1,0:T(8,128)}, f32[24,512]{1,0:T(8,128)S(1)}, u32[]{:S(2)}, u32[]{:S(2)}) collective-permute-start(f32[24,512]{1,0:T(8,128)} %param.4), channel_id=1, source_target_pairs={{1,0},{2,1},{3,2},{4,3},{5,4},{6,5},{7,6},{8,7},{9,8},{10,9},{11,1... | collective-permute-start | bytes 147464 | tf_op jit(solution)/shard_map/ppermute | solution.py:10
Sparse Core Ops, SparseCore 0:
  11.1 150.3 all-gather.1
where the time goes:
time: 358 us
  waiting for transfers between devices  131 us (37%)
  blocking collectives  102 us (28%)
  local copies, waits for them, and re-layouts  56.6 us (16%)
  matrix products  29 us (8%)
  starting transfers between devices  19 us (5%)
  between operations  13.5 us (4%)
  other arithmetic  5.36 us (1%)
    all_gather x1, waiting for transfers between devices, body(): collected = lax.all_gather(normalized, 'blk', axis=0, tiled=True)  129 us
    psum x1, blocking collectives, body(): power_sum = lax.psum(jnp.sum(stacked * stacked, axis=1), ('seg', 'blk'))  102 us
    another operation x48, local copies, waits for them, and re-layouts, one_channel(): repeated = jnp.tile(channel_row, window + 1)[:window * (span + 1)]  42.1 us
    dot_general x24, matrix products, one_channel(): product = jnp.dot(kernel_rows, hankel, preferred_element_type=jnp.float32)  28.2 us
    ppermute x1, starting transfers between devices, passed_along(): return lax.ppermute(block, axis, route)  19 us
    reshape x24, local copies, waits for them, and re-layouts, one_channel(): hankel = repeated.reshape(window, span + 1)[:, :samples]  11.8 us
  transfers between devices with their start and end apart: 2, of which 2 were waited for; matrix products, arithmetic and copies ran while one was open for 0% of the time, Pallas kernels for 0%

commit v1 on v0

v1 whole, which is shorter than its diff:
```python
import jax
import jax.numpy as jnp
from jax import lax
from jax.experimental import pallas as pl
from jax.experimental.pallas import tpu as pltpu
from jax.sharding import PartitionSpec as P

LAG_BLOCK = 128


def normalize(templates):
    widened = templates.astype(jnp.float32)
    centred = widened - jnp.mean(widened, axis=2, keepdims=True)
    return (centred / jnp.sqrt(jnp.sum(centred * centred, axis=2, keepdims=True) + 1e-06)).astype(
        jnp.bfloat16
    )


def gather_group(record, axis):
    size = lax.axis_size(axis)
    pieces = [record]
    for d in range(1, size):
        pieces.append(lax.ppermute(record, axis, [(i, (i + d) % size) for i in range(size)]))
    slots = jnp.stack(pieces)
    me = lax.axis_index(axis)
    order = (me - jnp.arange(size)) % size
    group = jnp.take(slots, order, axis=0)
    channels, samples = record.shape
    return jnp.transpose(group, (1, 0, 2)).reshape(channels, size * samples)


def next_group_head(record):
    nseg = lax.axis_size("seg")
    nblk = lax.axis_size("blk")
    total = jnp.zeros_like(record)
    for dest in range(nblk):
        route = [((s + 1) * nblk, s * nblk + dest) for s in range(nseg - 1)]
        total = total + lax.ppermute(record, ("seg", "blk"), route)
    return total


def window_scale(extended, window, outputs):
    channels = extended.shape[0]
    blocks = outputs // window
    rows = jnp.arange(2 * window, dtype=jnp.int32)[:, None]
    cols = jnp.arange(window, dtype=jnp.int32)[None, :]
    band = jnp.logical_and(rows >= cols, rows < cols + window).astype(jnp.float32)
    both = jnp.concatenate([extended, extended * extended], axis=0)
    pairs = jnp.stack([both[:, m * window : (m + 2) * window] for m in range(blocks)], axis=1)
    sums = jnp.dot(
        pairs.reshape(2 * channels * blocks, 2 * window),
        band,
        precision=lax.Precision.HIGHEST,
        preferred_element_type=jnp.float32,
    ).reshape(2 * channels, outputs)
    window_sum = sums[:channels]
    window_sq = sums[channels:]
    spread = window_sq - window_sum * window_sum / window
    return 1.0 / jnp.sqrt(jnp.maximum(spread, 1.0))


def corr_kernel(rec_ref, tr_ref, scale_ref, out_ref):
    channels, _, width = rec_ref.shape
    lag = tr_ref.shape[2]
    members, samples = out_ref.shape
    parts = tr_ref.shape[1] // members
    span = samples + (parts - 1) * lag

    def one_channel(c, acc):
        row = rec_ref[c]
        wide = jnp.broadcast_to(row, (lag, width))
        hankel = pltpu.roll(wide, width - (lag - 1), 1, stride=1, stride_axis=0)
        hankel = hankel[:, :span].astype(jnp.bfloat16)
        prod = jnp.dot(tr_ref[c], hankel, preferred_element_type=jnp.float32)
        raw = prod[0:members, 0:samples]
        for a in range(1, parts):
            raw = raw + prod[a * members : (a + 1) * members, a * lag : a * lag + samples]
        return acc + raw * scale_ref[c]

    acc = lax.fori_loop(0, channels, one_channel, jnp.zeros((members, samples), jnp.float32))
    out_ref[...] = acc / channels


def stacked_correlation(rec_bf, normalized, scale):
    members, channels, window = normalized.shape
    parts = window // LAG_BLOCK
    kernels = normalized.reshape(members, channels, parts, LAG_BLOCK)[..., ::-1]
    kernels = jnp.transpose(kernels, (1, 2, 0, 3)).reshape(channels, parts * members, LAG_BLOCK)
    samples = scale.shape[1]
    return pl.pallas_call(
        corr_kernel,
        out_shape=jax.ShapeDtypeStruct((members, samples), jnp.float32),
    )(rec_bf[:, None, :], kernels, scale[:, None, :])


def seg_sum(value):
    nseg = lax.axis_size("seg")
    if nseg & (nseg - 1):
        return lax.psum(value, "seg")
    bit = 1
    while bit < nseg:
        value = value + lax.ppermute(value, "seg", [(i, i ^ bit) for i in range(nseg)])
        bit *= 2
    return value


def body(record, templates):
    channels, samples = record.shape
    window = templates.shape[2]
    nblk = lax.axis_size("blk")
    group = gather_group(record, "blk")
    head = next_group_head(record)
    extended = jnp.concatenate([group, head], axis=1)
    outputs = group.shape[1]
    scale = window_scale(extended, window, outputs)
    rec_bf = extended.astype(jnp.bfloat16).astype(jnp.float32)
    normalized = normalize(templates)
    stacked = stacked_correlation(rec_bf, normalized, scale)
    power_sum = seg_sum(jnp.sum(stacked * stacked, axis=1))
    record_len = samples * lax.axis_size("seg") * nblk
    detection = stacked / jnp.sqrt(power_sum / record_len + 1e-06)[:, None]
    members = detection.shape[0]
    pieces = detection.reshape(members, nblk, samples)
    spread = lax.all_to_all(pieces, "blk", 1, 0, tiled=True)
    return spread.reshape(members * nblk, samples)


def solution(mesh):
    return jax.shard_map(
        body,
        mesh=mesh,
        in_specs=(P(None, ("seg", "blk")), P("blk", None, None)),
        out_specs=P(None, ("seg", "blk")),
        check_vma=False,
    )
```

time: 358 us -> 174 us (0.49)
  the two profiles are of different devices: /device:TPU:1 before, /device:TPU:18 now
where the time goes in v1:
time: 174 us; the launch traced here: 173 us
  starting transfers between devices  81.9 us (47%)
  waiting for transfers between devices  32.9 us (19%)
  blocking collectives  27.6 us (16%)
  Pallas kernels  15.3 us (9%)
  other arithmetic  7.39 us (4%)
  local copies, waits for them, and re-layouts  4.96 us (3%)
  matrix products  2.26 us (1%)
    ppermute x7, starting transfers between devices, gather_group(): lax.ppermute(record, axis, [(i, (i + d) % size) for i in range(size)])  45.1 us
    ppermute x6, starting transfers between devices, seg_sum(): lax.ppermute(value, 'seg', [(i, i ^ bit) for i in range(nseg)])  30.9 us
    all_to_all x1, blocking collectives, body(): spread = lax.all_to_all(pieces, 'blk', 1, 0, tiled=True)  27.6 us
    pallas_call x1, Pallas kernels, stacked_correlation(): pl.pallas_call(corr_kernel, out_shape=jax.ShapeDtypeStruct((members, samp...  15.3 us
    ppermute x6, waiting for transfers between devices, seg_sum(): lax.ppermute(value, 'seg', [(i, i ^ bit) for i in range(nseg)])  13.7 us
    ppermute x7, waiting for transfers between devices, gather_group(): lax.ppermute(record, axis, [(i, (i + d) % size) for i in range(size)])  10.1 us
    ppermute x8, waiting for transfers between devices, next_group_head(): total = total + lax.ppermute(record, ('seg', 'blk'), route)  9.13 us
    ppermute x8, starting transfers between devices, next_group_head(): total = total + lax.ppermute(record, ('seg', 'blk'), route)  5.93 us
  transfers between devices with their start and end apart: 21, of which 8 were waited for; matrix products, arithmetic and copies ran while one was open for 4% of the time, Pallas kernels for 0%

profile of v1, /device:TPU:18, one launch (start us, length us, event | category | flops | bytes accessed | tf_op | source)
XLA Modules:
  0.0 173.0 jit_solution(7913017598614232996)
XLA Ops:
  0.0 15.7 %collective-permute-start = (f32[24,512]{1,0:T(8,128)}, f32[24,512]{1,0:T(8,128)S(1)}, u32[]{:S(2)}, u32[]{:S(2)}) collective-permute-start(f32[24,512]{1,0:T(8,128)} %param.2), channel_id=1, source_target_pairs={{0,1},{1,2},{2,3},{3,4},{4,5},{5,6},{6,7},{7,0},{8,9},{9,10},{10,1... | collective-permute-start | bytes 147464 | tf_op jit(solution)/shard_map/ppermute | solution.py:23
  15.7 3.4 %collective-permute-start.1 = (f32[24,512]{1,0:T(8,128)}, f32[24,512]{1,0:T(8,128)S(1)}, u32[]{:S(2)}, u32[]{:S(2)}) collective-permute-start(f32[24,512]{1,0:T(8,128)} %param.2), channel_id=1, source_target_pairs={{0,2},{1,3},{2,4},{3,5},{4,6},{5,7},{6,0},{7,1},{8,10},{9,11},{10,... | collective-permute-start | bytes 147464 | tf_op jit(solution)/shard_map/ppermute | solution.py:23
  19.1 2.6 %collective-permute-start.2 = (f32[24,512]{1,0:T(8,128)}, f32[24,512]{1,0:T(8,128)S(1)}, u32[]{:S(2)}, u32[]{:S(2)}) collective-permute-start(f32[24,512]{1,0:T(8,128)} %param.2), channel_id=1, source_target_pairs={{0,3},{1,4},{2,5},{3,6},{4,7},{5,0},{6,1},{7,2},{8,11},{9,12},{10,... | collective-permute-start | bytes 147464 | tf_op jit(solution)/shard_map/ppermute | solution.py:23
  21.7 3.3 %collective-permute-start.3 = (f32[24,512]{1,0:T(8,128)}, f32[24,512]{1,0:T(8,128)S(1)}, u32[]{:S(2)}, u32[]{:S(2)}) collective-permute-start(f32[24,512]{1,0:T(8,128)} %param.2), channel_id=1, source_target_pairs={{0,4},{1,5},{2,6},{3,7},{4,0},{5,1},{6,2},{7,3},{8,12},{9,13},{10,... | collective-permute-start | bytes 147464 | tf_op jit(solution)/shard_map/ppermute | solution.py:23
  25.0 14.1 %collective-permute-start.4 = (f32[24,512]{1,0:T(8,128)}, f32[24,512]{1,0:T(8,128)S(1)}, u32[]{:S(2)}, u32[]{:S(2)}) collective-permute-start(f32[24,512]{1,0:T(8,128)} %param.2), channel_id=1, source_target_pairs={{0,5},{1,6},{2,7},{3,0},{4,1},{5,2},{6,3},{7,4},{8,13},{9,14},{10,... | collective-permute-start | bytes 147464 | tf_op jit(solution)/shard_map/ppermute | solution.py:23
  44.9 4.1 %collective-permute-start.5 = (f32[24,512]{1,0:T(8,128)S(1)}, f32[24,512]{1,0:T(8,128)S(1)}, u32[]{:S(2)}, u32[]{:S(2)}) collective-permute-start(f32[24,512]{1,0:T(8,128)S(1)} %copy-done), channel_id=1, source_target_pairs={{0,6},{1,7},{2,0},{3,1},{4,2},{5,3},{6,4},{7,5},{8,14},{9,15},{10,... | collective-permute-start | bytes 147464 | tf_op jit(solution)/shard_map/ppermute | solution.py:23
  49.0 1.9 %collective-permute-start.6 = (f32[24,512]{1,0:T(8,128)S(1)}, f32[24,512]{1,0:T(8,128)S(1)}, u32[]{:S(2)}, u32[]{:S(2)}) collective-permute-start(f32[24,512]{1,0:T(8,128)S(1)} %copy-done), channel_id=1, source_target_pairs={{0,7},{1,0},{2,1},{3,2},{4,3},{5,4},{6,5},{7,6},{8,15},{9,8},{10,9... | collective-permute-start | bytes 147464 | tf_op jit(solution)/shard_map/ppermute | solution.py:23
  53.7 10.0 %collective-permute-done.6 = f32[24,512]{1,0:T(8,128)S(1)} collective-permute-done((f32[24,512]{1,0:T(8,128)S(1)}, f32[24,512]{1,0:T(8,128)S(1)}, u32[]{:S(2)}, u32[]{:S(2)}) %collective-permute-start.6) | collective-permute-done | bytes 49184 | tf_op jit(solution)/shard_map/ppermute | solution.py:23
  66.4 1.3 collective-permute-start.9
  67.9 9.1 %collective-permute-done.9 = f32[24,512]{1,0:T(8,128)S(1)} collective-permute-done((f32[24,512]{1,0:T(8,128)S(1)}, f32[24,512]{1,0:T(8,128)S(1)}, u32[]{:S(2)}, u32[]{:S(2)}) %collective-permute-start.9) | collective-permute-done | bytes 49184 | tf_op jit(solution)/shard_map/ppermute | solution.py:38
  77.4 2.3 %fusion.1 = f32[384,512]{1,0:T(8,128)S(1)} fusion(f32[48,8,1024]{2,0,1:T(8,128)S(1)} %fusion.14, s32[512]{0:T(512)S(1)} %iota_add_fusion), kind=kOutput, calls=%fused_computation.4 | convolution fusion | flops 2417491968 | bytes 2361344 | tf_op jit(solution)/shard_map/dot_general | solution.py:50
  82.4 15.3 %shard_map.28 = f32[16,4096]{1,0:T(8,128)} custom-call(f32[24,1,4608]{2,1,0:T(1,128)} %maximum_convert_fusion.rec_ref, bf16[24,64,128]{2,1,0:T(8,128)(2,1)} %bitcast.74, f32[24,1,4096]{2,1,0:T(1,128)} %reshape.168.scale_ref), custom_call_target="tpu_custom_call" | custom-call | tf_op jit(solution)/shard_map/pallas_call | solution.py:90
  98.8 3.5 %collective-permute-start.15 = (f32[16]{0:T(128)S(1)}, f32[16]{0:T(128)S(1)}, u32[]{:S(2)}, u32[]{:S(2)}) collective-permute-start(f32[16]{0:T(128)S(1)} %multiply_reduce_fusion), channel_id=1, source_target_pairs={{0,8},{8,0},{16,24},{24,16},{32,40},{40,32},{48,56},{56,48},{64,72... | collective-permute-start | bytes 200 | tf_op jit(solution)/shard_map/ppermute | solution.py:102
  103.1 3.4 %collective-permute-start.16 = (f32[16]{0:T(128)S(1)}, f32[16]{0:T(128)S(1)}, u32[]{:S(2)}, u32[]{:S(2)}) collective-permute-start(f32[16]{0:T(128)S(1)} %add.111), channel_id=1, source_target_pairs={{0,16},{8,24},{16,0},{24,8},{32,48},{40,56},{48,32},{56,40},{64,80... | collective-permute-start | bytes 200 | tf_op jit(solution)/shard_map/ppermute | solution.py:102
  106.5 2.0 %collective-permute-done.16 = f32[16]{0:T(128)S(1)} collective-permute-done((f32[16]{0:T(128)S(1)}, f32[16]{0:T(128)S(1)}, u32[]{:S(2)}, u32[]{:S(2)}) %collective-permute-start.16) | collective-permute-done | bytes 96 | tf_op jit(solution)/shard_map/ppermute | solution.py:102
  108.5 4.1 %collective-permute-start.17 = (f32[16]{0:T(128)S(1)}, f32[16]{0:T(128)S(1)}, u32[]{:S(2)}, u32[]{:S(2)}) collective-permute-start(f32[16]{0:T(128)S(1)} %add.112), channel_id=1, source_target_pairs={{0,32},{8,40},{16,48},{24,56},{32,0},{40,8},{48,16},{56,24},{64,96... | collective-permute-start | bytes 200 | tf_op jit(solution)/shard_map/ppermute | solution.py:102
  112.6 2.2 %collective-permute-done.17 = f32[16]{0:T(128)S(1)} collective-permute-done((f32[16]{0:T(128)S(1)}, f32[16]{0:T(128)S(1)}, u32[]{:S(2)}, u32[]{:S(2)}) %collective-permute-start.17) | collective-permute-done | bytes 96 | tf_op jit(solution)/shard_map/ppermute | solution.py:102
  114.9 14.8 %collective-permute-start.18 = (f32[16]{0:T(128)S(1)}, f32[16]{0:T(128)S(1)}, u32[]{:S(2)}, u32[]{:S(2)}) collective-permute-start(f32[16]{0:T(128)S(1)} %add.113), channel_id=1, source_target_pairs={{0,64},{8,72},{16,80},{24,88},{32,96},{40,104},{48,112},{56,120},{... | collective-permute-start | bytes 200 | tf_op jit(solution)/shard_map/ppermute | solution.py:102
  129.7 1.5 collective-permute-done.18
  131.2 3.2 %collective-permute-start.19 = (f32[16]{0:T(128)S(1)}, f32[16]{0:T(128)S(1)}, u32[]{:S(2)}, u32[]{:S(2)}) collective-permute-start(f32[16]{0:T(128)S(1)} %add.114), channel_id=1, source_target_pairs={{0,128},{8,136},{16,144},{24,152},{32,160},{40,168},{48,176},{56,1... | collective-permute-start | bytes 200 | tf_op jit(solution)/shard_map/ppermute | solution.py:102
  134.4 2.2 %collective-permute-done.19 = f32[16]{0:T(128)S(1)} collective-permute-done((f32[16]{0:T(128)S(1)}, f32[16]{0:T(128)S(1)}, u32[]{:S(2)}, u32[]{:S(2)}) %collective-permute-start.19) | collective-permute-done | bytes 96 | tf_op jit(solution)/shard_map/ppermute | solution.py:102
  136.6 1.9 %collective-permute-start.20 = (f32[16]{0:T(128)S(1)}, f32[16]{0:T(128)S(1)}, u32[]{:S(2)}, u32[]{:S(2)}) collective-permute-start(f32[16]{0:T(128)S(1)} %add.115), channel_id=1, source_target_pairs={{0,256},{8,264},{16,272},{24,280},{32,288},{40,296},{48,304},{56,3... | collective-permute-start | bytes 200 | tf_op jit(solution)/shard_map/ppermute | solution.py:102
  138.5 5.0 %collective-permute-done.20 = f32[16]{0:T(128)S(1)} collective-permute-done((f32[16]{0:T(128)S(1)}, f32[16]{0:T(128)S(1)}, u32[]{:S(2)}, u32[]{:S(2)}) %collective-permute-start.20) | collective-permute-done | bytes 96 | tf_op jit(solution)/shard_map/ppermute | solution.py:102
  144.6 27.6 %all_to_all.15 = f32[16,8,512]{2,0,1:T(8,128)S(1)} all-to-all(f32[16,8,512]{2,0,1:T(8,128)S(1)} %bitcast.76), channel_id=1, replica_groups=mesh['seg'=64,'blk'=8] {'blk'}, dimensions={1} | all-to-all | bytes 524288 | tf_op jit(solution)/shard_map/all_to_all | solution.py:124
  (74 shorter events, 17.8 us)
Async XLA Ops:
  0.0 44.9 %collective-permute-start = (f32[24,512]{1,0:T(8,128)}, f32[24,512]{1,0:T(8,128)S(1)}, u32[]{:S(2)}, u32[]{:S(2)}) collective-permute-start(f32[24,512]{1,0:T(8,128)} %param.2), channel_id=1, source_target_pairs={{0,1},{1,2},{2,3},{3,4},{4,5},{5,6},{6,7},{7,0},{8,9},{9,10},{10,1... | collective-permute-start | bytes 147464 | tf_op jit(solution)/shard_map/ppermute | solution.py:23
  15.7 33.2 %collective-permute-start.1 = (f32[24,512]{1,0:T(8,128)}, f32[24,512]{1,0:T(8,128)S(1)}, u32[]{:S(2)}, u32[]{:S(2)}) collective-permute-start(f32[24,512]{1,0:T(8,128)} %param.2), channel_id=1, source_target_pairs={{0,2},{1,3},{2,4},{3,5},{4,6},{5,7},{6,0},{7,1},{8,10},{9,11},{10,... | collective-permute-start | bytes 147464 | tf_op jit(solution)/shard_map/ppermute | solution.py:23
  19.1 31.8 %collective-permute-start.2 = (f32[24,512]{1,0:T(8,128)}, f32[24,512]{1,0:T(8,128)S(1)}, u32[]{:S(2)}, u32[]{:S(2)}) collective-permute-start(f32[24,512]{1,0:T(8,128)} %param.2), channel_id=1, source_target_pairs={{0,3},{1,4},{2,5},{3,6},{4,7},{5,0},{6,1},{7,2},{8,11},{9,12},{10,... | collective-permute-start | bytes 147464 | tf_op jit(solution)/shard_map/ppermute | solution.py:23
  21.7 29.9 %collective-permute-start.3 = (f32[24,512]{1,0:T(8,128)}, f32[24,512]{1,0:T(8,128)S(1)}, u32[]{:S(2)}, u32[]{:S(2)}) collective-permute-start(f32[24,512]{1,0:T(8,128)} %param.2), channel_id=1, source_target_pairs={{0,4},{1,5},{2,6},{3,7},{4,0},{5,1},{6,2},{7,3},{8,12},{9,13},{10,... | collective-permute-start | bytes 147464 | tf_op jit(solution)/shard_map/ppermute | solution.py:23
  25.0 27.3 %collective-permute-start.4 = (f32[24,512]{1,0:T(8,128)}, f32[24,512]{1,0:T(8,128)S(1)}, u32[]{:S(2)}, u32[]{:S(2)}) collective-permute-start(f32[24,512]{1,0:T(8,128)} %param.2), channel_id=1, source_target_pairs={{0,5},{1,6},{2,7},{3,0},{4,1},{5,2},{6,3},{7,4},{8,13},{9,14},{10,... | collective-permute-start | bytes 147464 | tf_op jit(solution)/shard_map/ppermute | solution.py:23
  42.4 2.5 %copy-start = (f32[24,512]{1,0:T(8,128)S(1)}, f32[24,512]{1,0:T(8,128)}, u32[]{:S(2)}) copy-start(f32[24,512]{1,0:T(8,128)} %param.2) | copy-start | bytes 147460
  44.9 8.1 %collective-permute-start.5 = (f32[24,512]{1,0:T(8,128)S(1)}, f32[24,512]{1,0:T(8,128)S(1)}, u32[]{:S(2)}, u32[]{:S(2)}) collective-permute-start(f32[24,512]{1,0:T(8,128)S(1)} %copy-done), channel_id=1, source_target_pairs={{0,6},{1,7},{2,0},{3,1},{4,2},{5,3},{6,4},{7,5},{8,14},{9,15},{10,... | collective-permute-start | bytes 147464 | tf_op jit(solution)/shard_map/ppermute | solution.py:23
  49.0 14.8 %collective-permute-start.6 = (f32[24,512]{1,0:T(8,128)S(1)}, f32[24,512]{1,0:T(8,128)S(1)}, u32[]{:S(2)}, u32[]{:S(2)}) collective-permute-start(f32[24,512]{1,0:T(8,128)S(1)} %copy-done), channel_id=1, source_target_pairs={{0,7},{1,0},{2,1},{3,2},{4,3},{5,4},{6,5},{7,6},{8,15},{9,8},{10,9... | collective-permute-start | bytes 147464 | tf_op jit(solution)/shard_map/ppermute | solution.py:23
  50.9 14.2 %collective-permute-start.10 = (f32[24,512]{1,0:T(8,128)S(1)}, f32[24,512]{1,0:T(8,128)S(1)}, u32[]{:S(2)}, u32[]{:S(2)}) collective-permute-start(f32[24,512]{1,0:T(8,128)S(1)} %copy-done), channel_id=1, source_target_pairs={{8,3},{16,11},{24,19},{32,27},{40,35},{48,43},{56,51},{64,59},{72,... | collective-permute-start | bytes 147464 | tf_op jit(solution)/shard_map/ppermute | solution.py:38
  51.6 14.2 %collective-permute-start.11 = (f32[24,512]{1,0:T(8,128)S(1)}, f32[24,512]{1,0:T(8,128)S(1)}, u32[]{:S(2)}, u32[]{:S(2)}) collective-permute-start(f32[24,512]{1,0:T(8,128)S(1)} %copy-done), channel_id=1, source_target_pairs={{8,4},{16,12},{24,20},{32,28},{40,36},{48,44},{56,52},{64,60},{72,... | collective-permute-start | bytes 147464 | tf_op jit(solution)/shard_map/ppermute | solution.py:38
  52.3 14.1 %collective-permute-start.12 = (f32[24,512]{1,0:T(8,128)S(1)}, f32[24,512]{1,0:T(8,128)S(1)}, u32[]{:S(2)}, u32[]{:S(2)}) collective-permute-start(f32[24,512]{1,0:T(8,128)S(1)} %copy-done), channel_id=1, source_target_pairs={{8,5},{16,13},{24,21},{32,29},{40,37},{48,45},{56,53},{64,61},{72,... | collective-permute-start | bytes 147464 | tf_op jit(solution)/shard_map/ppermute | solution.py:38
  53.0 14.9 %collective-permute-start.13 = (f32[24,512]{1,0:T(8,128)S(1)}, f32[24,512]{1,0:T(8,128)S(1)}, u32[]{:S(2)}, u32[]{:S(2)}) collective-permute-start(f32[24,512]{1,0:T(8,128)S(1)} %copy-done), channel_id=1, source_target_pairs={{8,6},{16,14},{24,22},{32,30},{40,38},{48,46},{56,54},{64,62},{72,... | collective-permute-start | bytes 147464 | tf_op jit(solution)/shard_map/ppermute | solution.py:38
  63.7 4.2 %collective-permute-start.14 = (f32[24,512]{1,0:T(8,128)S(1)}, f32[24,512]{1,0:T(8,128)S(1)}, u32[]{:S(2)}, u32[]{:S(2)}) collective-permute-start(f32[24,512]{1,0:T(8,128)S(1)} %copy-done), channel_id=1, source_target_pairs={{8,7},{16,15},{24,23},{32,31},{40,39},{48,47},{56,55},{64,63},{72,... | collective-permute-start | bytes 147464 | tf_op jit(solution)/shard_map/ppermute | solution.py:38
  65.1 2.8 %collective-permute-start.7 = (f32[24,512]{1,0:T(8,128)S(1)}, f32[24,512]{1,0:T(8,128)S(1)}, u32[]{:S(2)}, u32[]{:S(2)}) collective-permute-start(f32[24,512]{1,0:T(8,128)S(1)} %copy-done), channel_id=1, source_target_pairs={{8,0},{16,8},{24,16},{32,24},{40,32},{48,40},{56,48},{64,56},{72,6... | collective-permute-start | bytes 147464 | tf_op jit(solution)/shard_map/ppermute | solution.py:38
  65.8 2.1 %collective-permute-start.8 = (f32[24,512]{1,0:T(8,128)S(1)}, f32[24,512]{1,0:T(8,128)S(1)}, u32[]{:S(2)}, u32[]{:S(2)}) collective-permute-start(f32[24,512]{1,0:T(8,128)S(1)} %copy-done), channel_id=1, source_target_pairs={{8,1},{16,9},{24,17},{32,25},{40,33},{48,41},{56,49},{64,57},{72,6... | collective-permute-start | bytes 147464 | tf_op jit(solution)/shard_map/ppermute | solution.py:38
  66.4 10.6 %collective-permute-start.9 = (f32[24,512]{1,0:T(8,128)S(1)}, f32[24,512]{1,0:T(8,128)S(1)}, u32[]{:S(2)}, u32[]{:S(2)}) collective-permute-start(f32[24,512]{1,0:T(8,128)S(1)} %copy-done), channel_id=1, source_target_pairs={{8,2},{16,10},{24,18},{32,26},{40,34},{48,42},{56,50},{64,58},{72,... | collective-permute-start | bytes 147464 | tf_op jit(solution)/shard_map/ppermute | solution.py:38
  98.8 4.3 %collective-permute-start.15 = (f32[16]{0:T(128)S(1)}, f32[16]{0:T(128)S(1)}, u32[]{:S(2)}, u32[]{:S(2)}) collective-permute-start(f32[16]{0:T(128)S(1)} %multiply_reduce_fusion), channel_id=1, source_target_pairs={{0,8},{8,0},{16,24},{24,16},{32,40},{40,32},{48,56},{56,48},{64,72... | collective-permute-start | bytes 200 | tf_op jit(solution)/shard_map/ppermute | solution.py:102
  103.1 5.4 %collective-permute-start.16 = (f32[16]{0:T(128)S(1)}, f32[16]{0:T(128)S(1)}, u32[]{:S(2)}, u32[]{:S(2)}) collective-permute-start(f32[16]{0:T(128)S(1)} %add.111), channel_id=1, source_target_pairs={{0,16},{8,24},{16,0},{24,8},{32,48},{40,56},{48,32},{56,40},{64,80... | collective-permute-start | bytes 200 | tf_op jit(solution)/shard_map/ppermute | solution.py:102
  108.5 6.3 %collective-permute-start.17 = (f32[16]{0:T(128)S(1)}, f32[16]{0:T(128)S(1)}, u32[]{:S(2)}, u32[]{:S(2)}) collective-permute-start(f32[16]{0:T(128)S(1)} %add.112), channel_id=1, source_target_pairs={{0,32},{8,40},{16,48},{24,56},{32,0},{40,8},{48,16},{56,24},{64,96... | collective-permute-start | bytes 200 | tf_op jit(solution)/shard_map/ppermute | solution.py:102
  114.9 16.3 %collective-permute-start.18 = (f32[16]{0:T(128)S(1)}, f32[16]{0:T(128)S(1)}, u32[]{:S(2)}, u32[]{:S(2)}) collective-permute-start(f32[16]{0:T(128)S(1)} %add.113), channel_id=1, source_target_pairs={{0,64},{8,72},{16,80},{24,88},{32,96},{40,104},{48,112},{56,120},{... | collective-permute-start | bytes 200 | tf_op jit(solution)/shard_map/ppermute | solution.py:102
  131.2 5.4 %collective-permute-start.19 = (f32[16]{0:T(128)S(1)}, f32[16]{0:T(128)S(1)}, u32[]{:S(2)}, u32[]{:S(2)}) collective-permute-start(f32[16]{0:T(128)S(1)} %add.114), channel_id=1, source_target_pairs={{0,128},{8,136},{16,144},{24,152},{32,160},{40,168},{48,176},{56,1... | collective-permute-start | bytes 200 | tf_op jit(solution)/shard_map/ppermute | solution.py:102
  136.6 6.9 %collective-permute-start.20 = (f32[16]{0:T(128)S(1)}, f32[16]{0:T(128)S(1)}, u32[]{:S(2)}, u32[]{:S(2)}) collective-permute-start(f32[16]{0:T(128)S(1)} %add.115), channel_id=1, source_target_pairs={{0,256},{8,264},{16,272},{24,280},{32,288},{40,296},{48,304},{56,3... | collective-permute-start | bytes 200 | tf_op jit(solution)/shard_map/ppermute | solution.py:102

commit v2 on v1

--- a/solution.py
+++ b/solution.py
@@ -18,14 +18,9 @@
 
 def gather_group(record, axis):
     size = lax.axis_size(axis)
-    pieces = [record]
-    for d in range(1, size):
-        pieces.append(lax.ppermute(record, axis, [(i, (i + d) % size) for i in range(size)]))
-    slots = jnp.stack(pieces)
-    me = lax.axis_index(axis)
-    order = (me - jnp.arange(size)) % size
-    group = jnp.take(slots, order, axis=0)
     channels, samples = record.shape
+    copies = jnp.broadcast_to(record[None], (size, channels, samples))
+    group = lax.all_to_all(copies, axis, 0, 0, tiled=True)
     return jnp.transpose(group, (1, 0, 2)).reshape(channels, size * samples)
 
 
@@ -95,21 +90,16 @@
 
 def seg_sum(value):
     nseg = lax.axis_size("seg")
-    if nseg & (nseg - 1):
-        return lax.psum(value, "seg")
-    bit = 1
-    while bit < nseg:
-        value = value + lax.ppermute(value, "seg", [(i, i ^ bit) for i in range(nseg)])
-        bit *= 2
-    return value
+    copies = jnp.broadcast_to(value[None], (nseg,) + value.shape)
+    return jnp.sum(lax.all_to_all(copies, "seg", 0, 0, tiled=True), axis=0)
 
 
 def body(record, templates):
     channels, samples = record.shape
     window = templates.shape[2]
     nblk = lax.axis_size("blk")
+    head = next_group_head(record)
     group = gather_group(record, "blk")
-    head = next_group_head(record)
     extended = jnp.concatenate([group, head], axis=1)
     outputs = group.shape[1]
     scale = window_scale(extended, window, outputs)

time: 174 us -> 146 us (0.84)
  the two profiles are of different devices: /device:TPU:18 before, /device:TPU:33 now
where the time goes in v2:
time: 146 us; the launch traced here: 145 us
  blocking collectives  70.5 us (48%)
  starting transfers between devices  38 us (26%)
  Pallas kernels  15.3 us (10%)
  local copies, waits for them, and re-layouts  9.9 us (7%)
  other arithmetic  5.26 us (4%)
  waiting for transfers between devices  4.23 us (3%)
  matrix products  1.6 us (1%)
    all_to_all x1, blocking collectives, body(): spread = lax.all_to_all(pieces, 'blk', 1, 0, tiled=True)  37.3 us
    all_to_all x1, blocking collectives, seg_sum(): return jnp.sum(lax.all_to_all(copies, 'seg', 0, 0, tiled=True), axis=0)  33.2 us
    ppermute x8, starting transfers between devices, next_group_head(): total = total + lax.ppermute(record, ('seg', 'blk'), route)  21.6 us
    all_to_all x1, starting transfers between devices, gather_group(): group = lax.all_to_all(copies, axis, 0, 0, tiled=True)  16.4 us
    pallas_call x1, Pallas kernels, stacked_correlation(): pl.pallas_call(corr_kernel, out_shape=jax.ShapeDtypeStruct((members, samp...  15.3 us
    another operation x9, local copies, waits for them, and re-layouts, window_scale(): jnp.stack([both[:, m * window:(m + 2) * window] for m in range(blocks)],...  3.98 us
    all_to_all x1, waiting for transfers between devices, gather_group(): group = lax.all_to_all(copies, axis, 0, 0, tiled=True)  3.97 us
  transfers between devices with their start and end apart: 9, of which 2 were waited for; matrix products, arithmetic and copies ran while one was open for 2% of the time, Pallas kernels for 0%

profile of v2, /device:TPU:33, one launch (start us, length us, event | category | flops | bytes accessed | tf_op | source)
XLA Modules:
  0.0 145.2 jit_solution(17453814778171795515)
XLA Ops:
  0.0 1.7 %broadcast_in_dim.4 = f32[8,24,512]{2,1,0:T(8,128)} broadcast(f32[24,512]{1,0:T(8,128)} %param.2), dimensions={1,2} | broadcast | bytes 442368 | tf_op jit(solution)/shard_map/broadcast_in_dim | solution.py:22
  1.7 16.4 %all-to-all-start = ((f32[8,24,512]{2,1,0:T(8,128)}), f32[8,24,512]{2,1,0:T(8,128)S(1)}, u32[]{:S(2)}, u32[]{:S(2)}) async-start(f32[8,24,512]{2,1,0:T(8,128)} %broadcast_in_dim.4), calls=%async_computation | async-start | bytes 786432 | tf_op jit(solution)/shard_map/all_to_all | solution.py:23
  18.0 2.9 %collective-permute-start = (f32[24,512]{1,0:T(8,128)}, f32[24,512]{1,0:T(8,128)S(1)}, u32[]{:S(2)}, u32[]{:S(2)}) collective-permute-start(f32[24,512]{1,0:T(8,128)} %param.2), channel_id=1, source_target_pairs={{8,0},{16,8},{24,16},{32,24},{40,32},{48,40},{56,48},{64,56},{72,6... | collective-permute-start | bytes 147464 | tf_op jit(solution)/shard_map/ppermute | solution.py:33
  20.9 11.0 %collective-permute-start.1 = (f32[24,512]{1,0:T(8,128)}, f32[24,512]{1,0:T(8,128)S(1)}, u32[]{:S(2)}, u32[]{:S(2)}) collective-permute-start(f32[24,512]{1,0:T(8,128)} %param.2), channel_id=1, source_target_pairs={{8,1},{16,9},{24,17},{32,25},{40,33},{48,41},{56,49},{64,57},{72,6... | collective-permute-start | bytes 147464 | tf_op jit(solution)/shard_map/ppermute | solution.py:33
  31.9 1.3 collective-permute-start.2
  33.2 1.3 collective-permute-start.3
  34.5 1.3 collective-permute-start.4
  35.8 1.1 convert_reduce_fusion
  37.5 1.3 collective-permute-start.5
  38.8 1.3 collective-permute-start.6
  40.1 1.3 collective-permute-start.7
  41.6 1.0 rev.3
  42.9 0.7 copy.44
  43.6 4.0 %all-to-all-done = f32[8,24,512]{2,1,0:T(8,128)S(1)} async-done(((f32[8,24,512]{2,1,0:T(8,128)}), f32[8,24,512]{2,1,0:T(8,128)S(1)}, u32[]{:S(2)}, u32[]{:S(2)}) %all-to-all-start) | async-done | bytes 393248 | tf_op jit(solution)/shard_map/all_to_all | solution.py:23
  49.5 2.4 %stack.35 = f32[48,8,1024]{2,1,0:T(8,128)S(1)} concatenate(f32[48,1,1024]{2,1,0:T(1,128)S(1)} %copy.47, f32[48,1,1024]{2,1,0:T(1,128)S(1)} %copy.48, f32[48,1,1024]{2,1,0:T(1,128)S(1)} %copy.49, f32[48,1,1024]{2,1,0:T(1,128)S(1)} %copy.50, f32[48,1,1024]{2,1,0:T(1,128)S(1)} %copy.51, f32[48,1,1024]{2,1,0:T(1,128)S(1)} %copy.52, f32[48,1,1024]{2,1,0:T(1,128)S(1)} %copy.53, ...), dimensions={1} | concatenate | bytes 3145728 | tf_op jit(solution)/shard_map/stack | solution.py:44
  52.0 1.6 %fusion.1 = f32[384,512]{1,0:T(8,128)S(1)} fusion(f32[48,8,1024]{2,1,0:T(8,128)S(1)} %stack.35, s32[512]{0:T(512)S(1)} %iota_add_fusion), kind=kOutput, calls=%fused_computation.3 | convolution fusion | flops 2417491968 | bytes 2361344 | tf_op jit(solution)/shard_map/dot_general | solution.py:45
  53.7 1.2 reshape.125.scale_ref
  55.1 1.2 maximum_convert_fusion.rec_ref
  56.3 15.3 %shard_map.28 = f32[16,4096]{1,0:T(8,128)} custom-call(f32[24,1,4608]{2,1,0:T(1,128)} %maximum_convert_fusion.rec_ref, bf16[24,64,128]{2,1,0:T(8,128)(2,1)} %bitcast.38, f32[24,1,4096]{2,1,0:T(1,128)} %reshape.125.scale_ref), custom_call_target="tpu_custom_call" | custom-call | tf_op jit(solution)/shard_map/pallas_call | solution.py:85
  71.7 1.1 multiply_reduce_fusion
  72.8 33.2 %all_to_all.26 = f32[64,1,16]{2,1,0:T(1,128)S(1)} all-to-all(f32[64,1,16]{2,1,0:T(1,128)S(1)} %broadcast_in_dim.5), channel_id=1, replica_groups=mesh['seg'=64,'blk'=8] {'seg'}, dimensions={0} | all-to-all | bytes 8192 | tf_op jit(solution)/shard_map/all_to_all | solution.py:94
  106.1 1.0 broadcast_divide_fusion
  107.2 37.3 %all_to_all.27 = f32[16,8,512]{2,0,1:T(8,128)S(1)} all-to-all(f32[16,8,512]{2,0,1:T(8,128)S(1)} %bitcast.40), channel_id=1, replica_groups=mesh['seg'=64,'blk'=8] {'blk'}, dimensions={1} | all-to-all | bytes 524288 | tf_op jit(solution)/shard_map/all_to_all | solution.py:114
  144.5 0.7 copy.62
  (42 shorter events, 3.3 us)
Async XLA Ops:
  0.0 37.4 %copy-start.2 = (f32[24,512]{1,0:T(8,128)S(1)}, f32[24,512]{1,0:T(8,128)}, u32[]{:S(2)}) copy-start(f32[24,512]{1,0:T(8,128)} %param.2) | copy-start | bytes 147460
  0.0 37.0 %copy-start = (bf16[16,24,512]{2,1,0:T(8,128)(2,1)S(1)}, bf16[16,24,512]{2,1,0:T(8,128)(2,1)}, u32[]{:S(2)}) copy-start(bf16[16,24,512]{2,1,0:T(8,128)(2,1)} %param.3) | copy-start | bytes 1179652
  1.7 45.9 %all-to-all-start = ((f32[8,24,512]{2,1,0:T(8,128)}), f32[8,24,512]{2,1,0:T(8,128)S(1)}, u32[]{:S(2)}, u32[]{:S(2)}) async-start(f32[8,24,512]{2,1,0:T(8,128)} %broadcast_in_dim.4), calls=%async_computation | async-start | bytes 786432 | tf_op jit(solution)/shard_map/all_to_all | solution.py:23
  18.0 19.4 %collective-permute-start = (f32[24,512]{1,0:T(8,128)}, f32[24,512]{1,0:T(8,128)S(1)}, u32[]{:S(2)}, u32[]{:S(2)}) collective-permute-start(f32[24,512]{1,0:T(8,128)} %param.2), channel_id=1, source_target_pairs={{8,0},{16,8},{24,16},{32,24},{40,32},{48,40},{56,48},{64,56},{72,6... | collective-permute-start | bytes 147464 | tf_op jit(solution)/shard_map/ppermute | solution.py:33
  20.9 17.9 %collective-permute-start.1 = (f32[24,512]{1,0:T(8,128)}, f32[24,512]{1,0:T(8,128)S(1)}, u32[]{:S(2)}, u32[]{:S(2)}) collective-permute-start(f32[24,512]{1,0:T(8,128)} %param.2), channel_id=1, source_target_pairs={{8,1},{16,9},{24,17},{32,25},{40,33},{48,41},{56,49},{64,57},{72,6... | collective-permute-start | bytes 147464 | tf_op jit(solution)/shard_map/ppermute | solution.py:33
  31.9 8.2 %collective-permute-start.2 = (f32[24,512]{1,0:T(8,128)}, f32[24,512]{1,0:T(8,128)S(1)}, u32[]{:S(2)}, u32[]{:S(2)}) collective-permute-start(f32[24,512]{1,0:T(8,128)} %param.2), channel_id=1, source_target_pairs={{8,2},{16,10},{24,18},{32,26},{40,34},{48,42},{56,50},{64,58},{72,... | collective-permute-start | bytes 147464 | tf_op jit(solution)/shard_map/ppermute | solution.py:33
  33.2 9.4 %collective-permute-start.3 = (f32[24,512]{1,0:T(8,128)}, f32[24,512]{1,0:T(8,128)S(1)}, u32[]{:S(2)}, u32[]{:S(2)}) collective-permute-start(f32[24,512]{1,0:T(8,128)} %param.2), channel_id=1, source_target_pairs={{8,3},{16,11},{24,19},{32,27},{40,35},{48,43},{56,51},{64,59},{72,... | collective-permute-start | bytes 147464 | tf_op jit(solution)/shard_map/ppermute | solution.py:33
  34.5 8.1 %collective-permute-start.4 = (f32[24,512]{1,0:T(8,128)}, f32[24,512]{1,0:T(8,128)S(1)}, u32[]{:S(2)}, u32[]{:S(2)}) collective-permute-start(f32[24,512]{1,0:T(8,128)} %param.2), channel_id=1, source_target_pairs={{8,4},{16,12},{24,20},{32,28},{40,36},{48,44},{56,52},{64,60},{72,... | collective-permute-start | bytes 147464 | tf_op jit(solution)/shard_map/ppermute | solution.py:33
  37.5 5.2 %collective-permute-start.5 = (f32[24,512]{1,0:T(8,128)S(1)}, f32[24,512]{1,0:T(8,128)S(1)}, u32[]{:S(2)}, u32[]{:S(2)}) collective-permute-start(f32[24,512]{1,0:T(8,128)S(1)} %copy-done.2), channel_id=1, source_target_pairs={{8,5},{16,13},{24,21},{32,29},{40,37},{48,45},{56,53},{64,61},{72,... | collective-permute-start | bytes 147464 | tf_op jit(solution)/shard_map/ppermute | solution.py:33
  38.8 3.9 %collective-permute-start.6 = (f32[24,512]{1,0:T(8,128)S(1)}, f32[24,512]{1,0:T(8,128)S(1)}, u32[]{:S(2)}, u32[]{:S(2)}) collective-permute-start(f32[24,512]{1,0:T(8,128)S(1)} %copy-done.2), channel_id=1, source_target_pairs={{8,6},{16,14},{24,22},{32,30},{40,38},{48,46},{56,54},{64,62},{72,... | collective-permute-start | bytes 147464 | tf_op jit(solution)/shard_map/ppermute | solution.py:33
  40.1 2.8 %collective-permute-start.7 = (f32[24,512]{1,0:T(8,128)S(1)}, f32[24,512]{1,0:T(8,128)S(1)}, u32[]{:S(2)}, u32[]{:S(2)}) collective-permute-start(f32[24,512]{1,0:T(8,128)S(1)} %copy-done.2), channel_id=1, source_target_pairs={{8,7},{16,15},{24,23},{32,31},{40,39},{48,47},{56,55},{64,63},{72,... | collective-permute-start | bytes 147464 | tf_op jit(solution)/shard_map/ppermute | solution.py:33
  53.6 1.5 %copy-start.1 = (bf16[24,1,512]{2,1,0:T(2,128)(2,1)S(1)}, bf16[24,1,512]{2,1,0:T(2,128)(2,1)}, u32[]{:S(2)}) copy-start(bf16[24,1,512]{2,1,0:T(2,128)(2,1)} %copy.44) | copy-start | bytes 73732

commit v3 on v2

--- a/solution.py
+++ b/solution.py
@@ -24,14 +24,9 @@
     return jnp.transpose(group, (1, 0, 2)).reshape(channels, size * samples)
 
 
-def next_group_head(record):
+def next_group_head(group, samples):
     nseg = lax.axis_size("seg")
-    nblk = lax.axis_size("blk")
-    total = jnp.zeros_like(record)
-    for dest in range(nblk):
-        route = [((s + 1) * nblk, s * nblk + dest) for s in range(nseg - 1)]
-        total = total + lax.ppermute(record, ("seg", "blk"), route)
-    return total
+    return lax.ppermute(group[:, :samples], "seg", [(i + 1, i) for i in range(nseg - 1)])
 
 
 def window_scale(extended, window, outputs):
@@ -54,38 +49,50 @@
     return 1.0 / jnp.sqrt(jnp.maximum(spread, 1.0))
 
 
+ROWS = 8
+
+
 def corr_kernel(rec_ref, tr_ref, scale_ref, out_ref):
-    channels, _, width = rec_ref.shape
+    channels, width = rec_ref.shape
     lag = tr_ref.shape[2]
     members, samples = out_ref.shape
     parts = tr_ref.shape[1] // members
     span = samples + (parts - 1) * lag
 
-    def one_channel(c, acc):
-        row = rec_ref[c]
-        wide = jnp.broadcast_to(row, (lag, width))
-        hankel = pltpu.roll(wide, width - (lag - 1), 1, stride=1, stride_axis=0)
-        hankel = hankel[:, :span].astype(jnp.bfloat16)
-        prod = jnp.dot(tr_ref[c], hankel, preferred_element_type=jnp.float32)
-        raw = prod[0:members, 0:samples]
-        for a in range(1, parts):
-            raw = raw + prod[a * members : (a + 1) * members, a * lag : a * lag + samples]
-        return acc + raw * scale_ref[c]
+    def one_group(g, acc):
+        first = pl.multiple_of(g * ROWS, ROWS)
+        rows = rec_ref[pl.ds(first, ROWS), :]
+        factors = scale_ref[pl.ds(first, ROWS), :]
+        for r in range(ROWS):
+            wide = jnp.broadcast_to(rows[r : r + 1, :], (lag, width))
+            hankel = pltpu.roll(wide, width - (lag - 1), 1, stride=1, stride_axis=0)
+            hankel = hankel[:, :span].astype(jnp.bfloat16)
+            prod = jnp.dot(tr_ref[first + r], hankel, preferred_element_type=jnp.float32)
+            raw = prod[0:members, 0:samples]
+            for a in range(1, parts):
+                raw = raw + prod[a * members : (a + 1) * members, a * lag : a * lag + samples]
+            acc = acc + raw * factors[r : r + 1, :]
+        return acc
 
-    acc = lax.fori_loop(0, channels, one_channel, jnp.zeros((members, samples), jnp.float32))
+    acc = lax.fori_loop(0, channels // ROWS, one_group, jnp.zeros((members, samples), jnp.float32))
     out_ref[...] = acc / channels
 
 
-def stacked_correlation(rec_bf, normalized, scale):
+def lag_kernels(normalized):
     members, channels, window = normalized.shape
     parts = window // LAG_BLOCK
     kernels = normalized.reshape(members, channels, parts, LAG_BLOCK)[..., ::-1]
-    kernels = jnp.transpose(kernels, (1, 2, 0, 3)).reshape(channels, parts * members, LAG_BLOCK)
-    samples = scale.shape[1]
+    return jnp.transpose(kernels, (1, 2, 0, 3)).reshape(channels, parts * members, LAG_BLOCK)
+
+
+def stacked_correlation(extended, kernels, window, outputs):
+    members = kernels.shape[1] * LAG_BLOCK // window
+    scale = window_scale(extended, window, outputs)
+    rec_bf = extended.astype(jnp.bfloat16).astype(jnp.float32)
     return pl.pallas_call(
         corr_kernel,
-        out_shape=jax.ShapeDtypeStruct((members, samples), jnp.float32),
-    )(rec_bf[:, None, :], kernels, scale[:, None, :])
+        out_shape=jax.ShapeDtypeStruct((members, outputs), jnp.float32),
+    )(rec_bf, kernels, scale)
 
 
 def seg_sum(value):
@@ -98,14 +105,14 @@
     channels, samples = record.shape
     window = templates.shape[2]
     nblk = lax.axis_size("blk")
-    head = next_group_head(record)
     group = gather_group(record, "blk")
-    extended = jnp.concatenate([group, head], axis=1)
-    outputs = group.shape[1]
-    scale = window_scale(extended, window, outputs)
-    rec_bf = extended.astype(jnp.bfloat16).astype(jnp.float32)
-    normalized = normalize(templates)
-    stacked = stacked_correlation(rec_bf, normalized, scale)
+    head = next_group_head(group, samples)
+    kernels = lag_kernels(normalize(templates))
+    inner = group.shape[1] - samples
+    early = stacked_correlation(group, kernels, window, inner)
+    tail = jnp.concatenate([group[:, inner:], head], axis=1)
+    late = stacked_correlation(tail, kernels, window, samples)
+    stacked = jnp.concatenate([early, late], axis=1)
     power_sum = seg_sum(jnp.sum(stacked * stacked, axis=1))
     record_len = samples * lax.axis_size("seg") * nblk
     detection = stacked / jnp.sqrt(power_sum / record_len + 1e-06)[:, None]

time: 146 us -> 122 us (0.84)
  blocking collectives: 70.5 us -> 46.5 us
  waiting for transfers between devices: 4.23 us -> 27.6 us
  starting transfers between devices: 38 us -> 19.7 us
  local copies, waits for them, and re-layouts: 9.9 us -> 5.55 us
    all_to_all x1, waiting for transfers between devices: 3.97 us -> 27.6 us  [gather_group(): group = lax.all_to_all(copies, axis, 0, 0, tiled=True)]
    ppermute x8 -> x1, starting transfers between devices: 21.6 us -> 3.37 us  [next_group_head(): lax.ppermute(group[:, :samples], 'seg', [(i + 1, i) for i in range(nseg -...]
    all_to_all x1, blocking collectives: 33.2 us -> 19.2 us  [seg_sum(): return jnp.sum(lax.all_to_all(copies, 'seg', 0, 0, tiled=True), axis=0)]
    all_to_all x1, blocking collectives: 37.3 us -> 27.3 us  [body(): spread = lax.all_to_all(pieces, 'blk', 1, 0, tiled=True)]
    another operation x9 -> x1, local copies, waits for them, and re-layouts: 3.98 us -> 0.81 us  [window_scale(): jnp.stack([both[:, m * window:(m + 2) * window] for m in range(blocks)],...]
    pallas_call x1 -> x2, Pallas kernels: 15.3 us -> 15.9 us  [stacked_correlation(): pl.pallas_call(corr_kernel, out_shape=jax.ShapeDtypeStruct((members, outp...]
  transfers between devices with their start and end apart: 9 -> 2, of which waited for: 2 -> 1; matrix products, arithmetic and copies ran while one was open for 2% -> 3% of each run, Pallas kernels for 0% -> 10%
where the time goes in v3:
time: 122 us
  blocking collectives  46.5 us (38%)
  waiting for transfers between devices  27.6 us (23%)
  starting transfers between devices  19.7 us (16%)
  Pallas kernels  15.9 us (13%)
  local copies, waits for them, and re-layouts  5.55 us (5%)
  other arithmetic  3.93 us (3%)
  matrix products  2.31 us (2%)
    all_to_all x1, waiting for transfers between devices, gather_group(): group = lax.all_to_all(copies, axis, 0, 0, tiled=True)  27.6 us
    all_to_all x1, blocking collectives, body(): spread = lax.all_to_all(pieces, 'blk', 1, 0, tiled=True)  27.3 us
    all_to_all x1, blocking collectives, seg_sum(): return jnp.sum(lax.all_to_all(copies, 'seg', 0, 0, tiled=True), axis=0)  19.2 us
    all_to_all x1, starting transfers between devices, gather_group(): group = lax.all_to_all(copies, axis, 0, 0, tiled=True)  16.4 us
    pallas_call x2, Pallas kernels, stacked_correlation(): pl.pallas_call(corr_kernel, out_shape=jax.ShapeDtypeStruct((members, outp...  15.9 us
    ppermute x1, starting transfers between devices, next_group_head(): lax.ppermute(group[:, :samples], 'seg', [(i + 1, i) for i in range(nseg -...  3.37 us
  transfers between devices with their start and end apart: 2, of which 1 were waited for; matrix products, arithmetic and copies ran while one was open for 3% of the time, Pallas kernels for 10%

profile of v3, /device:TPU:33, one launch (start us, length us, event | category | flops | bytes accessed | tf_op | source)
XLA Modules:
  0.0 121.7 jit_solution(3037055797265039815)
XLA Ops:
  0.0 1.6 %broadcast_in_dim.4 = f32[8,24,512]{2,1,0:T(8,128)} broadcast(f32[24,512]{1,0:T(8,128)} %param.2), dimensions={1,2} | broadcast | bytes 442368 | tf_op jit(solution)/shard_map/broadcast_in_dim | solution.py:22
  1.6 16.4 %all-to-all-start = ((f32[8,24,512]{2,1,0:T(8,128)}), f32[8,24,512]{2,1,0:T(8,128)S(1)}, u32[]{:S(2)}, u32[]{:S(2)}) async-start(f32[8,24,512]{2,1,0:T(8,128)} %broadcast_in_dim.4), calls=%async_computation | async-start | bytes 786432 | tf_op jit(solution)/shard_map/all_to_all | solution.py:23
  18.0 0.1 convert_reduce_fusion
  18.2 0.2 fusion.9
  18.4 0.2 fusion.10
  18.7 0.2 copy.17
  18.9 1.0 rev.3
  19.9 27.6 %all-to-all-done = f32[8,24,512]{2,1,0:T(8,128)S(1)} async-done(((f32[8,24,512]{2,1,0:T(8,128)}), f32[8,24,512]{2,1,0:T(8,128)S(1)}, u32[]{:S(2)}, u32[]{:S(2)}) %all-to-all-start) | async-done | bytes 393248 | tf_op jit(solution)/shard_map/all_to_all | solution.py:23
  47.6 0.8 convert_convert_fusion
  48.5 0.8 copy.18
  49.4 0.2 reshape.62
  49.6 3.4 %collective-permute-start = (f32[24,512]{1,0:T(8,128)S(1)}, f32[24,512]{1,0:T(8,128)S(1)}, u32[]{:S(2)}, u32[]{:S(2)}) collective-permute-start(f32[24,512]{1,0:T(8,128)S(1)} %get-tuple-element.8), channel_id=1, source_target_pairs={{8,0},{16,8},{24,16},{32,24},{40,32},{48,40},{56,48},{64,56},{72,6... | collective-permute-start | bytes 147464 | tf_op jit(solution)/shard_map/ppermute | solution.py:29
  52.9 1.5 %fusion.3 = f32[336,512]{1,0:T(8,128)S(1)} fusion(f32[336,1024]{1,0:T(8,128)S(1)} %reshape.62, s32[512]{0:T(512)S(1)} %iota_add_fusion), kind=kOutput, calls=%fused_computation.4 | convolution fusion | flops 2115502080 | bytes 2066432 | tf_op jit(solution)/shard_map/dot_general | solution.py:40
  54.5 0.9 reshape.64.scale_ref
  55.4 11.7 %shard_map.28 = f32[16,3584]{1,0:T(8,128)} custom-call(f32[24,4096]{1,0:T(8,128)} %get-tuple-element.5.rec_ref, bf16[24,64,128]{2,1,0:T(8,128)(2,1)} %bitcast.52, f32[24,3584]{1,0:T(8,128)} %reshape.64.scale_ref), custom_call_target="tpu_custom_call" | custom-call | tf_op jit(solution)/shard_map/pallas_call | solution.py:92
  67.1 0.8 fusion.1
  67.9 0.6 fusion.46.scale_ref
  68.6 0.6 fusion.42.rec_ref
  69.2 4.2 %shard_map.29 = f32[16,512]{1,0:T(8,128)} custom-call(f32[24,1024]{1,0:T(8,128)} %fusion.42.rec_ref, bf16[24,64,128]{2,1,0:T(8,128)(2,1)} %bitcast.53, f32[24,512]{1,0:T(8,128)} %fusion.46.scale_ref), custom_call_target="tpu_custom_call" | custom-call | tf_op jit(solution)/shard_map/pallas_call | solution.py:92
  73.4 0.9 multiply_reduce_fusion
  74.3 19.2 %all_to_all.26 = f32[64,1,16]{2,1,0:T(1,128)S(1)} all-to-all(f32[64,1,16]{2,1,0:T(1,128)S(1)} %broadcast_in_dim.5), channel_id=1, replica_groups=mesh['seg'=64,'blk'=8] {'seg'}, dimensions={0} | all-to-all | bytes 8192 | tf_op jit(solution)/shard_map/all_to_all | solution.py:101
  93.7 0.1 bitcast_divide_fusion
  93.8 27.3 %all_to_all.27 = f32[16,8,512]{2,0,1:T(8,128)S(1)} all-to-all(f32[16,8,512]{2,0,1:T(8,128)S(1)} %bitcast_divide_fusion), channel_id=1, replica_groups=mesh['seg'=64,'blk'=8] {'blk'}, dimensions={1} | all-to-all | bytes 524288 | tf_op jit(solution)/shard_map/all_to_all | solution.py:121
  121.0 0.7 copy.32
  (23 shorter events, 0.5 us)
Async XLA Ops:
  0.0 18.0 %copy-start = (bf16[16,24,512]{2,1,0:T(8,128)(2,1)S(1)}, bf16[16,24,512]{2,1,0:T(8,128)(2,1)}, u32[]{:S(2)}) copy-start(bf16[16,24,512]{2,1,0:T(8,128)(2,1)} %param.3) | copy-start | bytes 1179652
  1.6 45.9 %all-to-all-start = ((f32[8,24,512]{2,1,0:T(8,128)}), f32[8,24,512]{2,1,0:T(8,128)S(1)}, u32[]{:S(2)}, u32[]{:S(2)}) async-start(f32[8,24,512]{2,1,0:T(8,128)} %broadcast_in_dim.4), calls=%async_computation | async-start | bytes 786432 | tf_op jit(solution)/shard_map/all_to_all | solution.py:23
  49.6 17.5 %collective-permute-start = (f32[24,512]{1,0:T(8,128)S(1)}, f32[24,512]{1,0:T(8,128)S(1)}, u32[]{:S(2)}, u32[]{:S(2)}) collective-permute-start(f32[24,512]{1,0:T(8,128)S(1)} %get-tuple-element.8), channel_id=1, source_target_pairs={{8,0},{16,8},{24,16},{32,24},{40,32},{48,40},{56,48},{64,56},{72,6... | collective-permute-start | bytes 147464 | tf_op jit(solution)/shard_map/ppermute | solution.py:29
  67.1 6.3 %copy-start.1 = (f32[16,3584]{1,0:T(8,128)S(1)}, f32[16,3584]{1,0:T(8,128)}, u32[]{:S(2)}) copy-start(f32[16,3584]{1,0:T(8,128)} %shard_map.28) | copy-start | bytes 688132

commit v4 on v3

--- a/solution.py
+++ b/solution.py
@@ -5,7 +5,7 @@
 from jax.experimental.pallas import tpu as pltpu
 from jax.sharding import PartitionSpec as P
 
-LAG_BLOCK = 128
+LAG_BLOCK = 64
 
 
 def normalize(templates):
@@ -52,30 +52,41 @@
 ROWS = 8
 
 
-def corr_kernel(rec_ref, tr_ref, scale_ref, out_ref):
+def corr_kernel(rec_ref, tr_ref, even_scale_ref, odd_scale_ref, out_ref):
     channels, width = rec_ref.shape
     lag = tr_ref.shape[2]
     members, samples = out_ref.shape
     parts = tr_ref.shape[1] // members
-    span = samples + (parts - 1) * lag
+    span = samples + parts * lag
+    odd_width = samples + 2 * lag
 
-    def one_group(g, acc):
+    def one_group(g, carry):
+        even_acc, odd_acc = carry
         first = pl.multiple_of(g * ROWS, ROWS)
         rows = rec_ref[pl.ds(first, ROWS), :]
-        factors = scale_ref[pl.ds(first, ROWS), :]
+        even_factors = even_scale_ref[pl.ds(first, ROWS), :]
+        odd_factors = odd_scale_ref[pl.ds(first, ROWS), :]
         for r in range(ROWS):
             wide = jnp.broadcast_to(rows[r : r + 1, :], (lag, width))
             hankel = pltpu.roll(wide, width - (lag - 1), 1, stride=1, stride_axis=0)
             hankel = hankel[:, :span].astype(jnp.bfloat16)
             prod = jnp.dot(tr_ref[first + r], hankel, preferred_element_type=jnp.float32)
-            raw = prod[0:members, 0:samples]
-            for a in range(1, parts):
-                raw = raw + prod[a * members : (a + 1) * members, a * lag : a * lag + samples]
-            acc = acc + raw * factors[r : r + 1, :]
-        return acc
+            even = prod[0:members, 0:samples]
+            odd = prod[members : 2 * members, 0:odd_width]
+            for i in range(1, parts // 2):
+                lo = 2 * i * members
+                even = even + prod[lo : lo + members, 2 * i * lag : 2 * i * lag + samples]
+                odd = odd + prod[lo + members : lo + 2 * members, 2 * i * lag : 2 * i * lag + odd_width]
+            even_acc = even_acc + even * even_factors[r : r + 1, :]
+            odd_acc = odd_acc + odd * odd_factors[r : r + 1, :]
+        return even_acc, odd_acc
 
-    acc = lax.fori_loop(0, channels // ROWS, one_group, jnp.zeros((members, samples), jnp.float32))
-    out_ref[...] = acc / channels
+    start = (
+        jnp.zeros((members, samples), jnp.float32),
+        jnp.zeros((members, odd_width), jnp.float32),
+    )
+    even_acc, odd_acc = lax.fori_loop(0, channels // ROWS, one_group, start)
+    out_ref[...] = (even_acc + odd_acc[:, lag : lag + samples]) / channels
 
 
 def lag_kernels(normalized):
@@ -88,11 +99,14 @@
 def stacked_correlation(extended, kernels, window, outputs):
     members = kernels.shape[1] * LAG_BLOCK // window
     scale = window_scale(extended, window, outputs)
-    rec_bf = extended.astype(jnp.bfloat16).astype(jnp.float32)
+    odd_scale = jnp.pad(scale, ((0, 0), (LAG_BLOCK, LAG_BLOCK)))
+    width = outputs + window + 2 * LAG_BLOCK
+    padded = jnp.pad(extended, ((0, 0), (0, width - extended.shape[1])))
+    rec_bf = padded.astype(jnp.bfloat16).astype(jnp.float32)
     return pl.pallas_call(
         corr_kernel,
         out_shape=jax.ShapeDtypeStruct((members, outputs), jnp.float32),
-    )(rec_bf, kernels, scale)
+    )(rec_bf, kernels, scale, odd_scale)
 
 
 def seg_sum(value):
@@ -117,9 +131,9 @@
     record_len = samples * lax.axis_size("seg") * nblk
     detection = stacked / jnp.sqrt(power_sum / record_len + 1e-06)[:, None]
     members = detection.shape[0]
-    pieces = detection.reshape(members, nblk, samples)
+    pieces = detection.astype(jnp.bfloat16).reshape(members, nblk, samples)
     spread = lax.all_to_all(pieces, "blk", 1, 0, tiled=True)
-    return spread.reshape(members * nblk, samples)
+    return spread.reshape(members * nblk, samples).astype(jnp.float32)
 
 
 def solution(mesh):

time: 122 us -> 115 us (0.943)
  blocking collectives: 46.5 us -> 40.9 us
  local copies, waits for them, and re-layouts: 5.55 us -> 7.29 us
  Pallas kernels: 15.9 us -> 14.2 us
  waiting for transfers between devices: 27.6 us -> 26.1 us
    all_to_all x1, blocking collectives: 27.3 us -> 21.6 us  [body(): spread = lax.all_to_all(pieces, 'blk', 1, 0, tiled=True)]
    pallas_call x2, Pallas kernels: 15.9 us -> 14.2 us  [stacked_correlation(): pl.pallas_call(corr_kernel, out_shape=jax.ShapeDtypeStruct((members, outp...]
    pad x0 -> x2, local copies, waits for them, and re-layouts: none -> 1.62 us  [stacked_correlation(): odd_scale = jnp.pad(scale, ((0, 0), (LAG_BLOCK, LAG_BLOCK)))]
    all_to_all x1, waiting for transfers between devices: 27.6 us -> 26.1 us  [gather_group(): group = lax.all_to_all(copies, axis, 0, 0, tiled=True)]
  transfers between devices with their start and end apart: 2 -> 2, of which waited for: 1 -> 1; matrix products, arithmetic and copies ran while one was open for 3% -> 5% of each run, Pallas kernels for 10% -> 9%
where the time goes in v4:
time: 115 us
  blocking collectives  40.9 us (36%)
  waiting for transfers between devices  26.1 us (23%)
  starting transfers between devices  19.7 us (17%)
  Pallas kernels  14.2 us (12%)
  local copies, waits for them, and re-layouts  7.29 us (6%)
  other arithmetic  4.1 us (4%)
  matrix products  2.3 us (2%)
    all_to_all x1, waiting for transfers between devices, gather_group(): group = lax.all_to_all(copies, axis, 0, 0, tiled=True)  26.1 us
    all_to_all x1, blocking collectives, body(): spread = lax.all_to_all(pieces, 'blk', 1, 0, tiled=True)  21.6 us
    all_to_all x1, blocking collectives, seg_sum(): return jnp.sum(lax.all_to_all(copies, 'seg', 0, 0, tiled=True), axis=0)  19.3 us
    all_to_all x1, starting transfers between devices, gather_group(): group = lax.all_to_all(copies, axis, 0, 0, tiled=True)  16.4 us
    pallas_call x2, Pallas kernels, stacked_correlation(): pl.pallas_call(corr_kernel, out_shape=jax.ShapeDtypeStruct((members, outp...  14.2 us
    ppermute x1, starting transfers between devices, next_group_head(): lax.ppermute(group[:, :samples], 'seg', [(i + 1, i) for i in range(nseg -...  3.36 us
    dot_general x2, matrix products, window_scale(): jnp.dot(pairs.reshape(2 * channels * blocks, 2 * window), band, precision...  2.3 us
  transfers between devices with their start and end apart: 2, of which 1 were waited for; matrix products, arithmetic and copies ran while one was open for 5% of the time, Pallas kernels for 9%

profile of v4, /device:TPU:33, one launch (start us, length us, event | category | flops | bytes accessed | tf_op | source)
XLA Modules:
  0.0 114.9 jit_solution(6013679605307564171)
XLA Ops:
  0.0 1.6 %broadcast_in_dim.4 = f32[8,24,512]{2,1,0:T(8,128)} broadcast(f32[24,512]{1,0:T(8,128)} %param.2), dimensions={1,2} | broadcast | bytes 442368 | tf_op jit(solution)/shard_map/broadcast_in_dim | solution.py:22
  1.6 16.4 %all-to-all-start = ((f32[8,24,512]{2,1,0:T(8,128)}), f32[8,24,512]{2,1,0:T(8,128)S(1)}, u32[]{:S(2)}, u32[]{:S(2)}) async-start(f32[8,24,512]{2,1,0:T(8,128)} %broadcast_in_dim.4), calls=%async_computation | async-start | bytes 786432 | tf_op jit(solution)/shard_map/all_to_all | solution.py:23
  18.2 0.2 fusion.9
  18.4 0.2 fusion.10
  18.6 0.4 reshape.62
  19.0 0.5 copy.17
  19.5 1.9 %rev.3 = bf16[16,24,8,64]{3,0,2,1:T(8,128)(2,1)} reverse(bf16[16,24,8,64]{3,0,2,1:T(8,128)(2,1)S(1)} %copy.17), dimensions={3} | reverse | bytes 786432 | tf_op jit(solution)/shard_map/rev | solution.py:95
  21.4 26.1 %all-to-all-done = f32[8,24,512]{2,1,0:T(8,128)S(1)} async-done(((f32[8,24,512]{2,1,0:T(8,128)}), f32[8,24,512]{2,1,0:T(8,128)S(1)}, u32[]{:S(2)}, u32[]{:S(2)}) %all-to-all-start) | async-done | bytes 393248 | tf_op jit(solution)/shard_map/all_to_all | solution.py:23
  47.8 0.8 copy.18
  48.7 0.2 reshape.64
  48.9 0.8 pad_convert_fusion.rec_ref
  49.6 3.4 %collective-permute-start = (f32[24,512]{1,0:T(8,128)S(1)}, f32[24,512]{1,0:T(8,128)S(1)}, u32[]{:S(2)}, u32[]{:S(2)}) collective-permute-start(f32[24,512]{1,0:T(8,128)S(1)} %get-tuple-element.6), channel_id=1, source_target_pairs={{8,0},{16,8},{24,16},{32,24},{40,32},{48,40},{56,48},{64,56},{72,6... | collective-permute-start | bytes 147464 | tf_op jit(solution)/shard_map/ppermute | solution.py:29
  53.0 1.5 %fusion.3 = f32[336,512]{1,0:T(8,128)S(1)} fusion(f32[336,1024]{1,0:T(8,128)S(1)} %reshape.64, s32[512]{0:T(512)S(1)} %iota_add_fusion), kind=kOutput, calls=%fused_computation.4 | convolution fusion | flops 2115502080 | bytes 2066432 | tf_op jit(solution)/shard_map/dot_general | solution.py:40
  54.5 0.2 reshape.65.even_scale_ref
  54.7 0.9 pad.19.odd_scale_ref
  55.6 10.0 %shard_map.28 = f32[16,3584]{1,0:T(8,128)} custom-call(f32[24,4224]{1,0:T(8,128)} %pad_convert_fusion.rec_ref, bf16[24,128,64]{2,1,0:T(8,128)(2,1)} %bitcast.57, f32[24,3584]{1,0:T(8,128)} %copy-done.1, f32[24,3712]{1,0:T(8,128)} %pad.19.odd_scale_ref), custom_call_target="tpu_custom_call" | custom-call | tf_op jit(solution)/shard_map/pallas_call | solution.py:106
  65.7 0.8 fusion.1
  66.6 0.7 pad.21.odd_scale_ref
  67.3 0.7 pad_convert_fusion.1.rec_ref
  67.9 4.2 %shard_map.29 = f32[16,512]{1,0:T(8,128)} custom-call(f32[24,1152]{1,0:T(8,128)} %pad_convert_fusion.1.rec_ref, bf16[24,128,64]{2,1,0:T(8,128)(2,1)} %bitcast.58, f32[24,512]{1,0:T(8,128)} %copy-done.3, f32[24,640]{1,0:T(8,128)} %pad.21.odd_scale_ref), custom_call_target="tpu_custom_call" | custom-call | tf_op jit(solution)/shard_map/pallas_call | solution.py:106
  72.2 0.9 multiply_reduce_fusion
  73.1 19.3 %all_to_all.20 = f32[64,1,16]{2,1,0:T(1,128)S(1)} all-to-all(f32[64,1,16]{2,1,0:T(1,128)S(1)} %broadcast_in_dim.5), channel_id=1, replica_groups=mesh['seg'=64,'blk'=8] {'seg'}, dimensions={0} | all-to-all | bytes 8192 | tf_op jit(solution)/shard_map/all_to_all | solution.py:115
  92.5 21.6 %all_to_all.21 = bf16[16,8,512]{2,0,1:T(8,128)(2,1)S(1)} all-to-all(bf16[16,8,512]{2,0,1:T(8,128)(2,1)S(1)} %fusion.15), channel_id=1, replica_groups=mesh['seg'=64,'blk'=8] {'blk'}, dimensions={1} | all-to-all | bytes 262144 | tf_op jit(solution)/shard_map/all_to_all | solution.py:135
  114.2 0.7 bitcast_convert_fusion
  (32 shorter events, 0.7 us)
Async XLA Ops:
  0.0 18.0 %copy-start = (bf16[16,24,512]{2,1,0:T(8,128)(2,1)S(1)}, bf16[16,24,512]{2,1,0:T(8,128)(2,1)}, u32[]{:S(2)}) copy-start(bf16[16,24,512]{2,1,0:T(8,128)(2,1)} %param.3) | copy-start | bytes 1179652
  1.6 45.9 %all-to-all-start = ((f32[8,24,512]{2,1,0:T(8,128)}), f32[8,24,512]{2,1,0:T(8,128)S(1)}, u32[]{:S(2)}, u32[]{:S(2)}) async-start(f32[8,24,512]{2,1,0:T(8,128)} %broadcast_in_dim.4), calls=%async_computation | async-start | bytes 786432 | tf_op jit(solution)/shard_map/all_to_all | solution.py:23
  49.6 16.0 %collective-permute-start = (f32[24,512]{1,0:T(8,128)S(1)}, f32[24,512]{1,0:T(8,128)S(1)}, u32[]{:S(2)}, u32[]{:S(2)}) collective-permute-start(f32[24,512]{1,0:T(8,128)S(1)} %get-tuple-element.6), channel_id=1, source_target_pairs={{8,0},{16,8},{24,16},{32,24},{40,32},{48,40},{56,48},{64,56},{72,6... | collective-permute-start | bytes 147464 | tf_op jit(solution)/shard_map/ppermute | solution.py:29
  54.7 0.9 copy-start.1
  65.7 6.5 %copy-start.2 = (f32[16,3584]{1,0:T(8,128)S(1)}, f32[16,3584]{1,0:T(8,128)}, u32[]{:S(2)}) copy-start(f32[16,3584]{1,0:T(8,128)} %shard_map.28) | copy-start | bytes 688132
  66.6 1.4 %copy-start.3 = (f32[24,512]{1,0:T(8,128)}, f32[24,512]{1,0:T(8,128)S(1)}, u32[]{:S(2)}) copy-start(f32[24,512]{1,0:T(8,128)S(1)} %fusion.46.even_scale_ref) | copy-start | bytes 147460

commit v5 on v4

--- a/solution.py
+++ b/solution.py
@@ -52,7 +52,7 @@
 ROWS = 8
 
 
-def corr_kernel(rec_ref, tr_ref, even_scale_ref, odd_scale_ref, out_ref):
+def corr_kernel(rec_ref, tr_ref, scale_ref, out_ref):
     channels, width = rec_ref.shape
     lag = tr_ref.shape[2]
     members, samples = out_ref.shape
@@ -64,8 +64,9 @@
         even_acc, odd_acc = carry
         first = pl.multiple_of(g * ROWS, ROWS)
         rows = rec_ref[pl.ds(first, ROWS), :]
-        even_factors = even_scale_ref[pl.ds(first, ROWS), :]
-        odd_factors = odd_scale_ref[pl.ds(first, ROWS), :]
+        even_factors = scale_ref[pl.ds(first, ROWS), :]
+        blank = jnp.zeros((ROWS, 2 * lag), jnp.float32)
+        odd_factors = pltpu.roll(jnp.concatenate([even_factors, blank], axis=1), lag, 1)
         for r in range(ROWS):
             wide = jnp.broadcast_to(rows[r : r + 1, :], (lag, width))
             hankel = pltpu.roll(wide, width - (lag - 1), 1, stride=1, stride_axis=0)
@@ -99,14 +100,10 @@
 def stacked_correlation(extended, kernels, window, outputs):
     members = kernels.shape[1] * LAG_BLOCK // window
     scale = window_scale(extended, window, outputs)
-    odd_scale = jnp.pad(scale, ((0, 0), (LAG_BLOCK, LAG_BLOCK)))
-    width = outputs + window + 2 * LAG_BLOCK
-    padded = jnp.pad(extended, ((0, 0), (0, width - extended.shape[1])))
-    rec_bf = padded.astype(jnp.bfloat16).astype(jnp.float32)
     return pl.pallas_call(
         corr_kernel,
         out_shape=jax.ShapeDtypeStruct((members, outputs), jnp.float32),
-    )(rec_bf, kernels, scale, odd_scale)
+    )(extended, kernels, scale)
 
 
 def seg_sum(value):
@@ -131,9 +128,9 @@
     record_len = samples * lax.axis_size("seg") * nblk
     detection = stacked / jnp.sqrt(power_sum / record_len + 1e-06)[:, None]
     members = detection.shape[0]
-    pieces = detection.astype(jnp.bfloat16).reshape(members, nblk, samples)
+    pieces = detection.reshape(members, nblk, samples)
     spread = lax.all_to_all(pieces, "blk", 1, 0, tiled=True)
-    return spread.reshape(members * nblk, samples).astype(jnp.float32)
+    return spread.reshape(members * nblk, samples)
 
 
 def solution(mesh):

time: 115 us -> 120 us (1.043)
  blocking collectives: 40.9 us -> 46.5 us
    all_to_all x1, blocking collectives: 21.6 us -> 27.3 us  [body(): spread = lax.all_to_all(pieces, 'blk', 1, 0, tiled=True)]
    convert_element_type x4 -> x0, other arithmetic: 2.25 us -> none  [the longest x2 1.42 us: stacked_correlation(): rec_bf = padded.astype(jnp.bfloat16).astype(jnp.float32)]
    pad x2 -> x0, local copies, waits for them, and re-layouts: 1.62 us -> none  [stacked_correlation(): odd_scale = jnp.pad(scale, ((0, 0), (LAG_BLOCK, LAG_BLOCK)))]
    unnamed x8 -> x7, local copies, waits for them, and re-layouts: 0.02 us -> 1.24 us
  transfers between devices with their start and end apart: 2 -> 2, of which waited for: 1 -> 1; matrix products, arithmetic and copies ran while one was open for 5% -> 5% of each run, Pallas kernels for 9% -> 8%
where the time goes in v5:
time: 120 us
  blocking collectives  46.5 us (39%)
  waiting for transfers between devices  26.1 us (22%)
  starting transfers between devices  19.7 us (16%)
  Pallas kernels  14.2 us (12%)
  local copies, waits for them, and re-layouts  7.64 us (6%)
  other arithmetic  3.18 us (3%)
  matrix products  2.3 us (2%)
    all_to_all x1, blocking collectives, body(): spread = lax.all_to_all(pieces, 'blk', 1, 0, tiled=True)  27.3 us
    all_to_all x1, waiting for transfers between devices, gather_group(): group = lax.all_to_all(copies, axis, 0, 0, tiled=True)  26.1 us
    all_to_all x1, blocking collectives, seg_sum(): return jnp.sum(lax.all_to_all(copies, 'seg', 0, 0, tiled=True), axis=0)  19.2 us
    all_to_all x1, starting transfers between devices, gather_group(): group = lax.all_to_all(copies, axis, 0, 0, tiled=True)  16.4 us
    pallas_call x2, Pallas kernels, stacked_correlation(): pl.pallas_call(corr_kernel, out_shape=jax.ShapeDtypeStruct((members, outp...  14.2 us
    ppermute x1, starting transfers between devices, next_group_head(): lax.ppermute(group[:, :samples], 'seg', [(i + 1, i) for i in range(nseg -...  3.37 us
  transfers between devices with their start and end apart: 2, of which 1 were waited for; matrix products, arithmetic and copies ran while one was open for 5% of the time, Pallas kernels for 8%

profile of v5, /device:TPU:33, one launch (start us, length us, event | category | flops | bytes accessed | tf_op | source)
XLA Modules:
  0.0 119.9 jit_solution(6276425444986904776)
XLA Ops:
  0.0 1.6 %broadcast_in_dim.4 = f32[8,24,512]{2,1,0:T(8,128)} broadcast(f32[24,512]{1,0:T(8,128)} %param.2), dimensions={1,2} | broadcast | bytes 442368 | tf_op jit(solution)/shard_map/broadcast_in_dim | solution.py:22
  1.6 16.4 %all-to-all-start = ((f32[8,24,512]{2,1,0:T(8,128)}), f32[8,24,512]{2,1,0:T(8,128)S(1)}, u32[]{:S(2)}, u32[]{:S(2)}) async-start(f32[8,24,512]{2,1,0:T(8,128)} %broadcast_in_dim.4), calls=%async_computation | async-start | bytes 786432 | tf_op jit(solution)/shard_map/all_to_all | solution.py:23
  18.0 0.1 convert_reduce_fusion
  18.2 0.2 fusion.9
  18.4 0.2 fusion.10
  18.6 0.4 reshape.60
  19.0 0.5 copy.17
  19.5 1.9 %rev.3 = bf16[16,24,8,64]{3,0,2,1:T(8,128)(2,1)} reverse(bf16[16,24,8,64]{3,0,2,1:T(8,128)(2,1)S(1)} %copy.17), dimensions={3} | reverse | bytes 786432 | tf_op jit(solution)/shard_map/rev | solution.py:96
  21.4 26.1 %all-to-all-done = f32[8,24,512]{2,1,0:T(8,128)S(1)} async-done(((f32[8,24,512]{2,1,0:T(8,128)}), f32[8,24,512]{2,1,0:T(8,128)S(1)}, u32[]{:S(2)}, u32[]{:S(2)}) %all-to-all-start) | async-done | bytes 393248 | tf_op jit(solution)/shard_map/all_to_all | solution.py:23
  47.8 0.5 copy-done
  48.3 0.8 copy.18
  49.2 0.2 reshape.62
  49.4 3.4 %collective-permute-start = (f32[24,512]{1,0:T(8,128)S(1)}, f32[24,512]{1,0:T(8,128)S(1)}, u32[]{:S(2)}, u32[]{:S(2)}) collective-permute-start(f32[24,512]{1,0:T(8,128)S(1)} %get-tuple-element.6), channel_id=1, source_target_pairs={{8,0},{16,8},{24,16},{32,24},{40,32},{48,40},{56,48},{64,56},{72,6... | collective-permute-start | bytes 147464 | tf_op jit(solution)/shard_map/ppermute | solution.py:29
  52.7 1.5 %fusion.3 = f32[336,512]{1,0:T(8,128)S(1)} fusion(f32[336,1024]{1,0:T(8,128)S(1)} %reshape.62, s32[512]{0:T(512)S(1)} %iota_add_fusion), kind=kOutput, calls=%fused_computation.4 | convolution fusion | flops 2115502080 | bytes 2066432 | tf_op jit(solution)/shard_map/dot_general | solution.py:40
  54.3 0.9 reshape.64.scale_ref
  55.2 10.0 %shard_map.28 = f32[16,3584]{1,0:T(8,128)} custom-call(f32[24,4096]{1,0:T(8,128)} %bitcast.53, bf16[24,128,64]{2,1,0:T(8,128)(2,1)} %bitcast.54, f32[24,3584]{1,0:T(8,128)} %reshape.64.scale_ref), custom_call_target="tpu_custom_call" | custom-call | tf_op jit(solution)/shard_map/pallas_call | solution.py:103
  65.2 0.6 fusion.45
  65.8 0.8 fusion.1
  66.7 0.6 fusion.43.scale_ref
  67.3 4.2 %shard_map.29 = f32[16,512]{1,0:T(8,128)} custom-call(f32[24,1024]{1,0:T(8,128)} %get-tuple-element.10.rec_ref, bf16[24,128,64]{2,1,0:T(8,128)(2,1)} %bitcast.55, f32[24,512]{1,0:T(8,128)} %fusion.43.scale_ref), custom_call_target="tpu_custom_call" | custom-call | tf_op jit(solution)/shard_map/pallas_call | solution.py:103
  71.5 0.9 multiply_reduce_fusion
  72.5 19.2 %all_to_all.26 = f32[64,1,16]{2,1,0:T(1,128)S(1)} all-to-all(f32[64,1,16]{2,1,0:T(1,128)S(1)} %broadcast_in_dim.5), channel_id=1, replica_groups=mesh['seg'=64,'blk'=8] {'seg'}, dimensions={0} | all-to-all | bytes 8192 | tf_op jit(solution)/shard_map/all_to_all | solution.py:112
  91.9 27.3 %all_to_all.27 = f32[16,8,512]{2,0,1:T(8,128)S(1)} all-to-all(f32[16,8,512]{2,0,1:T(8,128)S(1)} %bitcast_divide_fusion), channel_id=1, replica_groups=mesh['seg'=64,'blk'=8] {'blk'}, dimensions={1} | all-to-all | bytes 524288 | tf_op jit(solution)/shard_map/all_to_all | solution.py:132
  119.2 0.7 copy.32
  (24 shorter events, 0.5 us)
Async XLA Ops:
  0.0 18.0 %copy-start.1 = (bf16[16,24,512]{2,1,0:T(8,128)(2,1)S(1)}, bf16[16,24,512]{2,1,0:T(8,128)(2,1)}, u32[]{:S(2)}) copy-start(bf16[16,24,512]{2,1,0:T(8,128)(2,1)} %param.3) | copy-start | bytes 1179652
  1.6 45.9 %all-to-all-start = ((f32[8,24,512]{2,1,0:T(8,128)}), f32[8,24,512]{2,1,0:T(8,128)S(1)}, u32[]{:S(2)}, u32[]{:S(2)}) async-start(f32[8,24,512]{2,1,0:T(8,128)} %broadcast_in_dim.4), calls=%async_computation | async-start | bytes 786432 | tf_op jit(solution)/shard_map/all_to_all | solution.py:23
  47.6 0.7 copy-start
  49.4 15.8 %collective-permute-start = (f32[24,512]{1,0:T(8,128)S(1)}, f32[24,512]{1,0:T(8,128)S(1)}, u32[]{:S(2)}, u32[]{:S(2)}) collective-permute-start(f32[24,512]{1,0:T(8,128)S(1)} %get-tuple-element.6), channel_id=1, source_target_pairs={{8,0},{16,8},{24,16},{32,24},{40,32},{48,40},{56,48},{64,56},{72,6... | collective-permute-start | bytes 147464 | tf_op jit(solution)/shard_map/ppermute | solution.py:29
  65.8 5.7 %copy-start.2 = (f32[16,3584]{1,0:T(8,128)S(1)}, f32[16,3584]{1,0:T(8,128)}, u32[]{:S(2)}) copy-start(f32[16,3584]{1,0:T(8,128)} %shard_map.28) | copy-start | bytes 688132

commit v6 on v5

--- a/solution.py
+++ b/solution.py
@@ -3,7 +3,8 @@
 from jax import lax
 from jax.experimental import pallas as pl
 from jax.experimental.pallas import tpu as pltpu
-from jax.sharding import PartitionSpec as P
+import numpy as np
+from jax.sharding import Mesh, PartitionSpec as P
 
 LAG_BLOCK = 64
 
@@ -16,12 +17,15 @@
     )
 
 
-def gather_group(record, axis):
-    size = lax.axis_size(axis)
-    channels, samples = record.shape
-    copies = jnp.broadcast_to(record[None], (size, channels, samples))
-    group = lax.all_to_all(copies, axis, 0, 0, tiled=True)
-    return jnp.transpose(group, (1, 0, 2)).reshape(channels, size * samples)
+def gather_group(record):
+    partner = lax.ppermute(record, "bz", [(0, 1), (1, 0)])
+    low = lax.axis_index("bz") == 0
+    pair = jnp.where(low, jnp.concatenate([record, partner], axis=1), jnp.concatenate([partner, record], axis=1))
+    size = lax.axis_size("bx")
+    channels, width = pair.shape
+    copies = jnp.broadcast_to(pair[None], (size, channels, width))
+    group = lax.all_to_all(copies, "bx", 0, 0, tiled=True)
+    return jnp.transpose(group, (1, 0, 2)).reshape(channels, size * width)
 
 
 def next_group_head(group, samples):
@@ -115,8 +119,8 @@
 def body(record, templates):
     channels, samples = record.shape
     window = templates.shape[2]
-    nblk = lax.axis_size("blk")
-    group = gather_group(record, "blk")
+    nblk = lax.axis_size(BLK)
+    group = gather_group(record)
     head = next_group_head(group, samples)
     kernels = lag_kernels(normalize(templates))
     inner = group.shape[1] - samples
@@ -129,15 +133,20 @@
     detection = stacked / jnp.sqrt(power_sum / record_len + 1e-06)[:, None]
     members = detection.shape[0]
     pieces = detection.reshape(members, nblk, samples)
-    spread = lax.all_to_all(pieces, "blk", 1, 0, tiled=True)
+    spread = lax.all_to_all(pieces, BLK, 1, 0, tiled=True)
     return spread.reshape(members * nblk, samples)
 
 
+BLK = ("bx", "bz")
+
+
 def solution(mesh):
+    nseg, nblk = mesh.shape["seg"], mesh.shape["blk"]
+    split = Mesh(np.asarray(mesh.devices).reshape(nseg, nblk // 2, 2), ("seg",) + BLK)
     return jax.shard_map(
         body,
-        mesh=mesh,
-        in_specs=(P(None, ("seg", "blk")), P("blk", None, None)),
-        out_specs=P(None, ("seg", "blk")),
+        mesh=split,
+        in_specs=(P(None, ("seg",) + BLK), P(BLK, None, None)),
+        out_specs=P(None, ("seg",) + BLK),
         check_vma=False,
     )

time: 120 us -> 113 us (0.942)
  waiting for transfers between devices: 26.1 us -> 3.23 us
  blocking collectives: 46.5 us -> 56.1 us
  starting transfers between devices: 19.7 us -> 23.9 us
  other arithmetic: 3.18 us -> 6.05 us
    all_to_all x1, waiting for transfers between devices: 26.1 us -> 3.23 us  [gather_group(): group = lax.all_to_all(copies, 'bx', 0, 0, tiled=True)]
    ppermute x0 -> x1, starting transfers between devices: none -> 14.7 us  [gather_group(): partner = lax.ppermute(record, 'bz', [(0, 1), (1, 0)])]
    all_to_all x1, starting transfers between devices: 16.4 us -> 4.01 us  [gather_group(): group = lax.all_to_all(copies, 'bx', 0, 0, tiled=True)]
    all_to_all x1, blocking collectives: 19.2 us -> 24.3 us  [seg_sum(): return jnp.sum(lax.all_to_all(copies, 'seg', 0, 0, tiled=True), axis=0)]
    all_to_all x1, blocking collectives: 27.3 us -> 31.8 us  [body(): spread = lax.all_to_all(pieces, BLK, 1, 0, tiled=True)]
    ppermute x1, starting transfers between devices: 3.37 us -> 5.22 us  [next_group_head(): lax.ppermute(group[:, :samples], 'seg', [(i + 1, i) for i in range(nseg -...]
  transfers between devices with their start and end apart: 2 -> 3, of which waited for: 1 -> 1; matrix products, arithmetic and copies ran while one was open for 5% -> 7% of each run, Pallas kernels for 8% -> 9%
where the time goes in v6:
time: 113 us
  blocking collectives  56.1 us (50%)
  starting transfers between devices  23.9 us (21%)
  Pallas kernels  14.2 us (13%)
  local copies, waits for them, and re-layouts  6.79 us (6%)
  other arithmetic  6.05 us (5%)
  waiting for transfers between devices  3.23 us (3%)
  matrix products  2.3 us (2%)
    all_to_all x1, blocking collectives, body(): spread = lax.all_to_all(pieces, BLK, 1, 0, tiled=True)  31.8 us
    all_to_all x1, blocking collectives, seg_sum(): return jnp.sum(lax.all_to_all(copies, 'seg', 0, 0, tiled=True), axis=0)  24.3 us
    ppermute x1, starting transfers between devices, gather_group(): partner = lax.ppermute(record, 'bz', [(0, 1), (1, 0)])  14.7 us
    pallas_call x2, Pallas kernels, stacked_correlation(): pl.pallas_call(corr_kernel, out_shape=jax.ShapeDtypeStruct((members, outp...  14.2 us
    ppermute x1, starting transfers between devices, next_group_head(): lax.ppermute(group[:, :samples], 'seg', [(i + 1, i) for i in range(nseg -...  5.22 us
    all_to_all x1, starting transfers between devices, gather_group(): group = lax.all_to_all(copies, 'bx', 0, 0, tiled=True)  4.01 us
    all_to_all x1, waiting for transfers between devices, gather_group(): group = lax.all_to_all(copies, 'bx', 0, 0, tiled=True)  3.23 us
    dot_general x2, matrix products, window_scale(): jnp.dot(pairs.reshape(2 * channels * blocks, 2 * window), band, precision...  2.3 us
  transfers between devices with their start and end apart: 3, of which 1 were waited for; matrix products, arithmetic and copies ran while one was open for 7% of the time, Pallas kernels for 9%

profile of v6, /device:TPU:33, one launch (start us, length us, event | category | flops | bytes accessed | tf_op | source)
XLA Modules:
  0.0 112.8 jit_solution(17657318250395212886)
XLA Ops:
  0.0 14.7 %collective-permute-start = (f32[24,512]{1,0:T(8,128)}, f32[24,512]{1,0:T(8,128)S(1)}, u32[]{:S(2)}, u32[]{:S(2)}) collective-permute-start(f32[24,512]{1,0:T(8,128)} %param.2), channel_id=1, source_target_pairs={{0,1},{1,0},{2,3},{3,2},{4,5},{5,4},{6,7},{7,6},{8,9},{9,8},{10,11... | collective-permute-start | bytes 147464 | tf_op jit(solution)/shard_map/ppermute | solution.py:21
  14.7 1.1 convert_reduce_fusion
  15.8 1.2 %fusion.9 = f32[16,24]{1,0:T(8,128)S(1)} fusion(bf16[16,24,512]{2,1,0:T(8,128)(2,1)} %param.3, f32[16,24]{1,0:T(8,128)S(1)} %broadcast_multiply_fusion), kind=kLoop, calls=%fused_computation.23 | loop fusion | flops 786048 | bytes 396288 | tf_op jit(solution)/shard_map/reduce_sum | solution.py:15
  17.1 0.9 maximum_select_fusion
  18.0 0.8 broadcast_in_dim.4
  18.8 4.0 %all-to-all-start = ((f32[4,24,1024]{2,1,0:T(8,128)}), f32[4,24,1024]{2,1,0:T(8,128)S(1)}, u32[]{:S(2)}, u32[]{:S(2)}) async-start(f32[4,24,1024]{2,1,0:T(8,128)} %broadcast_in_dim.4), calls=%async_computation | async-start | bytes 786432 | tf_op jit(solution)/shard_map/all_to_all | solution.py:27
  23.0 0.4 reshape.88
  23.4 0.5 copy.17
  23.9 1.9 %rev.3 = bf16[16,24,8,64]{3,0,2,1:T(8,128)(2,1)} reverse(bf16[16,24,8,64]{3,0,2,1:T(8,128)(2,1)S(1)} %copy.17), dimensions={3} | reverse | bytes 786432 | tf_op jit(solution)/shard_map/rev | solution.py:100
  25.8 3.2 %all-to-all-done = f32[4,24,1024]{2,1,0:T(8,128)S(1)} async-done(((f32[4,24,1024]{2,1,0:T(8,128)}), f32[4,24,1024]{2,1,0:T(8,128)S(1)}, u32[]{:S(2)}, u32[]{:S(2)}) %all-to-all-start) | async-done | bytes 393248 | tf_op jit(solution)/shard_map/all_to_all | solution.py:27
  29.3 0.5 copy-done
  29.8 0.8 copy.18
  30.8 5.2 %collective-permute-start.1 = (f32[24,512]{1,0:T(8,128)S(1)}, f32[24,512]{1,0:T(8,128)S(1)}, u32[]{:S(2)}, u32[]{:S(2)}) collective-permute-start(f32[24,512]{1,0:T(8,128)S(1)} %get-tuple-element.6), channel_id=1, source_target_pairs={{8,0},{16,8},{24,16},{32,24},{40,32},{48,40},{56,48},{64,56},{72,6... | collective-permute-start | bytes 147464 | tf_op jit(solution)/shard_map/ppermute | solution.py:33
  36.1 1.5 %fusion.3 = f32[336,512]{1,0:T(8,128)S(1)} fusion(f32[336,1024]{1,0:T(8,128)S(1)} %reshape.90, s32[512]{0:T(512)S(1)} %iota_add_fusion), kind=kOutput, calls=%fused_computation.4 | convolution fusion | flops 2115502080 | bytes 2066432 | tf_op jit(solution)/shard_map/dot_general | solution.py:44
  37.6 0.9 reshape.92.scale_ref
  38.5 10.0 %shard_map.28 = f32[16,3584]{1,0:T(8,128)} custom-call(f32[24,4096]{1,0:T(8,128)} %bitcast.53, bf16[24,128,64]{2,1,0:T(8,128)(2,1)} %bitcast.54, f32[24,3584]{1,0:T(8,128)} %reshape.92.scale_ref), custom_call_target="tpu_custom_call" | custom-call | tf_op jit(solution)/shard_map/pallas_call | solution.py:107
  48.5 0.6 fusion.45
  49.2 0.8 fusion.1
  50.0 0.6 fusion.43.scale_ref
  50.6 4.2 %shard_map.29 = f32[16,512]{1,0:T(8,128)} custom-call(f32[24,1024]{1,0:T(8,128)} %get-tuple-element.10.rec_ref, bf16[24,128,64]{2,1,0:T(8,128)(2,1)} %bitcast.55, f32[24,512]{1,0:T(8,128)} %fusion.43.scale_ref), custom_call_target="tpu_custom_call" | custom-call | tf_op jit(solution)/shard_map/pallas_call | solution.py:107
  54.9 0.9 multiply_reduce_fusion
  55.8 24.3 %all_to_all.26 = f32[64,1,16]{2,1,0:T(1,128)S(1)} all-to-all(f32[64,1,16]{2,1,0:T(1,128)S(1)} %broadcast_in_dim.5), channel_id=1, replica_groups=mesh['seg'=64,'bx'=4,'bz'=2] {'seg'}, dimensions={0} | all-to-all | bytes 8192 | tf_op jit(solution)/shard_map/all_to_all | solution.py:116
  80.3 31.8 %all_to_all.27 = f32[16,8,512]{2,0,1:T(8,128)S(1)} all-to-all(f32[16,8,512]{2,0,1:T(8,128)S(1)} %bitcast_divide_fusion), channel_id=1, replica_groups=mesh['seg'=64,'bx'=4,'bz'=2] {'bx','bz'}, dimensions={1} | all-to-all | bytes 524288 | tf_op jit(solution)/shard_map/all_to_all | solution.py:136
  112.1 0.7 copy.32
  (27 shorter events, 0.9 us)
Async XLA Ops:
  0.0 22.8 %copy-start.1 = (bf16[16,24,512]{2,1,0:T(8,128)(2,1)S(1)}, bf16[16,24,512]{2,1,0:T(8,128)(2,1)}, u32[]{:S(2)}) copy-start(bf16[16,24,512]{2,1,0:T(8,128)(2,1)} %param.3) | copy-start | bytes 1179652
  0.0 17.1 %collective-permute-start = (f32[24,512]{1,0:T(8,128)}, f32[24,512]{1,0:T(8,128)S(1)}, u32[]{:S(2)}, u32[]{:S(2)}) collective-permute-start(f32[24,512]{1,0:T(8,128)} %param.2), channel_id=1, source_target_pairs={{0,1},{1,0},{2,3},{3,2},{4,5},{5,4},{6,7},{7,6},{8,9},{9,8},{10,11... | collective-permute-start | bytes 147464 | tf_op jit(solution)/shard_map/ppermute | solution.py:21
  18.8 10.2 %all-to-all-start = ((f32[4,24,1024]{2,1,0:T(8,128)}), f32[4,24,1024]{2,1,0:T(8,128)S(1)}, u32[]{:S(2)}, u32[]{:S(2)}) async-start(f32[4,24,1024]{2,1,0:T(8,128)} %broadcast_in_dim.4), calls=%async_computation | async-start | bytes 786432 | tf_op jit(solution)/shard_map/all_to_all | solution.py:27
  29.0 0.7 copy-start
  30.8 17.7 %collective-permute-start.1 = (f32[24,512]{1,0:T(8,128)S(1)}, f32[24,512]{1,0:T(8,128)S(1)}, u32[]{:S(2)}, u32[]{:S(2)}) collective-permute-start(f32[24,512]{1,0:T(8,128)S(1)} %get-tuple-element.6), channel_id=1, source_target_pairs={{8,0},{16,8},{24,16},{32,24},{40,32},{48,40},{56,48},{64,56},{72,6... | collective-permute-start | bytes 147464 | tf_op jit(solution)/shard_map/ppermute | solution.py:33
  49.2 5.7 %copy-start.2 = (f32[16,3584]{1,0:T(8,128)S(1)}, f32[16,3584]{1,0:T(8,128)}, u32[]{:S(2)}) copy-start(f32[16,3584]{1,0:T(8,128)} %shard_map.28) | copy-start | bytes 688132

commit v7 on v6

--- a/solution.py
+++ b/solution.py
@@ -33,34 +33,25 @@
     return lax.ppermute(group[:, :samples], "seg", [(i + 1, i) for i in range(nseg - 1)])
 
 
-def window_scale(extended, window, outputs):
-    channels = extended.shape[0]
-    blocks = outputs // window
-    rows = jnp.arange(2 * window, dtype=jnp.int32)[:, None]
-    cols = jnp.arange(window, dtype=jnp.int32)[None, :]
-    band = jnp.logical_and(rows >= cols, rows < cols + window).astype(jnp.float32)
-    both = jnp.concatenate([extended, extended * extended], axis=0)
-    pairs = jnp.stack([both[:, m * window : (m + 2) * window] for m in range(blocks)], axis=1)
-    sums = jnp.dot(
-        pairs.reshape(2 * channels * blocks, 2 * window),
-        band,
-        precision=lax.Precision.HIGHEST,
-        preferred_element_type=jnp.float32,
-    ).reshape(2 * channels, outputs)
-    window_sum = sums[:channels]
-    window_sq = sums[channels:]
-    spread = window_sq - window_sum * window_sum / window
-    return 1.0 / jnp.sqrt(jnp.maximum(spread, 1.0))
-
-
 ROWS = 8
 
 
-def corr_kernel(rec_ref, tr_ref, scale_ref, out_ref):
+def window_sums(values, window, samples):
+    width = values.shape[1]
+    total = values
+    step = 1
+    while step < window:
+        total = total + pltpu.roll(total, width - step, 1)
+        step *= 2
+    return total[:, :samples]
+
+
+def corr_kernel(rec_ref, tr_ref, out_ref):
     channels, width = rec_ref.shape
     lag = tr_ref.shape[2]
     members, samples = out_ref.shape
     parts = tr_ref.shape[1] // members
+    window = parts * lag
     span = samples + parts * lag
     odd_width = samples + 2 * lag
 
@@ -68,7 +59,10 @@
         even_acc, odd_acc = carry
         first = pl.multiple_of(g * ROWS, ROWS)
         rows = rec_ref[pl.ds(first, ROWS), :]
-        even_factors = scale_ref[pl.ds(first, ROWS), :]
+        window_sum = window_sums(rows, window, samples)
+        window_sq = window_sums(rows * rows, window, samples)
+        spread = window_sq - window_sum * window_sum / window
+        even_factors = 1.0 / jnp.sqrt(jnp.maximum(spread, 1.0))
         blank = jnp.zeros((ROWS, 2 * lag), jnp.float32)
         odd_factors = pltpu.roll(jnp.concatenate([even_factors, blank], axis=1), lag, 1)
         for r in range(ROWS):
@@ -103,11 +97,10 @@
 
 def stacked_correlation(extended, kernels, window, outputs):
     members = kernels.shape[1] * LAG_BLOCK // window
-    scale = window_scale(extended, window, outputs)
     return pl.pallas_call(
         corr_kernel,
         out_shape=jax.ShapeDtypeStruct((members, outputs), jnp.float32),
-    )(extended, kernels, scale)
+    )(extended, kernels)
 
 
 def seg_sum(value):

time: 113 us -> 111 us (0.982)
  waiting for transfers between devices: 3.23 us -> 6.47 us
  other arithmetic: 6.05 us -> 3.32 us
  local copies, waits for them, and re-layouts: 6.79 us -> 4.34 us
  matrix products: 2.3 us -> 0 us
  Pallas kernels: 14.2 us -> 16 us
    all_to_all x1, waiting for transfers between devices: 3.23 us -> 5.96 us  [gather_group(): group = lax.all_to_all(copies, 'bx', 0, 0, tiled=True)]
    dot_general x2 -> x0, matrix products: 2.3 us -> none  [window_scale(): jnp.dot(pairs.reshape(2 * channels * blocks, 2 * window), band, precision...]
    pallas_call x2, Pallas kernels: 14.2 us -> 16 us  [stacked_correlation(): pl.pallas_call(corr_kernel, out_shape=jax.ShapeDtypeStruct((members, outp...]
  transfers between devices with their start and end apart: 3 -> 3, of which waited for: 1 -> 2; matrix products, arithmetic and copies ran while one was open for 7% -> 4% of each run, Pallas kernels for 9% -> 10%
where the time goes in v7:
time: 111 us
  blocking collectives  56.1 us (51%)
  starting transfers between devices  24.6 us (22%)
  Pallas kernels  16 us (14%)
  waiting for transfers between devices  6.47 us (6%)
  local copies, waits for them, and re-layouts  4.34 us (4%)
  other arithmetic  3.32 us (3%)
    all_to_all x1, blocking collectives, body(): spread = lax.all_to_all(pieces, BLK, 1, 0, tiled=True)  31.8 us
    all_to_all x1, blocking collectives, seg_sum(): return jnp.sum(lax.all_to_all(copies, 'seg', 0, 0, tiled=True), axis=0)  24.3 us
    pallas_call x2, Pallas kernels, stacked_correlation(): pl.pallas_call(corr_kernel, out_shape=jax.ShapeDtypeStruct((members, outp...  16 us
    ppermute x1, starting transfers between devices, gather_group(): partner = lax.ppermute(record, 'bz', [(0, 1), (1, 0)])  14.5 us
    ppermute x1, starting transfers between devices, next_group_head(): lax.ppermute(group[:, :samples], 'seg', [(i + 1, i) for i in range(nseg -...  5.97 us
    all_to_all x1, waiting for transfers between devices, gather_group(): group = lax.all_to_all(copies, 'bx', 0, 0, tiled=True)  5.96 us
    all_to_all x1, starting transfers between devices, gather_group(): group = lax.all_to_all(copies, 'bx', 0, 0, tiled=True)  4.14 us
  transfers between devices with their start and end apart: 3, of which 2 were waited for; matrix products, arithmetic and copies ran while one was open for 4% of the time, Pallas kernels for 10%

profile of v7, /device:TPU:33, one launch (start us, length us, event | category | flops | bytes accessed | tf_op | source)
XLA Modules:
  0.0 111.0 jit_solution(1670847097800170040)
XLA Ops:
  0.0 14.5 %collective-permute-start = (f32[24,512]{1,0:T(8,128)}, f32[24,512]{1,0:T(8,128)S(1)}, u32[]{:S(2)}, u32[]{:S(2)}) collective-permute-start(f32[24,512]{1,0:T(8,128)} %param.2), channel_id=1, source_target_pairs={{0,1},{1,0},{2,3},{3,2},{4,5},{5,4},{6,7},{7,6},{8,9},{9,8},{10,11... | collective-permute-start | bytes 147464 | tf_op jit(solution)/shard_map/ppermute | solution.py:21
  14.5 0.0 copy-start.3
  14.5 1.1 %convert_reduce_fusion = f32[16,24]{1,0:T(8,128)S(1)} fusion(bf16[16,24,512]{2,1,0:T(8,128)(2,1)} %param.3), kind=kLoop, calls=%fused_computation.1 | loop fusion | flops 392832 | bytes 394752 | tf_op jit(solution)/shard_map/reduce_sum | solution.py:14
  15.7 0.5 collective-permute-done
  16.2 0.0 copy-done.3
  16.2 0.8 broadcast_in_dim.4
  17.0 4.1 %all-to-all-start = ((f32[4,24,1024]{2,1,0:T(8,128)}), f32[4,24,1024]{2,1,0:T(8,128)S(1)}, u32[]{:S(2)}, u32[]{:S(2)}) async-start(f32[4,24,1024]{2,1,0:T(8,128)} %broadcast_in_dim.4), calls=%async_computation | async-start | bytes 786432 | tf_op jit(solution)/shard_map/all_to_all | solution.py:27
  21.2 0.2 fusion.2
  21.4 6.0 %all-to-all-done = f32[4,24,1024]{2,1,0:T(8,128)S(1)} async-done(((f32[4,24,1024]{2,1,0:T(8,128)}), f32[4,24,1024]{2,1,0:T(8,128)S(1)}, u32[]{:S(2)}, u32[]{:S(2)}) %all-to-all-start) | async-done | bytes 393248 | tf_op jit(solution)/shard_map/all_to_all | solution.py:27
  27.4 6.0 %collective-permute-start.1 = (f32[24,512]{1,0:T(8,128)S(1)}, f32[24,512]{1,0:T(8,128)S(1)}, u32[]{:S(2)}, u32[]{:S(2)}) collective-permute-start(f32[24,512]{1,0:T(8,128)S(1)} %get-tuple-element.6), channel_id=1, source_target_pairs={{8,0},{16,8},{24,16},{32,24},{40,32},{48,40},{56,48},{64,56},{72,6... | collective-permute-start | bytes 147464 | tf_op jit(solution)/shard_map/ppermute | solution.py:33
  33.4 0.2 fusion.3
  33.6 0.4 reshape.71
  34.0 0.5 copy.12
  34.5 1.9 %rev.3 = bf16[16,24,8,64]{3,0,2,1:T(8,128)(2,1)} reverse(bf16[16,24,8,64]{3,0,2,1:T(8,128)(2,1)S(1)} %copy.12), dimensions={3} | reverse | bytes 786432 | tf_op jit(solution)/shard_map/rev | solution.py:94
  36.4 11.5 %shard_map.28 = f32[16,3584]{1,0:T(8,128)} custom-call(f32[24,4096]{1,0:T(8,128)} %bitcast.17, bf16[24,128,64]{2,1,0:T(8,128)(2,1)} %bitcast.14), custom_call_target="tpu_custom_call" | custom-call | tf_op jit(solution)/shard_map/pallas_call | solution.py:100
  48.0 0.0 collective-permute-done.1
  48.0 0.6 pad_maximum_fusion.1.rec_ref
  48.6 4.5 %shard_map.29 = f32[16,512]{1,0:T(8,128)} custom-call(f32[24,1024]{1,0:T(8,128)} %pad_maximum_fusion.1.rec_ref, bf16[24,128,64]{2,1,0:T(8,128)(2,1)} %bitcast.15), custom_call_target="tpu_custom_call" | custom-call | tf_op jit(solution)/shard_map/pallas_call | solution.py:100
  53.1 0.9 multiply_reduce_fusion
  54.0 24.3 %all_to_all.26 = f32[64,1,16]{2,1,0:T(1,128)S(1)} all-to-all(f32[64,1,16]{2,1,0:T(1,128)S(1)} %broadcast_in_dim.5), channel_id=1, replica_groups=mesh['seg'=64,'bx'=4,'bz'=2] {'seg'}, dimensions={0} | all-to-all | bytes 8192 | tf_op jit(solution)/shard_map/all_to_all | solution.py:109
  78.3 0.1 reduce_sum.39
  78.4 0.1 bitcast_divide_fusion
  78.5 31.8 %all_to_all.27 = f32[16,8,512]{2,0,1:T(8,128)S(1)} all-to-all(f32[16,8,512]{2,0,1:T(8,128)S(1)} %bitcast_divide_fusion), channel_id=1, replica_groups=mesh['seg'=64,'bx'=4,'bz'=2] {'bx','bz'}, dimensions={1} | all-to-all | bytes 524288 | tf_op jit(solution)/shard_map/all_to_all | solution.py:129
  110.3 0.7 copy.20
  (13 shorter events, 0.1 us)
Async XLA Ops:
  0.0 16.2 %collective-permute-start = (f32[24,512]{1,0:T(8,128)}, f32[24,512]{1,0:T(8,128)S(1)}, u32[]{:S(2)}, u32[]{:S(2)}) collective-permute-start(f32[24,512]{1,0:T(8,128)} %param.2), channel_id=1, source_target_pairs={{0,1},{1,0},{2,3},{3,2},{4,5},{5,4},{6,7},{7,6},{8,9},{9,8},{10,11... | collective-permute-start | bytes 147464 | tf_op jit(solution)/shard_map/ppermute | solution.py:21
  14.5 1.7 %copy-start.3 = (f32[24,512]{1,0:T(8,128)S(1)}, f32[24,512]{1,0:T(8,128)}, u32[]{:S(2)}) copy-start(f32[24,512]{1,0:T(8,128)} %param.2) | copy-start | bytes 147460
  17.0 4.1 %copy-start = (bf16[16,24,512]{2,1,0:T(8,128)(2,1)S(1)}, bf16[16,24,512]{2,1,0:T(8,128)(2,1)}, u32[]{:S(2)}) copy-start(bf16[16,24,512]{2,1,0:T(8,128)(2,1)} %param.3) | copy-start | bytes 1179652
  17.0 10.4 %all-to-all-start = ((f32[4,24,1024]{2,1,0:T(8,128)}), f32[4,24,1024]{2,1,0:T(8,128)S(1)}, u32[]{:S(2)}, u32[]{:S(2)}) async-start(f32[4,24,1024]{2,1,0:T(8,128)} %broadcast_in_dim.4), calls=%async_computation | async-start | bytes 786432 | tf_op jit(solution)/shard_map/all_to_all | solution.py:27
  27.4 6.2 %copy-start.1 = (f32[4,3,8,1024]{3,2,0,1:T(8,128)}, f32[4,3,8,1024]{3,2,0,1:T(8,128)S(1)}, u32[]{:S(2)}) copy-start(f32[4,3,8,1024]{3,2,0,1:T(8,128)S(1)} %copy.17) | copy-start | bytes 1179652
  27.4 20.5 %collective-permute-start.1 = (f32[24,512]{1,0:T(8,128)S(1)}, f32[24,512]{1,0:T(8,128)S(1)}, u32[]{:S(2)}, u32[]{:S(2)}) collective-permute-start(f32[24,512]{1,0:T(8,128)S(1)} %get-tuple-element.6), channel_id=1, source_target_pairs={{8,0},{16,8},{24,16},{32,24},{40,32},{48,40},{56,48},{64,56},{72,6... | collective-permute-start | bytes 147464 | tf_op jit(solution)/shard_map/ppermute | solution.py:33
  48.6 4.5 %copy-start.2 = (f32[16,3584]{1,0:T(8,128)S(1)}, f32[16,3584]{1,0:T(8,128)}, u32[]{:S(2)}) copy-start(f32[16,3584]{1,0:T(8,128)} %shard_map.28) | copy-start | bytes 688132

commit v8 on v7

--- a/solution.py
+++ b/solution.py
@@ -7,14 +7,6 @@
 from jax.sharding import Mesh, PartitionSpec as P
 
 LAG_BLOCK = 64
-
-
-def normalize(templates):
-    widened = templates.astype(jnp.float32)
-    centred = widened - jnp.mean(widened, axis=2, keepdims=True)
-    return (centred / jnp.sqrt(jnp.sum(centred * centred, axis=2, keepdims=True) + 1e-06)).astype(
-        jnp.bfloat16
-    )
 
 
 def gather_group(record):
@@ -88,11 +80,14 @@
     out_ref[...] = (even_acc + odd_acc[:, lag : lag + samples]) / channels
 
 
-def lag_kernels(normalized):
-    members, channels, window = normalized.shape
+def lag_kernels(templates):
+    members, channels, window = templates.shape
     parts = window // LAG_BLOCK
-    kernels = normalized.reshape(members, channels, parts, LAG_BLOCK)[..., ::-1]
-    return jnp.transpose(kernels, (1, 2, 0, 3)).reshape(channels, parts * members, LAG_BLOCK)
+    laid = templates.reshape(members, channels, parts, LAG_BLOCK)[..., ::-1]
+    laid = jnp.transpose(laid, (1, 2, 0, 3)).astype(jnp.float32)
+    centred = laid - jnp.mean(laid, axis=(1, 3), keepdims=True)
+    norm = jnp.sqrt(jnp.sum(centred * centred, axis=(1, 3), keepdims=True) + 1e-06)
+    return (centred / norm).astype(jnp.bfloat16).reshape(channels, parts * members, LAG_BLOCK)
 
 
 def stacked_correlation(extended, kernels, window, outputs):
@@ -115,7 +110,7 @@
     nblk = lax.axis_size(BLK)
     group = gather_group(record)
     head = next_group_head(group, samples)
-    kernels = lag_kernels(normalize(templates))
+    kernels = lag_kernels(templates)
     inner = group.shape[1] - samples
     early = stacked_correlation(group, kernels, window, inner)
     tail = jnp.concatenate([group[:, inner:], head], axis=1)

time: 111 us -> 109 us (0.982)
  starting transfers between devices: 24.6 us -> 22.9 us
    ppermute x1, starting transfers between devices: 5.97 us -> 4.36 us  [next_group_head(): lax.ppermute(group[:, :samples], 'seg', [(i + 1, i) for i in range(nseg -...]
    rev x1, local copies, waits for them, and re-layouts: 1.89 us -> 0.68 us  [lag_kernels(): laid = templates.reshape(members, channels, parts, LAG_BLOCK)[..., ::-1]]
    reshape x2, local copies, waits for them, and re-layouts: 0.9 us -> 2.05 us  [lag_kernels(): laid = templates.reshape(members, channels, parts, LAG_BLOCK)[..., ::-1]]
  transfers between devices with their start and end apart: 3 -> 3, of which waited for: 2 -> 1; matrix products, arithmetic and copies ran while one was open for 4% -> 4% of each run, Pallas kernels for 10% -> 11%
where the time goes in v8:
time: 109 us
  blocking collectives  55.5 us (51%)
  starting transfers between devices  22.9 us (21%)
  Pallas kernels  16 us (15%)
  waiting for transfers between devices  6.17 us (6%)
  local copies, waits for them, and re-layouts  4.81 us (4%)
  other arithmetic  3.54 us (3%)
    all_to_all x1, blocking collectives, body(): spread = lax.all_to_all(pieces, BLK, 1, 0, tiled=True)  31.8 us
    all_to_all x1, blocking collectives, seg_sum(): return jnp.sum(lax.all_to_all(copies, 'seg', 0, 0, tiled=True), axis=0)  23.7 us
    pallas_call x2, Pallas kernels, stacked_correlation(): pl.pallas_call(corr_kernel, out_shape=jax.ShapeDtypeStruct((members, outp...  16 us
    ppermute x1, starting transfers between devices, gather_group(): partner = lax.ppermute(record, 'bz', [(0, 1), (1, 0)])  14.5 us
    all_to_all x1, waiting for transfers between devices, gather_group(): group = lax.all_to_all(copies, 'bx', 0, 0, tiled=True)  6.16 us
    ppermute x1, starting transfers between devices, next_group_head(): lax.ppermute(group[:, :samples], 'seg', [(i + 1, i) for i in range(nseg -...  4.36 us
    all_to_all x1, starting transfers between devices, gather_group(): group = lax.all_to_all(copies, 'bx', 0, 0, tiled=True)  4.01 us
  transfers between devices with their start and end apart: 3, of which 1 were waited for; matrix products, arithmetic and copies ran while one was open for 4% of the time, Pallas kernels for 11%

profile of v8, /device:TPU:33, one launch (start us, length us, event | category | flops | bytes accessed | tf_op | source)
XLA Modules:
  0.0 109.0 jit_solution(13234441319398774004)
XLA Ops:
  0.0 14.5 %collective-permute-start = (f32[24,512]{1,0:T(8,128)}, f32[24,512]{1,0:T(8,128)S(1)}, u32[]{:S(2)}, u32[]{:S(2)}) collective-permute-start(f32[24,512]{1,0:T(8,128)} %param.2), channel_id=1, source_target_pairs={{0,1},{1,0},{2,3},{3,2},{4,5},{5,4},{6,7},{7,6},{8,9},{9,8},{10,11... | collective-permute-start | bytes 147464 | tf_op jit(solution)/shard_map/ppermute | solution.py:13
  14.5 1.5 %reshape.71 = bf16[16,24,8,64]{3,2,1,0:T(8,128)(2,1)S(1)} reshape(bf16[16,24,512]{2,1,0:T(8,128)(2,1)} %param.3) | data formatting | bytes 786432 | tf_op jit(solution)/shard_map/reshape | solution.py:86
  16.1 0.5 copy.12
  16.6 0.7 rev.3
  17.3 0.0 copy-start.2
  17.3 0.2 bitcast_reduce_fusion
  17.6 0.0 collective-permute-done
  17.6 0.5 copy-done.2
  18.1 0.8 broadcast_in_dim.4
  18.9 4.0 %all-to-all-start = ((f32[4,24,1024]{2,1,0:T(8,128)}), f32[4,24,1024]{2,1,0:T(8,128)S(1)}, u32[]{:S(2)}, u32[]{:S(2)}) async-start(f32[4,24,1024]{2,1,0:T(8,128)} %broadcast_in_dim.4), calls=%async_computation | async-start | bytes 786432 | tf_op jit(solution)/shard_map/all_to_all | solution.py:19
  22.9 0.4 fusion.2
  23.3 6.2 %all-to-all-done = f32[4,24,1024]{2,1,0:T(8,128)S(1)} async-done(((f32[4,24,1024]{2,1,0:T(8,128)}), f32[4,24,1024]{2,1,0:T(8,128)S(1)}, u32[]{:S(2)}, u32[]{:S(2)}) %all-to-all-start) | async-done | bytes 393248 | tf_op jit(solution)/shard_map/all_to_all | solution.py:19
  29.5 4.4 %collective-permute-start.1 = (f32[24,512]{1,0:T(8,128)S(1)}, f32[24,512]{1,0:T(8,128)S(1)}, u32[]{:S(2)}, u32[]{:S(2)}) collective-permute-start(f32[24,512]{1,0:T(8,128)S(1)} %get-tuple-element.6), channel_id=1, source_target_pairs={{8,0},{16,8},{24,16},{32,24},{40,32},{48,40},{56,48},{64,56},{72,6... | collective-permute-start | bytes 147464 | tf_op jit(solution)/shard_map/ppermute | solution.py:25
  33.9 1.2 %fusion.3 = bf16[24,8,16,64]{3,2,1,0:T(8,128)(2,1)} fusion(bf16[16,24,8,64]{3,0,2,1:T(8,128)(2,1)S(1)} %rev.3, f32[24,16]{1,0:T(8,128)S(1)} %add_sqrt_fusion, f32[24,16]{1,0:T(8,128)S(1)} %broadcast_multiply_fusion), kind=kLoop, calls=%fused_computation.5 | loop fusion | flops 786432 | bytes 789504 | tf_op jit(solution)/shard_map/convert_element_type | solution.py:90
  35.1 11.6 %shard_map.28 = f32[16,3584]{1,0:T(8,128)} custom-call(f32[24,4096]{1,0:T(8,128)} %bitcast.26, bf16[24,128,64]{2,1,0:T(8,128)(2,1)} %bitcast.23), custom_call_target="tpu_custom_call" | custom-call | tf_op jit(solution)/shard_map/pallas_call | solution.py:95
  46.6 0.0 collective-permute-done.1
  46.6 0.6 pad_maximum_fusion.1.rec_ref
  47.3 4.4 %shard_map.29 = f32[16,512]{1,0:T(8,128)} custom-call(f32[24,1024]{1,0:T(8,128)} %pad_maximum_fusion.1.rec_ref, bf16[24,128,64]{2,1,0:T(8,128)(2,1)} %bitcast.24), custom_call_target="tpu_custom_call" | custom-call | tf_op jit(solution)/shard_map/pallas_call | solution.py:95
  51.7 0.9 multiply_reduce_fusion
  52.6 23.7 %all_to_all.26 = f32[64,1,16]{2,1,0:T(1,128)S(1)} all-to-all(f32[64,1,16]{2,1,0:T(1,128)S(1)} %broadcast_in_dim.5), channel_id=1, replica_groups=mesh['seg'=64,'bx'=4,'bz'=2] {'seg'}, dimensions={0} | all-to-all | bytes 8192 | tf_op jit(solution)/shard_map/all_to_all | solution.py:104
  76.3 0.1 reduce_sum.39
  76.4 0.1 bitcast_divide_fusion
  76.5 31.8 %all_to_all.27 = f32[16,8,512]{2,0,1:T(8,128)S(1)} all-to-all(f32[16,8,512]{2,0,1:T(8,128)S(1)} %bitcast_divide_fusion), channel_id=1, replica_groups=mesh['seg'=64,'bx'=4,'bz'=2] {'bx','bz'}, dimensions={1} | all-to-all | bytes 524288 | tf_op jit(solution)/shard_map/all_to_all | solution.py:124
  108.3 0.7 copy.20
  (11 shorter events, 0.1 us)
Async XLA Ops:
  0.0 17.6 %collective-permute-start = (f32[24,512]{1,0:T(8,128)}, f32[24,512]{1,0:T(8,128)S(1)}, u32[]{:S(2)}, u32[]{:S(2)}) collective-permute-start(f32[24,512]{1,0:T(8,128)} %param.2), channel_id=1, source_target_pairs={{0,1},{1,0},{2,3},{3,2},{4,5},{5,4},{6,7},{7,6},{8,9},{9,8},{10,11... | collective-permute-start | bytes 147464 | tf_op jit(solution)/shard_map/ppermute | solution.py:13
  17.3 0.8 copy-start.2
  18.9 10.6 %all-to-all-start = ((f32[4,24,1024]{2,1,0:T(8,128)}), f32[4,24,1024]{2,1,0:T(8,128)S(1)}, u32[]{:S(2)}, u32[]{:S(2)}) async-start(f32[4,24,1024]{2,1,0:T(8,128)} %broadcast_in_dim.4), calls=%async_computation | async-start | bytes 786432 | tf_op jit(solution)/shard_map/all_to_all | solution.py:19
  29.5 5.6 %copy-start = (f32[4,3,8,1024]{3,2,0,1:T(8,128)}, f32[4,3,8,1024]{3,2,0,1:T(8,128)S(1)}, u32[]{:S(2)}) copy-start(f32[4,3,8,1024]{3,2,0,1:T(8,128)S(1)} %copy.17) | copy-start | bytes 1179652
  29.5 17.1 %collective-permute-start.1 = (f32[24,512]{1,0:T(8,128)S(1)}, f32[24,512]{1,0:T(8,128)S(1)}, u32[]{:S(2)}, u32[]{:S(2)}) collective-permute-start(f32[24,512]{1,0:T(8,128)S(1)} %get-tuple-element.6), channel_id=1, source_target_pairs={{8,0},{16,8},{24,16},{32,24},{40,32},{48,40},{56,48},{64,56},{72,6... | collective-permute-start | bytes 147464 | tf_op jit(solution)/shard_map/ppermute | solution.py:25
  46.6 5.1 %copy-start.1 = (f32[16,3584]{1,0:T(8,128)S(1)}, f32[16,3584]{1,0:T(8,128)}, u32[]{:S(2)}) copy-start(f32[16,3584]{1,0:T(8,128)} %shard_map.28) | copy-start | bytes 688132

commit v9 on v8

--- a/solution.py
+++ b/solution.py
@@ -120,9 +120,15 @@
     record_len = samples * lax.axis_size("seg") * nblk
     detection = stacked / jnp.sqrt(power_sum / record_len + 1e-06)[:, None]
     members = detection.shape[0]
-    pieces = detection.reshape(members, nblk, samples)
-    spread = lax.all_to_all(pieces, BLK, 1, 0, tiled=True)
-    return spread.reshape(members * nblk, samples)
+    pieces = detection.reshape(members, nblk // 2, 2, samples)
+    near = lax.all_to_all(pieces, "bx", 1, 1, tiled=True)
+    side = lax.axis_index("bz")
+    own = lax.dynamic_index_in_dim(near, side, axis=2, keepdims=False)
+    other = lax.dynamic_index_in_dim(near, 1 - side, axis=2, keepdims=False)
+    far = lax.ppermute(other, "bz", [(0, 1), (1, 0)])
+    low = side == 0
+    both = jnp.where(low, jnp.stack([own, far], axis=2), jnp.stack([far, own], axis=2))
+    return jnp.transpose(both, (1, 2, 0, 3)).reshape(members * nblk, samples)
 
 
 BLK = ("bx", "bz")

time: 109 us -> 113 us (1.037)
  blocking collectives: 55.5 us -> 0 us
  waiting for transfers between devices: 6.17 us -> 39.8 us
  starting transfers between devices: 22.9 us -> 46.5 us
  local copies, waits for them, and re-layouts: 4.81 us -> 6.14 us
    all_to_all x2 -> x0, blocking collectives: 55.5 us -> none  [the longest x1 31.8 us: body(): spread = lax.all_to_all(pieces, BLK, 1, 0, tiled=True)]
    ppermute x0 -> x1, waiting for transfers between devices: none -> 17.3 us  [body(): far = lax.ppermute(other, 'bz', [(0, 1), (1, 0)])]
    all_to_all x0 -> x2, starting transfers between devices: none -> 16.4 us  [the longest x1 13 us: seg_sum(): return jnp.sum(lax.all_to_all(copies, 'seg', 0, 0, tiled=True), axis=0)]
    all_to_all x0 -> x2, waiting for transfers between devices: none -> 16.4 us  [the longest x1 10.6 us: seg_sum(): return jnp.sum(lax.all_to_all(copies, 'seg', 0, 0, tiled=True), axis=0)]
    ppermute x0 -> x1, starting transfers between devices: none -> 7.16 us  [body(): far = lax.ppermute(other, 'bz', [(0, 1), (1, 0)])]
  transfers between devices with their start and end apart: 3 -> 6, of which waited for: 1 -> 4; matrix products, arithmetic and copies ran while one was open for 4% -> 4% of each run, Pallas kernels for 11% -> 10%
where the time goes in v9:
time: 113 us
  starting transfers between devices  46.5 us (41%)
  waiting for transfers between devices  39.8 us (35%)
  Pallas kernels  16 us (14%)
  local copies, waits for them, and re-layouts  6.14 us (5%)
  other arithmetic  4.34 us (4%)
    ppermute x1, waiting for transfers between devices, body(): far = lax.ppermute(other, 'bz', [(0, 1), (1, 0)])  17.3 us
    pallas_call x2, Pallas kernels, stacked_correlation(): pl.pallas_call(corr_kernel, out_shape=jax.ShapeDtypeStruct((members, outp...  16 us
    ppermute x1, starting transfers between devices, gather_group(): partner = lax.ppermute(record, 'bz', [(0, 1), (1, 0)])  14.5 us
    all_to_all x1, starting transfers between devices, seg_sum(): return jnp.sum(lax.all_to_all(copies, 'seg', 0, 0, tiled=True), axis=0)  13 us
    all_to_all x1, waiting for transfers between devices, seg_sum(): return jnp.sum(lax.all_to_all(copies, 'seg', 0, 0, tiled=True), axis=0)  10.6 us
    ppermute x1, starting transfers between devices, body(): far = lax.ppermute(other, 'bz', [(0, 1), (1, 0)])  7.16 us
    all_to_all x1, waiting for transfers between devices, gather_group(): group = lax.all_to_all(copies, 'bx', 0, 0, tiled=True)  6.16 us
    all_to_all x1, waiting for transfers between devices, body(): near = lax.all_to_all(pieces, 'bx', 1, 1, tiled=True)  5.77 us
  transfers between devices with their start and end apart: 6, of which 4 were waited for; matrix products, arithmetic and copies ran while one was open for 4% of the time, Pallas kernels for 10%

profile of v9, /device:TPU:33, one launch (start us, length us, event | category | flops | bytes accessed | tf_op | source)
XLA Modules:
  0.0 112.9 jit_solution(12433083638229206581)
XLA Ops:
  0.0 14.5 %collective-permute-start = (f32[24,512]{1,0:T(8,128)}, f32[24,512]{1,0:T(8,128)S(1)}, u32[]{:S(2)}, u32[]{:S(2)}) collective-permute-start(f32[24,512]{1,0:T(8,128)} %param.2), channel_id=1, source_target_pairs={{0,1},{1,0},{2,3},{3,2},{4,5},{5,4},{6,7},{7,6},{8,9},{9,8},{10,11... | collective-permute-start | bytes 147464 | tf_op jit(solution)/shard_map/ppermute | solution.py:13
  14.5 1.5 %reshape.70 = bf16[16,24,8,64]{3,2,1,0:T(8,128)(2,1)S(1)} reshape(bf16[16,24,512]{2,1,0:T(8,128)(2,1)} %param.3) | data formatting | bytes 786432 | tf_op jit(solution)/shard_map/reshape | solution.py:86
  16.1 0.5 copy.22
  16.6 0.7 rev.3
  17.6 0.5 copy-done.2
  18.1 0.8 broadcast_in_dim.4
  18.9 4.0 %all-to-all-start = ((f32[4,24,1024]{2,1,0:T(8,128)}), f32[4,24,1024]{2,1,0:T(8,128)S(1)}, u32[]{:S(2)}, u32[]{:S(2)}) async-start(f32[4,24,1024]{2,1,0:T(8,128)} %broadcast_in_dim.4), calls=%async_computation | async-start | bytes 786432 | tf_op jit(solution)/shard_map/all_to_all | solution.py:19
  22.9 0.4 fusion.2
  23.3 6.2 %all-to-all-done = f32[4,24,1024]{2,1,0:T(8,128)S(1)} async-done(((f32[4,24,1024]{2,1,0:T(8,128)}), f32[4,24,1024]{2,1,0:T(8,128)S(1)}, u32[]{:S(2)}, u32[]{:S(2)}) %all-to-all-start) | async-done | bytes 393248 | tf_op jit(solution)/shard_map/all_to_all | solution.py:19
  29.5 4.4 %collective-permute-start.1 = (f32[24,512]{1,0:T(8,128)S(1)}, f32[24,512]{1,0:T(8,128)S(1)}, u32[]{:S(2)}, u32[]{:S(2)}) collective-permute-start(f32[24,512]{1,0:T(8,128)S(1)} %get-tuple-element.6), channel_id=1, source_target_pairs={{8,0},{16,8},{24,16},{32,24},{40,32},{48,40},{56,48},{64,56},{72,6... | collective-permute-start | bytes 147464 | tf_op jit(solution)/shard_map/ppermute | solution.py:25
  33.9 1.2 %fusion.3 = bf16[24,8,16,64]{3,2,1,0:T(8,128)(2,1)} fusion(bf16[16,24,8,64]{3,0,2,1:T(8,128)(2,1)S(1)} %rev.3, f32[24,16]{1,0:T(8,128)S(1)} %add_sqrt_fusion, f32[24,16]{1,0:T(8,128)S(1)} %broadcast_multiply_fusion), kind=kLoop, calls=%fused_computation.5 | loop fusion | flops 786432 | bytes 789504 | tf_op jit(solution)/shard_map/convert_element_type | solution.py:90
  35.1 11.5 %shard_map.28 = f32[16,3584]{1,0:T(8,128)} custom-call(f32[24,4096]{1,0:T(8,128)} %bitcast.25, bf16[24,128,64]{2,1,0:T(8,128)(2,1)} %bitcast.22), custom_call_target="tpu_custom_call" | custom-call | tf_op jit(solution)/shard_map/pallas_call | solution.py:95
  46.6 0.6 pad_maximum_fusion.1.rec_ref
  47.3 4.4 %shard_map.29 = f32[16,512]{1,0:T(8,128)} custom-call(f32[24,1024]{1,0:T(8,128)} %pad_maximum_fusion.1.rec_ref, bf16[24,128,64]{2,1,0:T(8,128)(2,1)} %bitcast.23), custom_call_target="tpu_custom_call" | custom-call | tf_op jit(solution)/shard_map/pallas_call | solution.py:95
  51.7 0.9 multiply_reduce_fusion
  52.6 0.6 broadcast_in_dim.5
  53.3 13.0 %all-to-all-start.1 = ((f32[64,1,16]{2,1,0:T(1,128)}), f32[64,1,16]{2,1,0:T(1,128)S(1)}, u32[]{:S(2)}, u32[]{:S(2)}) async-start(f32[64,1,16]{2,1,0:T(1,128)} %broadcast_in_dim.5), calls=%async_computation.1 | async-start | bytes 65536 | tf_op jit(solution)/shard_map/all_to_all | solution.py:104
  66.5 10.6 %all-to-all-done.1 = f32[64,1,16]{2,1,0:T(1,128)S(1)} async-done(((f32[64,1,16]{2,1,0:T(1,128)}), f32[64,1,16]{2,1,0:T(1,128)S(1)}, u32[]{:S(2)}, u32[]{:S(2)}) %all-to-all-start.1) | async-done | bytes 4128 | tf_op jit(solution)/shard_map/all_to_all | solution.py:104
  77.4 0.9 copy.25
  78.3 3.4 %all-to-all-start.2 = ((f32[16,4,2,512]{3,2,0,1:T(2,128)}), f32[16,4,2,512]{3,2,0,1:T(2,128)S(1)}, u32[]{:S(2)}, u32[]{:S(2)}) async-start(f32[16,4,2,512]{3,2,0,1:T(2,128)} %copy.25), calls=%async_computation.2 | async-start | bytes 524288 | tf_op jit(solution)/shard_map/all_to_all | solution.py:124
  81.7 5.8 %all-to-all-done.2 = f32[16,4,2,512]{3,2,0,1:T(2,128)S(1)} async-done(((f32[16,4,2,512]{3,2,0,1:T(2,128)}), f32[16,4,2,512]{3,2,0,1:T(2,128)S(1)}, u32[]{:S(2)}, u32[]{:S(2)}) %all-to-all-start.2) | async-done | bytes 262176 | tf_op jit(solution)/shard_map/all_to_all | solution.py:124
  87.7 7.2 %collective-permute-start.2 = (f32[16,4,512]{2,0,1:T(8,128)S(1)}, f32[16,4,512]{2,0,1:T(8,128)S(1)}, u32[]{:S(2)}, u32[]{:S(2)}) collective-permute-start(f32[16,4,512]{2,0,1:T(8,128)S(1)} %bitcast.28), channel_id=1, source_target_pairs={{0,1},{1,0},{2,3},{3,2},{4,5},{5,4},{6,7},{7,6},{8,9},{9,8},{10,11... | collective-permute-start | bytes 393224 | tf_op jit(solution)/shard_map/ppermute | solution.py:128
  94.9 17.3 %collective-permute-done.2 = f32[16,4,512]{2,0,1:T(8,128)S(1)} collective-permute-done((f32[16,4,512]{2,0,1:T(8,128)S(1)}, f32[16,4,512]{2,0,1:T(8,128)S(1)}, u32[]{:S(2)}, u32[]{:S(2)}) %collective-permute-start.2) | collective-permute-done | bytes 131104 | tf_op jit(solution)/shard_map/ppermute | solution.py:128
  112.1 0.7 maximum_select_fusion
  (20 shorter events, 1.1 us)
Async XLA Ops:
  0.0 17.6 %collective-permute-start = (f32[24,512]{1,0:T(8,128)}, f32[24,512]{1,0:T(8,128)S(1)}, u32[]{:S(2)}, u32[]{:S(2)}) collective-permute-start(f32[24,512]{1,0:T(8,128)} %param.2), channel_id=1, source_target_pairs={{0,1},{1,0},{2,3},{3,2},{4,5},{5,4},{6,7},{7,6},{8,9},{9,8},{10,11... | collective-permute-start | bytes 147464 | tf_op jit(solution)/shard_map/ppermute | solution.py:13
  17.3 0.8 copy-start.2
  18.9 10.6 %all-to-all-start = ((f32[4,24,1024]{2,1,0:T(8,128)}), f32[4,24,1024]{2,1,0:T(8,128)S(1)}, u32[]{:S(2)}, u32[]{:S(2)}) async-start(f32[4,24,1024]{2,1,0:T(8,128)} %broadcast_in_dim.4), calls=%async_computation | async-start | bytes 786432 | tf_op jit(solution)/shard_map/all_to_all | solution.py:19
  29.5 5.6 %copy-start = (f32[4,3,8,1024]{3,2,0,1:T(8,128)}, f32[4,3,8,1024]{3,2,0,1:T(8,128)S(1)}, u32[]{:S(2)}) copy-start(f32[4,3,8,1024]{3,2,0,1:T(8,128)S(1)} %copy.30) | copy-start | bytes 1179652
  29.5 17.1 %collective-permute-start.1 = (f32[24,512]{1,0:T(8,128)S(1)}, f32[24,512]{1,0:T(8,128)S(1)}, u32[]{:S(2)}, u32[]{:S(2)}) collective-permute-start(f32[24,512]{1,0:T(8,128)S(1)} %get-tuple-element.6), channel_id=1, source_target_pairs={{8,0},{16,8},{24,16},{32,24},{40,32},{48,40},{56,48},{64,56},{72,6... | collective-permute-start | bytes 147464 | tf_op jit(solution)/shard_map/ppermute | solution.py:25
  46.6 5.1 %copy-start.1 = (f32[16,3584]{1,0:T(8,128)S(1)}, f32[16,3584]{1,0:T(8,128)}, u32[]{:S(2)}) copy-start(f32[16,3584]{1,0:T(8,128)} %shard_map.28) | copy-start | bytes 688132
  53.3 23.8 %all-to-all-start.1 = ((f32[64,1,16]{2,1,0:T(1,128)}), f32[64,1,16]{2,1,0:T(1,128)S(1)}, u32[]{:S(2)}, u32[]{:S(2)}) async-start(f32[64,1,16]{2,1,0:T(1,128)} %broadcast_in_dim.5), calls=%async_computation.1 | async-start | bytes 65536 | tf_op jit(solution)/shard_map/all_to_all | solution.py:104
  78.3 9.2 %all-to-all-start.2 = ((f32[16,4,2,512]{3,2,0,1:T(2,128)}), f32[16,4,2,512]{3,2,0,1:T(2,128)S(1)}, u32[]{:S(2)}, u32[]{:S(2)}) async-start(f32[16,4,2,512]{3,2,0,1:T(2,128)} %copy.25), calls=%async_computation.2 | async-start | bytes 524288 | tf_op jit(solution)/shard_map/all_to_all | solution.py:124
  87.7 24.4 %collective-permute-start.2 = (f32[16,4,512]{2,0,1:T(8,128)S(1)}, f32[16,4,512]{2,0,1:T(8,128)S(1)}, u32[]{:S(2)}, u32[]{:S(2)}) collective-permute-start(f32[16,4,512]{2,0,1:T(8,128)S(1)} %bitcast.28), channel_id=1, source_target_pairs={{0,1},{1,0},{2,3},{3,2},{4,5},{5,4},{6,7},{7,6},{8,9},{9,8},{10,11... | collective-permute-start | bytes 393224 | tf_op jit(solution)/shard_map/ppermute | solution.py:128

commit v10 on v8

--- a/solution.py
+++ b/solution.py
@@ -76,7 +76,7 @@
         jnp.zeros((members, samples), jnp.float32),
         jnp.zeros((members, odd_width), jnp.float32),
     )
-    even_acc, odd_acc = lax.fori_loop(0, channels // ROWS, one_group, start)
+    even_acc, odd_acc = lax.fori_loop(0, channels // ROWS, one_group, start, unroll=True)
     out_ref[...] = (even_acc + odd_acc[:, lag : lag + samples]) / channels
 
 

time: 109 us -> 108 us (level)
  Pallas kernels: 16 us -> 14.7 us
    pallas_call x2, Pallas kernels: 16 us -> 14.7 us  [stacked_correlation(): pl.pallas_call(corr_kernel, out_shape=jax.ShapeDtypeStruct((members, outp...]
  transfers between devices with their start and end apart: 3 -> 3, of which waited for: 1 -> 1; matrix products, arithmetic and copies ran while one was open for 4% -> 4% of each run, Pallas kernels for 11% -> 10%
where the time goes in v10:
time: 108 us
  blocking collectives  55.5 us (51%)
  starting transfers between devices  22.9 us (21%)
  Pallas kernels  14.7 us (14%)
  waiting for transfers between devices  6.17 us (6%)
  local copies, waits for them, and re-layouts  4.81 us (4%)
  other arithmetic  3.54 us (3%)
    all_to_all x1, blocking collectives, body(): spread = lax.all_to_all(pieces, BLK, 1, 0, tiled=True)  31.8 us
    all_to_all x1, blocking collectives, seg_sum(): return jnp.sum(lax.all_to_all(copies, 'seg', 0, 0, tiled=True), axis=0)  23.7 us
    pallas_call x2, Pallas kernels, stacked_correlation(): pl.pallas_call(corr_kernel, out_shape=jax.ShapeDtypeStruct((members, outp...  14.7 us
    ppermute x1, starting transfers between devices, gather_group(): partner = lax.ppermute(record, 'bz', [(0, 1), (1, 0)])  14.5 us
    all_to_all x1, waiting for transfers between devices, gather_group(): group = lax.all_to_all(copies, 'bx', 0, 0, tiled=True)  6.16 us
    ppermute x1, starting transfers between devices, next_group_head(): lax.ppermute(group[:, :samples], 'seg', [(i + 1, i) for i in range(nseg -...  4.36 us
    all_to_all x1, starting transfers between devices, gather_group(): group = lax.all_to_all(copies, 'bx', 0, 0, tiled=True)  4.01 us
  transfers between devices with their start and end apart: 3, of which 1 were waited for; matrix products, arithmetic and copies ran while one was open for 4% of the time, Pallas kernels for 10%

profile of v10, /device:TPU:33, one launch (start us, length us, event | category | flops | bytes accessed | tf_op | source)
XLA Modules:
  0.0 107.8 jit_solution(17616215213939610936)
XLA Ops:
  0.0 14.5 %collective-permute-start = (f32[24,512]{1,0:T(8,128)}, f32[24,512]{1,0:T(8,128)S(1)}, u32[]{:S(2)}, u32[]{:S(2)}) collective-permute-start(f32[24,512]{1,0:T(8,128)} %param.2), channel_id=1, source_target_pairs={{0,1},{1,0},{2,3},{3,2},{4,5},{5,4},{6,7},{7,6},{8,9},{9,8},{10,11... | collective-permute-start | bytes 147464 | tf_op jit(solution)/shard_map/ppermute | solution.py:13
  14.5 1.5 %reshape.71 = bf16[16,24,8,64]{3,2,1,0:T(8,128)(2,1)S(1)} reshape(bf16[16,24,512]{2,1,0:T(8,128)(2,1)} %param.3) | data formatting | bytes 786432 | tf_op jit(solution)/shard_map/reshape | solution.py:86
  16.1 0.5 copy.12
  16.6 0.7 rev.3
  17.3 0.0 copy-start.2
  17.3 0.2 bitcast_reduce_fusion
  17.6 0.0 collective-permute-done
  17.6 0.5 copy-done.2
  18.1 0.8 broadcast_in_dim.4
  18.9 4.0 %all-to-all-start = ((f32[4,24,1024]{2,1,0:T(8,128)}), f32[4,24,1024]{2,1,0:T(8,128)S(1)}, u32[]{:S(2)}, u32[]{:S(2)}) async-start(f32[4,24,1024]{2,1,0:T(8,128)} %broadcast_in_dim.4), calls=%async_computation | async-start | bytes 786432 | tf_op jit(solution)/shard_map/all_to_all | solution.py:19
  22.9 0.4 fusion.2
  23.3 6.2 %all-to-all-done = f32[4,24,1024]{2,1,0:T(8,128)S(1)} async-done(((f32[4,24,1024]{2,1,0:T(8,128)}), f32[4,24,1024]{2,1,0:T(8,128)S(1)}, u32[]{:S(2)}, u32[]{:S(2)}) %all-to-all-start) | async-done | bytes 393248 | tf_op jit(solution)/shard_map/all_to_all | solution.py:19
  29.5 4.4 %collective-permute-start.1 = (f32[24,512]{1,0:T(8,128)S(1)}, f32[24,512]{1,0:T(8,128)S(1)}, u32[]{:S(2)}, u32[]{:S(2)}) collective-permute-start(f32[24,512]{1,0:T(8,128)S(1)} %get-tuple-element.6), channel_id=1, source_target_pairs={{8,0},{16,8},{24,16},{32,24},{40,32},{48,40},{56,48},{64,56},{72,6... | collective-permute-start | bytes 147464 | tf_op jit(solution)/shard_map/ppermute | solution.py:25
  33.9 1.2 %fusion.3 = bf16[24,8,16,64]{3,2,1,0:T(8,128)(2,1)} fusion(bf16[16,24,8,64]{3,0,2,1:T(8,128)(2,1)S(1)} %rev.3, f32[24,16]{1,0:T(8,128)S(1)} %add_sqrt_fusion, f32[24,16]{1,0:T(8,128)S(1)} %broadcast_multiply_fusion), kind=kLoop, calls=%fused_computation.5 | loop fusion | flops 786432 | bytes 789504 | tf_op jit(solution)/shard_map/convert_element_type | solution.py:90
  35.1 10.6 %shard_map.28 = f32[16,3584]{1,0:T(8,128)} custom-call(f32[24,4096]{1,0:T(8,128)} %bitcast.26, bf16[24,128,64]{2,1,0:T(8,128)(2,1)} %bitcast.23), custom_call_target="tpu_custom_call" | custom-call | tf_op jit(solution)/shard_map/pallas_call | solution.py:95
  45.7 0.0 collective-permute-done.1
  45.7 0.6 pad_maximum_fusion.1.rec_ref
  46.3 4.1 %shard_map.29 = f32[16,512]{1,0:T(8,128)} custom-call(f32[24,1024]{1,0:T(8,128)} %pad_maximum_fusion.1.rec_ref, bf16[24,128,64]{2,1,0:T(8,128)(2,1)} %bitcast.24), custom_call_target="tpu_custom_call" | custom-call | tf_op jit(solution)/shard_map/pallas_call | solution.py:95
  50.4 0.9 multiply_reduce_fusion
  51.4 23.7 %all_to_all.26 = f32[64,1,16]{2,1,0:T(1,128)S(1)} all-to-all(f32[64,1,16]{2,1,0:T(1,128)S(1)} %broadcast_in_dim.5), channel_id=1, replica_groups=mesh['seg'=64,'bx'=4,'bz'=2] {'seg'}, dimensions={0} | all-to-all | bytes 8192 | tf_op jit(solution)/shard_map/all_to_all | solution.py:104
  75.1 0.1 reduce_sum.39
  75.2 0.1 bitcast_divide_fusion
  75.3 31.8 %all_to_all.27 = f32[16,8,512]{2,0,1:T(8,128)S(1)} all-to-all(f32[16,8,512]{2,0,1:T(8,128)S(1)} %bitcast_divide_fusion), channel_id=1, replica_groups=mesh['seg'=64,'bx'=4,'bz'=2] {'bx','bz'}, dimensions={1} | all-to-all | bytes 524288 | tf_op jit(solution)/shard_map/all_to_all | solution.py:124
  107.1 0.7 copy.20
  (11 shorter events, 0.1 us)
Async XLA Ops:
  0.0 17.6 %collective-permute-start = (f32[24,512]{1,0:T(8,128)}, f32[24,512]{1,0:T(8,128)S(1)}, u32[]{:S(2)}, u32[]{:S(2)}) collective-permute-start(f32[24,512]{1,0:T(8,128)} %param.2), channel_id=1, source_target_pairs={{0,1},{1,0},{2,3},{3,2},{4,5},{5,4},{6,7},{7,6},{8,9},{9,8},{10,11... | collective-permute-start | bytes 147464 | tf_op jit(solution)/shard_map/ppermute | solution.py:13
  17.3 0.8 copy-start.2
  18.9 10.6 %all-to-all-start = ((f32[4,24,1024]{2,1,0:T(8,128)}), f32[4,24,1024]{2,1,0:T(8,128)S(1)}, u32[]{:S(2)}, u32[]{:S(2)}) async-start(f32[4,24,1024]{2,1,0:T(8,128)} %broadcast_in_dim.4), calls=%async_computation | async-start | bytes 786432 | tf_op jit(solution)/shard_map/all_to_all | solution.py:19
  29.5 5.6 %copy-start = (f32[4,3,8,1024]{3,2,0,1:T(8,128)}, f32[4,3,8,1024]{3,2,0,1:T(8,128)S(1)}, u32[]{:S(2)}) copy-start(f32[4,3,8,1024]{3,2,0,1:T(8,128)S(1)} %copy.17) | copy-start | bytes 1179652
  29.5 16.1 %collective-permute-start.1 = (f32[24,512]{1,0:T(8,128)S(1)}, f32[24,512]{1,0:T(8,128)S(1)}, u32[]{:S(2)}, u32[]{:S(2)}) collective-permute-start(f32[24,512]{1,0:T(8,128)S(1)} %get-tuple-element.6), channel_id=1, source_target_pairs={{8,0},{16,8},{24,16},{32,24},{40,32},{48,40},{56,48},{64,56},{72,6... | collective-permute-start | bytes 147464 | tf_op jit(solution)/shard_map/ppermute | solution.py:25
  45.7 4.8 %copy-start.1 = (f32[16,3584]{1,0:T(8,128)S(1)}, f32[16,3584]{1,0:T(8,128)}, u32[]{:S(2)}) copy-start(f32[16,3584]{1,0:T(8,128)} %shard_map.28) | copy-start | bytes 688132

commit v11 on v10

--- a/solution.py
+++ b/solution.py
@@ -16,8 +16,7 @@
     size = lax.axis_size("bx")
     channels, width = pair.shape
     copies = jnp.broadcast_to(pair[None], (size, channels, width))
-    group = lax.all_to_all(copies, "bx", 0, 0, tiled=True)
-    return jnp.transpose(group, (1, 0, 2)).reshape(channels, size * width)
+    return lax.all_to_all(copies, "bx", 0, 0, tiled=True)
 
 
 def next_group_head(group, samples):
@@ -38,8 +37,7 @@
     return total[:, :samples]
 
 
-def corr_kernel(rec_ref, tr_ref, out_ref):
-    channels, width = rec_ref.shape
+def corr_kernel(load_rows, channels, width, tr_ref, out_ref):
     lag = tr_ref.shape[2]
     members, samples = out_ref.shape
     parts = tr_ref.shape[1] // members
@@ -50,7 +48,7 @@
     def one_group(g, carry):
         even_acc, odd_acc = carry
         first = pl.multiple_of(g * ROWS, ROWS)
-        rows = rec_ref[pl.ds(first, ROWS), :]
+        rows = load_rows(first)
         window_sum = window_sums(rows, window, samples)
         window_sq = window_sums(rows * rows, window, samples)
         spread = window_sq - window_sum * window_sum / window
@@ -90,12 +88,39 @@
     return (centred / norm).astype(jnp.bfloat16).reshape(channels, parts * members, LAG_BLOCK)
 
 
-def stacked_correlation(extended, kernels, window, outputs):
+def early_kernel(group_ref, tr_ref, out_ref):
+    pairs, channels, width = group_ref.shape
+
+    def load_rows(first):
+        return jnp.concatenate([group_ref[m, pl.ds(first, ROWS), :] for m in range(pairs)], axis=1)
+
+    corr_kernel(load_rows, channels, pairs * width, tr_ref, out_ref)
+
+
+def late_kernel(group_ref, head_ref, tr_ref, out_ref):
+    pairs, channels, width = group_ref.shape
+    samples = head_ref.shape[1]
+
+    def load_rows(first):
+        last = group_ref[pairs - 1, pl.ds(first, ROWS), :]
+        return jnp.concatenate([last[:, width - samples :], head_ref[pl.ds(first, ROWS), :]], axis=1)
+
+    corr_kernel(load_rows, channels, 2 * samples, tr_ref, out_ref)
+
+
+def stacked_correlation(group, head, kernels, window):
+    pairs, channels, width = group.shape
+    samples = head.shape[1]
     members = kernels.shape[1] * LAG_BLOCK // window
-    return pl.pallas_call(
-        corr_kernel,
-        out_shape=jax.ShapeDtypeStruct((members, outputs), jnp.float32),
-    )(extended, kernels)
+    early = pl.pallas_call(
+        early_kernel,
+        out_shape=jax.ShapeDtypeStruct((members, pairs * width - samples), jnp.float32),
+    )(group, kernels)
+    late = pl.pallas_call(
+        late_kernel,
+        out_shape=jax.ShapeDtypeStruct((members, samples), jnp.float32),
+    )(group, head, kernels)
+    return jnp.concatenate([early, late], axis=1)
 
 
 def seg_sum(value):
@@ -109,13 +134,9 @@
     window = templates.shape[2]
     nblk = lax.axis_size(BLK)
     group = gather_group(record)
-    head = next_group_head(group, samples)
+    head = next_group_head(group[0], samples)
     kernels = lag_kernels(templates)
-    inner = group.shape[1] - samples
-    early = stacked_correlation(group, kernels, window, inner)
-    tail = jnp.concatenate([group[:, inner:], head], axis=1)
-    late = stacked_correlation(tail, kernels, window, samples)
-    stacked = jnp.concatenate([early, late], axis=1)
+    stacked = stacked_correlation(group, head, kernels, window)
     power_sum = seg_sum(jnp.sum(stacked * stacked, axis=1))
     record_len = samples * lax.axis_size("seg") * nblk
     detection = stacked / jnp.sqrt(power_sum / record_len + 1e-06)[:, None]

time: 108 us -> 108 us (level)
  no operation moved by 1% of the time
where the time goes in v11:
time: 108 us
  blocking collectives  55.5 us (51%)
  starting transfers between devices  22.9 us (21%)
  Pallas kernels  14.8 us (14%)
  waiting for transfers between devices  6.17 us (6%)
  local copies, waits for them, and re-layouts  5.4 us (5%)
  other arithmetic  2.9 us (3%)
    all_to_all x1, blocking collectives, body(): spread = lax.all_to_all(pieces, BLK, 1, 0, tiled=True)  31.8 us
    all_to_all x1, blocking collectives, seg_sum(): return jnp.sum(lax.all_to_all(copies, 'seg', 0, 0, tiled=True), axis=0)  23.7 us
    ppermute x1, starting transfers between devices, gather_group(): partner = lax.ppermute(record, 'bz', [(0, 1), (1, 0)])  14.5 us
    pallas_call x1, Pallas kernels, stacked_correlation(): pl.pallas_call(early_kernel, out_shape=jax.ShapeDtypeStruct((members, pai...  10.6 us
    all_to_all x1, waiting for transfers between devices, gather_group(): return lax.all_to_all(copies, 'bx', 0, 0, tiled=True)  6.16 us
    ppermute x1, starting transfers between devices, next_group_head(): lax.ppermute(group[:, :samples], 'seg', [(i + 1, i) for i in range(nseg -...  4.36 us
    pallas_call x1, Pallas kernels, stacked_correlation(): pl.pallas_call(late_kernel, out_shape=jax.ShapeDtypeStruct((members, samp...  4.24 us
    all_to_all x1, starting transfers between devices, gather_group(): return lax.all_to_all(copies, 'bx', 0, 0, tiled=True)  4.01 us
  transfers between devices with their start and end apart: 3, of which 1 were waited for; matrix products, arithmetic and copies ran while one was open for 4% of the time, Pallas kernels for 10%

profile of v11, /device:TPU:33, one launch (start us, length us, event | category | flops | bytes accessed | tf_op | source)
XLA Modules:
  0.0 107.8 jit_solution(8168496074341427944)
XLA Ops:
  0.0 14.5 %collective-permute-start = (f32[24,512]{1,0:T(8,128)}, f32[24,512]{1,0:T(8,128)S(1)}, u32[]{:S(2)}, u32[]{:S(2)}) collective-permute-start(f32[24,512]{1,0:T(8,128)} %param.2), channel_id=1, source_target_pairs={{0,1},{1,0},{2,3},{3,2},{4,5},{5,4},{6,7},{7,6},{8,9},{9,8},{10,11... | collective-permute-start | bytes 147464 | tf_op jit(solution)/shard_map/ppermute | solution.py:13
  14.5 1.5 %reshape.67 = bf16[16,24,8,64]{3,2,1,0:T(8,128)(2,1)S(1)} reshape(bf16[16,24,512]{2,1,0:T(8,128)(2,1)} %param.3) | data formatting | bytes 786432 | tf_op jit(solution)/shard_map/reshape | solution.py:84
  16.1 0.5 copy.9
  16.6 0.7 rev.3
  17.3 0.0 copy-start.3
  17.3 0.2 bitcast_reduce_fusion
  17.6 0.0 collective-permute-done
  17.6 0.5 copy-done.3
  18.1 0.8 broadcast_in_dim.4
  18.9 4.0 %all-to-all-start = ((f32[4,24,1024]{2,1,0:T(8,128)}), f32[4,24,1024]{2,1,0:T(8,128)S(1)}, u32[]{:S(2)}, u32[]{:S(2)}) async-start(f32[4,24,1024]{2,1,0:T(8,128)} %broadcast_in_dim.4), calls=%async_computation | async-start | bytes 786432 | tf_op jit(solution)/shard_map/all_to_all | solution.py:19
  22.9 0.4 fusion.2
  23.3 6.2 %all-to-all-done.group_ref = f32[4,24,1024]{2,1,0:T(8,128)S(1)} async-done(((f32[4,24,1024]{2,1,0:T(8,128)}), f32[4,24,1024]{2,1,0:T(8,128)S(1)}, u32[]{:S(2)}, u32[]{:S(2)}) %all-to-all-start) | async-done | bytes 393248 | tf_op jit(solution)/shard_map/all_to_all | solution.py:19
  29.5 4.4 %collective-permute-start.1 = (f32[24,512]{1,0:T(8,128)S(1)}, f32[24,512]{1,0:T(8,128)S(1)}, u32[]{:S(2)}, u32[]{:S(2)}) collective-permute-start(f32[24,512]{1,0:T(8,128)S(1)} %slice.9), channel_id=1, source_target_pairs={{8,0},{16,8},{24,16},{32,24},{40,32},{48,40},{56,48},{64,56},{72,6... | collective-permute-start | bytes 147464 | tf_op jit(solution)/shard_map/ppermute | solution.py:24
  33.9 1.2 %fusion.3 = bf16[24,8,16,64]{3,2,1,0:T(8,128)(2,1)} fusion(bf16[16,24,8,64]{3,0,2,1:T(8,128)(2,1)S(1)} %rev.3, f32[24,16]{1,0:T(8,128)S(1)} %add_sqrt_fusion, f32[24,16]{1,0:T(8,128)S(1)} %broadcast_multiply_fusion), kind=kLoop, calls=%fused_computation.5 | loop fusion | flops 786432 | bytes 789504 | tf_op jit(solution)/shard_map/convert_element_type | solution.py:88
  35.0 10.6 %shard_map.28 = f32[16,3584]{1,0:T(8,128)} custom-call(f32[4,24,1024]{2,1,0:T(8,128)} %copy-done, bf16[24,128,64]{2,1,0:T(8,128)(2,1)} %bitcast.22), custom_call_target="tpu_custom_call" | custom-call | tf_op jit(solution)/shard_map/pallas_call | solution.py:115
  45.6 0.0 collective-permute-done.1.head_ref
  45.6 0.6 copy-done.2
  46.2 4.2 %shard_map.29 = f32[16,512]{1,0:T(8,128)} custom-call(f32[4,24,1024]{2,1,0:T(8,128)} %copy-done, f32[24,512]{1,0:T(8,128)} %copy-done.2, bf16[24,128,64]{2,1,0:T(8,128)(2,1)} %bitcast.23), custom_call_target="tpu_custom_call" | custom-call | tf_op jit(solution)/shard_map/pallas_call | solution.py:119
  50.5 0.9 multiply_reduce_fusion
  51.4 23.7 %all_to_all.26 = f32[64,1,16]{2,1,0:T(1,128)S(1)} all-to-all(f32[64,1,16]{2,1,0:T(1,128)S(1)} %broadcast_in_dim.5), channel_id=1, replica_groups=mesh['seg'=64,'bx'=4,'bz'=2] {'seg'}, dimensions={0} | all-to-all | bytes 8192 | tf_op jit(solution)/shard_map/all_to_all | solution.py:129
  75.1 0.1 reduce_sum.39
  75.2 0.1 bitcast_divide_fusion
  75.3 31.8 %all_to_all.27 = f32[16,8,512]{2,0,1:T(8,128)S(1)} all-to-all(f32[16,8,512]{2,0,1:T(8,128)S(1)} %bitcast_divide_fusion), channel_id=1, replica_groups=mesh['seg'=64,'bx'=4,'bz'=2] {'bx','bz'}, dimensions={1} | all-to-all | bytes 524288 | tf_op jit(solution)/shard_map/all_to_all | solution.py:145
  107.1 0.7 copy.16
  (12 shorter events, 0.1 us)
Async XLA Ops:
  0.0 17.6 %collective-permute-start = (f32[24,512]{1,0:T(8,128)}, f32[24,512]{1,0:T(8,128)S(1)}, u32[]{:S(2)}, u32[]{:S(2)}) collective-permute-start(f32[24,512]{1,0:T(8,128)} %param.2), channel_id=1, source_target_pairs={{0,1},{1,0},{2,3},{3,2},{4,5},{5,4},{6,7},{7,6},{8,9},{9,8},{10,11... | collective-permute-start | bytes 147464 | tf_op jit(solution)/shard_map/ppermute | solution.py:13
  17.3 0.8 copy-start.3
  18.9 10.6 %all-to-all-start = ((f32[4,24,1024]{2,1,0:T(8,128)}), f32[4,24,1024]{2,1,0:T(8,128)S(1)}, u32[]{:S(2)}, u32[]{:S(2)}) async-start(f32[4,24,1024]{2,1,0:T(8,128)} %broadcast_in_dim.4), calls=%async_computation | async-start | bytes 786432 | tf_op jit(solution)/shard_map/all_to_all | solution.py:19
  29.5 5.6 %copy-start = (f32[4,24,1024]{2,1,0:T(8,128)}, f32[4,24,1024]{2,1,0:T(8,128)S(1)}, u32[]{:S(2)}) copy-start(f32[4,24,1024]{2,1,0:T(8,128)S(1)} %all-to-all-done.group_ref) | copy-start | bytes 1179652
  29.5 16.1 %collective-permute-start.1 = (f32[24,512]{1,0:T(8,128)S(1)}, f32[24,512]{1,0:T(8,128)S(1)}, u32[]{:S(2)}, u32[]{:S(2)}) collective-permute-start(f32[24,512]{1,0:T(8,128)S(1)} %slice.9), channel_id=1, source_target_pairs={{8,0},{16,8},{24,16},{32,24},{40,32},{48,40},{56,48},{64,56},{72,6... | collective-permute-start | bytes 147464 | tf_op jit(solution)/shard_map/ppermute | solution.py:24
  45.6 4.9 %copy-start.1 = (f32[16,3584]{1,0:T(8,128)S(1)}, f32[16,3584]{1,0:T(8,128)}, u32[]{:S(2)}) copy-start(f32[16,3584]{1,0:T(8,128)} %shard_map.28) | copy-start | bytes 688132
  45.6 0.6 copy-start.2

commit v12 on v11

--- a/solution.py
+++ b/solution.py
@@ -9,14 +9,15 @@
 LAG_BLOCK = 64
 
 
-def gather_group(record):
+def gather_group(record, kernels):
     partner = lax.ppermute(record, "bz", [(0, 1), (1, 0)])
     low = lax.axis_index("bz") == 0
     pair = jnp.where(low, jnp.concatenate([record, partner], axis=1), jnp.concatenate([partner, record], axis=1))
+    pair, kernels = lax.optimization_barrier((pair, kernels))
     size = lax.axis_size("bx")
     channels, width = pair.shape
     copies = jnp.broadcast_to(pair[None], (size, channels, width))
-    return lax.all_to_all(copies, "bx", 0, 0, tiled=True)
+    return lax.all_to_all(copies, "bx", 0, 0, tiled=True), kernels
 
 
 def next_group_head(group, samples):
@@ -133,9 +134,8 @@
     channels, samples = record.shape
     window = templates.shape[2]
     nblk = lax.axis_size(BLK)
-    group = gather_group(record)
+    group, kernels = gather_group(record, lag_kernels(templates))
     head = next_group_head(group[0], samples)
-    kernels = lag_kernels(templates)
     stacked = stacked_correlation(group, head, kernels, window)
     power_sum = seg_sum(jnp.sum(stacked * stacked, axis=1))
     record_len = samples * lax.axis_size("seg") * nblk

time: 108 us -> 106 us (0.981)
  blocking collectives: 55.5 us -> 64.8 us
  waiting for transfers between devices: 6.17 us -> 0.01 us
  starting transfers between devices: 22.9 us -> 19.1 us
  local copies, waits for them, and re-layouts: 5.4 us -> 4.13 us
    all_to_all x0 -> x1, blocking collectives: none -> 10.4 us  [gather_group(): return (lax.all_to_all(copies, 'bx', 0, 0, tiled=True), kernels)]
    all_to_all x1 -> x0, waiting for transfers between devices: 6.16 us -> none  [gather_group(): return lax.all_to_all(copies, 'bx', 0, 0, tiled=True)]
    all_to_all x1 -> x0, starting transfers between devices: 4.01 us -> none  [gather_group(): return lax.all_to_all(copies, 'bx', 0, 0, tiled=True)]
  transfers between devices with their start and end apart: 3 -> 2, of which waited for: 1 -> 0; matrix products, arithmetic and copies ran while one was open for 4% -> 4% of each run, Pallas kernels for 10% -> 10%
where the time goes in v12:
time: 106 us
  blocking collectives  64.8 us (61%)
  starting transfers between devices  19.1 us (18%)
  Pallas kernels  14.8 us (14%)
  local copies, waits for them, and re-layouts  4.13 us (4%)
  other arithmetic  2.9 us (3%)
    all_to_all x1, blocking collectives, body(): spread = lax.all_to_all(pieces, BLK, 1, 0, tiled=True)  31.8 us
    all_to_all x1, blocking collectives, seg_sum(): return jnp.sum(lax.all_to_all(copies, 'seg', 0, 0, tiled=True), axis=0)  22.7 us
    ppermute x1, starting transfers between devices, gather_group(): partner = lax.ppermute(record, 'bz', [(0, 1), (1, 0)])  14.5 us
    pallas_call x1, Pallas kernels, stacked_correlation(): pl.pallas_call(early_kernel, out_shape=jax.ShapeDtypeStruct((members, pai...  10.6 us
    all_to_all x1, blocking collectives, gather_group(): return (lax.all_to_all(copies, 'bx', 0, 0, tiled=True), kernels)  10.4 us
    ppermute x1, starting transfers between devices, next_group_head(): lax.ppermute(group[:, :samples], 'seg', [(i + 1, i) for i in range(nseg -...  4.54 us
    pallas_call x1, Pallas kernels, stacked_correlation(): pl.pallas_call(late_kernel, out_shape=jax.ShapeDtypeStruct((members, samp...  4.23 us
  transfers between devices with their start and end apart: 2, of which 0 were waited for; matrix products, arithmetic and copies ran while one was open for 4% of the time, Pallas kernels for 10%

profile of v12, /device:TPU:33, one launch (start us, length us, event | category | flops | bytes accessed | tf_op | source)
XLA Modules:
  0.0 105.9 jit_solution(13654518270290757573)
XLA Ops:
  0.0 14.5 %collective-permute-start = (f32[24,512]{1,0:T(8,128)}, f32[24,512]{1,0:T(8,128)S(1)}, u32[]{:S(2)}, u32[]{:S(2)}) collective-permute-start(f32[24,512]{1,0:T(8,128)} %param.2), channel_id=1, source_target_pairs={{0,1},{1,0},{2,3},{3,2},{4,5},{5,4},{6,7},{7,6},{8,9},{9,8},{10,11... | collective-permute-start | bytes 147464 | tf_op jit(solution)/shard_map/ppermute | solution.py:13
  14.5 1.5 %reshape.39 = bf16[16,24,8,64]{3,2,1,0:T(8,128)(2,1)S(1)} reshape(bf16[16,24,512]{2,1,0:T(8,128)(2,1)} %param.3) | data formatting | bytes 786432 | tf_op jit(solution)/shard_map/reshape | solution.py:85
  16.1 0.5 copy.9
  16.6 0.7 rev.3
  17.3 0.2 bitcast_reduce_fusion
  17.5 0.4 fusion.2
  17.9 0.0 copy-start.3
  18.0 1.2 %fusion.3 = bf16[24,8,16,64]{3,2,1,0:T(8,128)(2,1)} fusion(bf16[16,24,8,64]{3,0,2,1:T(8,128)(2,1)S(1)} %rev.3, f32[24,16]{1,0:T(8,128)S(1)} %add_sqrt_fusion, f32[24,16]{1,0:T(8,128)S(1)} %broadcast_multiply_fusion), kind=kLoop, calls=%fused_computation.5 | loop fusion | flops 786432 | bytes 789504 | tf_op jit(solution)/shard_map/convert_element_type | solution.py:89
  19.1 0.0 collective-permute-done
  19.1 0.0 copy-done.3
  19.2 10.4 %all_to_all.26.group_ref = f32[4,24,1024]{2,1,0:T(8,128)S(1)} all-to-all(f32[4,24,1024]{2,1,0:T(8,128)S(1)} %broadcast_in_dim.4), channel_id=1, replica_groups=mesh['seg'=64,'bx'=4,'bz'=2] {'bx'}, dimensions={0} | all-to-all | bytes 786432 | tf_op jit(solution)/shard_map/all_to_all | solution.py:20
  29.6 4.5 %collective-permute-start.1 = (f32[24,512]{1,0:T(8,128)S(1)}, f32[24,512]{1,0:T(8,128)S(1)}, u32[]{:S(2)}, u32[]{:S(2)}) collective-permute-start(f32[24,512]{1,0:T(8,128)S(1)} %slice.9), channel_id=1, source_target_pairs={{8,0},{16,8},{24,16},{32,24},{40,32},{48,40},{56,48},{64,56},{72,6... | collective-permute-start | bytes 147464 | tf_op jit(solution)/shard_map/ppermute | solution.py:25
  34.1 0.0 copy-done
  34.2 10.6 %shard_map.28 = f32[16,3584]{1,0:T(8,128)} custom-call(f32[4,24,1024]{2,1,0:T(8,128)} %copy-done, bf16[24,128,64]{2,1,0:T(8,128)(2,1)} %bitcast.22), custom_call_target="tpu_custom_call" | custom-call | tf_op jit(solution)/shard_map/pallas_call | solution.py:116
  44.8 0.0 collective-permute-done.1.head_ref
  44.8 0.6 copy-done.2
  45.4 4.2 %shard_map.29 = f32[16,512]{1,0:T(8,128)} custom-call(f32[4,24,1024]{2,1,0:T(8,128)} %copy-done, f32[24,512]{1,0:T(8,128)} %copy-done.2, bf16[24,128,64]{2,1,0:T(8,128)(2,1)} %bitcast.23), custom_call_target="tpu_custom_call" | custom-call | tf_op jit(solution)/shard_map/pallas_call | solution.py:120
  49.6 0.0 copy-done.1
  49.6 0.9 multiply_reduce_fusion
  50.5 22.7 %all_to_all.27 = f32[64,1,16]{2,1,0:T(1,128)S(1)} all-to-all(f32[64,1,16]{2,1,0:T(1,128)S(1)} %broadcast_in_dim.5), channel_id=1, replica_groups=mesh['seg'=64,'bx'=4,'bz'=2] {'seg'}, dimensions={0} | all-to-all | bytes 8192 | tf_op jit(solution)/shard_map/all_to_all | solution.py:130
  73.2 0.1 reduce_sum.39
  73.3 0.1 bitcast_divide_fusion
  73.4 31.8 %all_to_all.28 = f32[16,8,512]{2,0,1:T(8,128)S(1)} all-to-all(f32[16,8,512]{2,0,1:T(8,128)S(1)} %bitcast_divide_fusion), channel_id=1, replica_groups=mesh['seg'=64,'bx'=4,'bz'=2] {'bx','bz'}, dimensions={1} | all-to-all | bytes 524288 | tf_op jit(solution)/shard_map/all_to_all | solution.py:145
  105.2 0.7 copy.16
  (11 shorter events, 0.1 us)
Async XLA Ops:
  0.0 19.1 %collective-permute-start = (f32[24,512]{1,0:T(8,128)}, f32[24,512]{1,0:T(8,128)S(1)}, u32[]{:S(2)}, u32[]{:S(2)}) collective-permute-start(f32[24,512]{1,0:T(8,128)} %param.2), channel_id=1, source_target_pairs={{0,1},{1,0},{2,3},{3,2},{4,5},{5,4},{6,7},{7,6},{8,9},{9,8},{10,11... | collective-permute-start | bytes 147464 | tf_op jit(solution)/shard_map/ppermute | solution.py:13
  17.9 1.2 %copy-start.3 = (f32[24,512]{1,0:T(8,128)S(1)}, f32[24,512]{1,0:T(8,128)}, u32[]{:S(2)}) copy-start(f32[24,512]{1,0:T(8,128)} %param.2) | copy-start | bytes 147460
  29.6 4.6 %copy-start = (f32[4,24,1024]{2,1,0:T(8,128)}, f32[4,24,1024]{2,1,0:T(8,128)S(1)}, u32[]{:S(2)}) copy-start(f32[4,24,1024]{2,1,0:T(8,128)S(1)} %all_to_all.26.group_ref) | copy-start | bytes 1179652
  29.6 15.2 %collective-permute-start.1 = (f32[24,512]{1,0:T(8,128)S(1)}, f32[24,512]{1,0:T(8,128)S(1)}, u32[]{:S(2)}, u32[]{:S(2)}) collective-permute-start(f32[24,512]{1,0:T(8,128)S(1)} %slice.9), channel_id=1, source_target_pairs={{8,0},{16,8},{24,16},{32,24},{40,32},{48,40},{56,48},{64,56},{72,6... | collective-permute-start | bytes 147464 | tf_op jit(solution)/shard_map/ppermute | solution.py:25
  44.8 4.9 %copy-start.1 = (f32[16,3584]{1,0:T(8,128)S(1)}, f32[16,3584]{1,0:T(8,128)}, u32[]{:S(2)}) copy-start(f32[16,3584]{1,0:T(8,128)} %shard_map.28) | copy-start | bytes 688132
  44.8 0.6 copy-start.2

commit v13 on v12

--- a/solution.py
+++ b/solution.py
@@ -38,7 +38,7 @@
     return total[:, :samples]
 
 
-def corr_kernel(load_rows, channels, width, tr_ref, out_ref):
+def corr_kernel(load_rows, channels, width, tr_ref, out_ref, power_ref):
     lag = tr_ref.shape[2]
     members, samples = out_ref.shape
     parts = tr_ref.shape[1] // members
@@ -76,7 +76,9 @@
         jnp.zeros((members, odd_width), jnp.float32),
     )
     even_acc, odd_acc = lax.fori_loop(0, channels // ROWS, one_group, start, unroll=True)
-    out_ref[...] = (even_acc + odd_acc[:, lag : lag + samples]) / channels
+    stacked = (even_acc + odd_acc[:, lag : lag + samples]) / channels
+    out_ref[...] = stacked
+    power_ref[...] = jnp.sum(stacked * stacked, axis=1, keepdims=True)
 
 
 def lag_kernels(templates):
@@ -89,16 +91,16 @@
     return (centred / norm).astype(jnp.bfloat16).reshape(channels, parts * members, LAG_BLOCK)
 
 
-def early_kernel(group_ref, tr_ref, out_ref):
+def early_kernel(group_ref, tr_ref, out_ref, power_ref):
     pairs, channels, width = group_ref.shape
 
     def load_rows(first):
         return jnp.concatenate([group_ref[m, pl.ds(first, ROWS), :] for m in range(pairs)], axis=1)
 
-    corr_kernel(load_rows, channels, pairs * width, tr_ref, out_ref)
+    corr_kernel(load_rows, channels, pairs * width, tr_ref, out_ref, power_ref)
 
 
-def late_kernel(group_ref, head_ref, tr_ref, out_ref):
+def late_kernel(group_ref, head_ref, tr_ref, out_ref, power_ref):
     pairs, channels, width = group_ref.shape
     samples = head_ref.shape[1]
 
@@ -106,22 +108,23 @@
         last = group_ref[pairs - 1, pl.ds(first, ROWS), :]
         return jnp.concatenate([last[:, width - samples :], head_ref[pl.ds(first, ROWS), :]], axis=1)
 
-    corr_kernel(load_rows, channels, 2 * samples, tr_ref, out_ref)
+    corr_kernel(load_rows, channels, 2 * samples, tr_ref, out_ref, power_ref)
 
 
 def stacked_correlation(group, head, kernels, window):
     pairs, channels, width = group.shape
     samples = head.shape[1]
     members = kernels.shape[1] * LAG_BLOCK // window
-    early = pl.pallas_call(
+    sums = jax.ShapeDtypeStruct((members, 1), jnp.float32)
+    early, early_power = pl.pallas_call(
         early_kernel,
-        out_shape=jax.ShapeDtypeStruct((members, pairs * width - samples), jnp.float32),
+        out_shape=(jax.ShapeDtypeStruct((members, pairs * width - samples), jnp.float32), sums),
     )(group, kernels)
-    late = pl.pallas_call(
+    late, late_power = pl.pallas_call(
         late_kernel,
-        out_shape=jax.ShapeDtypeStruct((members, samples), jnp.float32),
+        out_shape=(jax.ShapeDtypeStruct((members, samples), jnp.float32), sums),
     )(group, head, kernels)
-    return jnp.concatenate([early, late], axis=1)
+    return jnp.concatenate([early, late], axis=1), (early_power + late_power)[:, 0]
 
 
 def seg_sum(value):
@@ -136,8 +139,8 @@
     nblk = lax.axis_size(BLK)
     group, kernels = gather_group(record, lag_kernels(templates))
     head = next_group_head(group[0], samples)
-    stacked = stacked_correlation(group, head, kernels, window)
-    power_sum = seg_sum(jnp.sum(stacked * stacked, axis=1))
+    stacked, partial = stacked_correlation(group, head, kernels, window)
+    power_sum = seg_sum(partial)
     record_len = samples * lax.axis_size("seg") * nblk
     detection = stacked / jnp.sqrt(power_sum / record_len + 1e-06)[:, None]
     members = detection.shape[0]

time: 106 us -> 107 us (level)
  blocking collectives: 64.8 us -> 42.2 us
  starting transfers between devices: 19.1 us -> 31 us
  waiting for transfers between devices: 0.01 us -> 10.1 us
    all_to_all x1 -> x0, blocking collectives: 22.7 us -> none  [seg_sum(): return jnp.sum(lax.all_to_all(copies, 'seg', 0, 0, tiled=True), axis=0)]
    all_to_all x0 -> x1, starting transfers between devices: none -> 12 us  [seg_sum(): return jnp.sum(lax.all_to_all(copies, 'seg', 0, 0, tiled=True), axis=0)]
    all_to_all x0 -> x1, waiting for transfers between devices: none -> 10.1 us  [seg_sum(): return jnp.sum(lax.all_to_all(copies, 'seg', 0, 0, tiled=True), axis=0)]
  transfers between devices with their start and end apart: 2 -> 3, of which waited for: 0 -> 1; matrix products, arithmetic and copies ran while one was open for 4% -> 5% of each run, Pallas kernels for 10% -> 10%
where the time goes in v13:
time: 107 us; the launch traced here: 106 us
  blocking collectives  42.2 us (39%)
  starting transfers between devices  31 us (29%)
  Pallas kernels  14.6 us (14%)
  waiting for transfers between devices  10.1 us (9%)
  local copies, waits for them, and re-layouts  4.73 us (4%)
  other arithmetic  3.59 us (3%)
    all_to_all x1, blocking collectives, body(): spread = lax.all_to_all(pieces, BLK, 1, 0, tiled=True)  31.8 us
    ppermute x1, starting transfers between devices, gather_group(): partner = lax.ppermute(record, 'bz', [(0, 1), (1, 0)])  14.5 us
    all_to_all x1, starting transfers between devices, seg_sum(): return jnp.sum(lax.all_to_all(copies, 'seg', 0, 0, tiled=True), axis=0)  12 us
    pallas_call x1, Pallas kernels, stacked_correlation(): pl.pallas_call(early_kernel, out_shape=(jax.ShapeDtypeStruct((members, pa...  10.5 us
    all_to_all x1, blocking collectives, gather_group(): return (lax.all_to_all(copies, 'bx', 0, 0, tiled=True), kernels)  10.4 us
    all_to_all x1, waiting for transfers between devices, seg_sum(): return jnp.sum(lax.all_to_all(copies, 'seg', 0, 0, tiled=True), axis=0)  10.1 us
    ppermute x1, starting transfers between devices, next_group_head(): lax.ppermute(group[:, :samples], 'seg', [(i + 1, i) for i in range(nseg -...  4.54 us
    pallas_call x1, Pallas kernels, stacked_correlation(): pl.pallas_call(late_kernel, out_shape=(jax.ShapeDtypeStruct((members, sam...  4.09 us
  transfers between devices with their start and end apart: 3, of which 1 were waited for; matrix products, arithmetic and copies ran while one was open for 5% of the time, Pallas kernels for 10%

profile of v13, /device:TPU:33, one launch (start us, length us, event | category | flops | bytes accessed | tf_op | source)
XLA Modules:
  0.0 106.4 jit_solution(15153481579694444211)
XLA Ops:
  0.0 14.5 %collective-permute-start = (f32[24,512]{1,0:T(8,128)}, f32[24,512]{1,0:T(8,128)S(1)}, u32[]{:S(2)}, u32[]{:S(2)}) collective-permute-start(f32[24,512]{1,0:T(8,128)} %param.2), channel_id=1, source_target_pairs={{0,1},{1,0},{2,3},{3,2},{4,5},{5,4},{6,7},{7,6},{8,9},{9,8},{10,11... | collective-permute-start | bytes 147464 | tf_op jit(solution)/shard_map/ppermute | solution.py:13
  14.5 1.5 %reshape.41 = bf16[16,24,8,64]{3,2,1,0:T(8,128)(2,1)S(1)} reshape(bf16[16,24,512]{2,1,0:T(8,128)(2,1)} %param.3) | data formatting | bytes 786432 | tf_op jit(solution)/shard_map/reshape | solution.py:87
  16.1 0.5 copy.11
  16.6 0.7 rev.3
  17.3 0.2 bitcast_reduce_fusion
  17.5 0.4 fusion.2
  17.9 0.0 copy-start.3
  18.0 1.2 %fusion.3 = bf16[24,8,16,64]{3,2,1,0:T(8,128)(2,1)} fusion(bf16[16,24,8,64]{3,0,2,1:T(8,128)(2,1)S(1)} %rev.3, f32[24,16]{1,0:T(8,128)S(1)} %add_sqrt_fusion, f32[24,16]{1,0:T(8,128)S(1)} %broadcast_multiply_fusion), kind=kLoop, calls=%fused_computation.5 | loop fusion | flops 786432 | bytes 789504 | tf_op jit(solution)/shard_map/convert_element_type | solution.py:91
  19.1 0.0 collective-permute-done
  19.2 10.4 %all_to_all.26.group_ref = f32[4,24,1024]{2,1,0:T(8,128)S(1)} all-to-all(f32[4,24,1024]{2,1,0:T(8,128)S(1)} %broadcast_in_dim.6), channel_id=1, replica_groups=mesh['seg'=64,'bx'=4,'bz'=2] {'bx'}, dimensions={0} | all-to-all | bytes 786432 | tf_op jit(solution)/shard_map/all_to_all | solution.py:20
  29.6 4.5 %collective-permute-start.1 = (f32[24,512]{1,0:T(8,128)S(1)}, f32[24,512]{1,0:T(8,128)S(1)}, u32[]{:S(2)}, u32[]{:S(2)}) collective-permute-start(f32[24,512]{1,0:T(8,128)S(1)} %slice.9), channel_id=1, source_target_pairs={{8,0},{16,8},{24,16},{32,24},{40,32},{48,40},{56,48},{64,56},{72,6... | collective-permute-start | bytes 147464 | tf_op jit(solution)/shard_map/ppermute | solution.py:25
  34.2 10.5 %shard_map.28 = (f32[16,3584]{1,0:T(8,128)}, f32[16,1]{1,0:T(8,128)}) custom-call(f32[4,24,1024]{2,1,0:T(8,128)} %copy-done, bf16[24,128,64]{2,1,0:T(8,128)(2,1)} %bitcast.22), custom_call_target="tpu_custom_call" | custom-call | tf_op jit(solution)/shard_map/pallas_call | solution.py:119
  44.7 0.0 collective-permute-done.1.head_ref
  44.7 0.6 copy-done.2
  45.3 4.1 %shard_map.29 = (f32[16,512]{1,0:T(8,128)}, f32[16,1]{1,0:T(8,128)}) custom-call(f32[4,24,1024]{2,1,0:T(8,128)} %copy-done, f32[24,512]{1,0:T(8,128)} %copy-done.2, bf16[24,128,64]{2,1,0:T(8,128)(2,1)} %bitcast.23), custom_call_target="tpu_custom_call" | custom-call | tf_op jit(solution)/shard_map/pallas_call | solution.py:123
  49.4 0.8 add_reduce_fusion
  50.2 0.6 broadcast_in_dim.8
  50.8 12.0 %all-to-all-start.1 = ((f32[64,1,16]{2,1,0:T(1,128)}), f32[64,1,16]{2,1,0:T(1,128)S(1)}, u32[]{:S(2)}, u32[]{:S(2)}) async-start(f32[64,1,16]{2,1,0:T(1,128)} %broadcast_in_dim.8), calls=%async_computation.1 | async-start | bytes 65536 | tf_op jit(solution)/shard_map/all_to_all | solution.py:133
  62.8 0.8 pad_maximum_fusion
  63.6 10.1 %all-to-all-done.1 = f32[64,1,16]{2,1,0:T(1,128)S(1)} async-done(((f32[64,1,16]{2,1,0:T(1,128)}), f32[64,1,16]{2,1,0:T(1,128)S(1)}, u32[]{:S(2)}, u32[]{:S(2)}) %all-to-all-start.1) | async-done | bytes 4128 | tf_op jit(solution)/shard_map/all_to_all | solution.py:133
  73.7 0.1 reduce_sum.29
  73.8 0.1 bitcast_divide_fusion
  73.9 31.8 %all_to_all.27 = f32[16,8,512]{2,0,1:T(8,128)S(1)} all-to-all(f32[16,8,512]{2,0,1:T(8,128)S(1)} %bitcast_divide_fusion), channel_id=1, replica_groups=mesh['seg'=64,'bx'=4,'bz'=2] {'bx','bz'}, dimensions={1} | all-to-all | bytes 524288 | tf_op jit(solution)/shard_map/all_to_all | solution.py:148
  105.7 0.7 copy.18
  (15 shorter events, 0.1 us)
Async XLA Ops:
  0.0 19.1 %collective-permute-start = (f32[24,512]{1,0:T(8,128)}, f32[24,512]{1,0:T(8,128)S(1)}, u32[]{:S(2)}, u32[]{:S(2)}) collective-permute-start(f32[24,512]{1,0:T(8,128)} %param.2), channel_id=1, source_target_pairs={{0,1},{1,0},{2,3},{3,2},{4,5},{5,4},{6,7},{7,6},{8,9},{9,8},{10,11... | collective-permute-start | bytes 147464 | tf_op jit(solution)/shard_map/ppermute | solution.py:13
  17.9 1.2 %copy-start.3 = (f32[24,512]{1,0:T(8,128)S(1)}, f32[24,512]{1,0:T(8,128)}, u32[]{:S(2)}) copy-start(f32[24,512]{1,0:T(8,128)} %param.2) | copy-start | bytes 147460
  29.6 4.6 %copy-start = (f32[4,24,1024]{2,1,0:T(8,128)}, f32[4,24,1024]{2,1,0:T(8,128)S(1)}, u32[]{:S(2)}) copy-start(f32[4,24,1024]{2,1,0:T(8,128)S(1)} %all_to_all.26.group_ref) | copy-start | bytes 1179652
  29.6 15.1 %collective-permute-start.1 = (f32[24,512]{1,0:T(8,128)S(1)}, f32[24,512]{1,0:T(8,128)S(1)}, u32[]{:S(2)}, u32[]{:S(2)}) collective-permute-start(f32[24,512]{1,0:T(8,128)S(1)} %slice.9), channel_id=1, source_target_pairs={{8,0},{16,8},{24,16},{32,24},{40,32},{48,40},{56,48},{64,56},{72,6... | collective-permute-start | bytes 147464 | tf_op jit(solution)/shard_map/ppermute | solution.py:25
  44.7 4.7 %copy-start.4 = (f32[16,1]{1,0:T(8,128)S(1)}, f32[16,1]{1,0:T(8,128)}, u32[]{:S(2)}) copy-start(f32[16,1]{1,0:T(8,128)} %get-tuple-element.15) | copy-start | bytes 196
  44.7 18.1 %copy-start.1 = (f32[16,3584]{1,0:T(8,128)S(1)}, f32[16,3584]{1,0:T(8,128)}, u32[]{:S(2)}) copy-start(f32[16,3584]{1,0:T(8,128)} %get-tuple-element.13) | copy-start | bytes 688132
  44.7 0.6 copy-start.2
  50.8 22.9 %all-to-all-start.1 = ((f32[64,1,16]{2,1,0:T(1,128)}), f32[64,1,16]{2,1,0:T(1,128)S(1)}, u32[]{:S(2)}, u32[]{:S(2)}) async-start(f32[64,1,16]{2,1,0:T(1,128)} %broadcast_in_dim.8), calls=%async_computation.1 | async-start | bytes 65536 | tf_op jit(solution)/shard_map/all_to_all | solution.py:133
